TPU v7x, 128 devices: a whole 4x4x4 slice. The times are simulated.
128 devices in a mesh: req: 4 (over x_lo, core), kv: 32 (over z, x_hi, y).
Axes of the slice: x: 4 (x_hi: 2, x_lo: 2; x = x_hi * 2 + x_lo), y: 4, z: 4, core: 2. Of those that a mesh axis runs over, the one named last changes fastest.
Arguments:
- hidden_in: bfloat16 [2048, 4096], P('req'), may hold values from -6 to 6
- ln_gains: float32 [2, 4096], replicated, may hold values from 0.1 to 1.9
- qkv_weight: bfloat16 [4096, 3, 4096], P('req', None, 'kv'), may hold values from -0.09375 to 0.09375
- dense_weight: bfloat16 [4096, 4096], P('kv', 'req'), may hold values from -0.09375 to 0.09375
- up_weight: bfloat16 [4096, 16384], P('req', 'kv'), may hold values from -0.09375 to 0.09375
- down_weight: bfloat16 [16384, 4096], P('kv', 'req'), may hold values from -0.046875 to 0.046875
- cache: bfloat16 [4, 256, 2, 32, 128, 128], P('req', 'kv'), may hold values from -200 to 200
- cached_len: int32 [8], P('req'), may hold values from 1 to 16384, as said below
- page_table: int32 [8, 128], P('req'), may hold values from 0 to 255, as said below
Outputs:
- hidden_out: float32 [2048, 4096], P('req', 'kv')
Inputs may be any that keep to these rules, and one draw needn't show every extreme that they name: `page_table`: within each group of 2 consecutive requests the entries are distinct and together name each of the group's 256 slots once. `cached_len`: some request has exactly 16384 cached tokens.
All inputs are finite; a program needn't handle non-finite values.
Results may differ from a plain program's by a relative error of at most 0.012.
The roundings to bfloat16 on the way count: a program that leaves them out, or rounds other values in their place, can miss the bound.
Values may be sent and summed in bfloat16 or wider, within the bound.
No kernel may reach another device: no remote copies, remote signals or barrier semaphores. Data moves between devices by JAX's collectives and lax.ppermute only.
A program may use at most 192 MiB of HBM per device.

v0:
```python
import jax
import jax.numpy as jnp
from jax import lax
from jax.sharding import PartitionSpec as P

D = 4096
HEADS = 32
HD = 128
ROT = 32
PAGE = 128


def layer_norm(x, gain):
    mean = jnp.mean(x, axis=-1, keepdims=True)
    cent = x - mean
    var = jnp.mean(cent * cent, axis=-1, keepdims=True)
    return cent * lax.rsqrt(var + 1e-05) * gain


def rotate(t, pos):
    half = ROT // 2
    freq = 10000.0 ** (-(jnp.arange(half, dtype=jnp.float32) * 2.0 / ROT))
    angle = pos[:, None] * freq[None, :]
    cosine = jnp.cos(angle)[:, None, :]
    sine = jnp.sin(angle)[:, None, :]
    first = t[..., :half]
    second = t[..., half:ROT]
    return jnp.concatenate(
        [first * cosine - second * sine, second * cosine + first * sine, t[..., ROT:]], axis=-1
    )


def online_update(state, scores, live, values):
    top, total, accum = state
    masked = jnp.where(live, scores, -1e30)
    new_top = jnp.maximum(top, jnp.max(masked, axis=-1))
    weights = jnp.where(live, jnp.exp(scores - new_top[..., None]), 0.0).astype(jnp.bfloat16)
    factor = jnp.exp(top - new_top)
    total = total * factor + jnp.sum(weights.astype(jnp.float32), axis=-1)
    accum = accum * factor[..., None] + jnp.einsum(
        "hqk,hkd->hqd", weights, values, preferred_element_type=jnp.float32
    )
    return (new_top, total, accum)


def per_device(
    hidden_in,
    ln_gains,
    qkv_weight,
    dense_weight,
    up_weight,
    down_weight,
    cache,
    cached_len,
    page_table,
):
    n_kv = lax.axis_size("kv")
    me_kv = lax.axis_index("kv")
    rows = hidden_in.shape[0]
    groups_here = cached_len.shape[0]
    span_rows = rows // groups_here
    width_loc = qkv_weight.shape[2]
    heads_loc = width_loc // HD
    scale = 1.0 / HD**0.5
    x = hidden_in.astype(jnp.float32)
    h1 = layer_norm(x, ln_gains[0]).astype(jnp.bfloat16)
    h2 = layer_norm(x, ln_gains[1]).astype(jnp.bfloat16)
    qkv_piece = lax.all_gather(qkv_weight, "req", axis=0, tiled=True)
    up_piece = lax.all_gather(up_weight, "req", axis=0, tiled=True)
    count = qkv_piece.shape[0]
    qkv_acc = jnp.dot(
        h1, qkv_piece.reshape(count, 3 * width_loc), preferred_element_type=jnp.float32
    )
    up_acc = jnp.dot(h2, up_piece, preferred_element_type=jnp.float32)
    qkv = qkv_acc
    qkv = qkv.reshape(rows, 3, heads_loc, HD)
    offsets = jnp.arange(span_rows, dtype=jnp.int32)
    pos = (cached_len[:, None] + offsets[None, :]).reshape(rows).astype(jnp.float32)
    query = rotate(qkv[:, 0], pos).astype(jnp.bfloat16)
    key_new = rotate(qkv[:, 1], pos).astype(jnp.bfloat16)
    value_new = qkv[:, 2].astype(jnp.bfloat16)
    q_grp = query.reshape(groups_here, span_rows, heads_loc, HD)
    k_grp = key_new.reshape(groups_here, span_rows, heads_loc, HD)
    v_grp = value_new.reshape(groups_here, span_rows, heads_loc, HD)
    causal = offsets[None, :] <= offsets[:, None]
    s_new = jnp.einsum("gqhd,gkhd->ghqk", q_grp, k_grp, preferred_element_type=jnp.float32) * scale
    s_new = jnp.where(causal[None, None], s_new, -1e30)
    top_new = jnp.max(s_new, axis=-1)
    p_new = jnp.where(causal[None, None], jnp.exp(s_new - top_new[..., None]), 0.0).astype(
        jnp.bfloat16
    )
    total_new = jnp.sum(p_new.astype(jnp.float32), axis=-1)
    accum_new = jnp.einsum("ghqk,gkhd->ghqd", p_new, v_grp, preferred_element_type=jnp.float32)
    q_all = lax.all_gather(query.reshape(rows, width_loc), "kv", axis=1, tiled=True)
    q_all = q_all.reshape(groups_here, span_rows, HEADS, HD)
    local_cache = cache[0]
    slots_here = local_cache.shape[0]
    slot_ids = me_kv * slots_here + jnp.arange(slots_here, dtype=jnp.int32)
    match = (page_table[None, :, :] == slot_ids[:, None, None]).astype(jnp.int32)
    owner_req = jnp.sum(
        match * jnp.arange(groups_here, dtype=jnp.int32)[None, :, None], axis=(1, 2)
    )
    owner_page = jnp.sum(
        match * jnp.arange(page_table.shape[1], dtype=jnp.int32)[None, None, :], axis=(1, 2)
    )
    page_pos = jnp.arange(PAGE, dtype=jnp.int32)

    def visit(slot, state):
        tops, totals, accums = state
        req = owner_req[slot]
        page_kv = lax.dynamic_index_in_dim(local_cache, slot, 0, keepdims=False)
        q_req = lax.dynamic_index_in_dim(q_all, req, 0, keepdims=False)
        scores = (
            jnp.einsum("qhd,hkd->hqk", q_req, page_kv[0], preferred_element_type=jnp.float32)
            * scale
        )
        length = lax.dynamic_index_in_dim(cached_len, req, 0, keepdims=False)
        live = (owner_page[slot] * PAGE + page_pos < length)[None, None, :]
        part_state = (
            lax.dynamic_index_in_dim(tops, req, 0, keepdims=False),
            lax.dynamic_index_in_dim(totals, req, 0, keepdims=False),
            lax.dynamic_index_in_dim(accums, req, 0, keepdims=False),
        )
        top, total, accum = online_update(part_state, scores, live, page_kv[1])
        tops = lax.dynamic_update_index_in_dim(tops, top, req, 0)
        totals = lax.dynamic_update_index_in_dim(totals, total, req, 0)
        accums = lax.dynamic_update_index_in_dim(accums, accum, req, 0)
        return (tops, totals, accums)

    empty = (
        jnp.full((groups_here, HEADS, span_rows), -1e30, jnp.float32),
        jnp.zeros((groups_here, HEADS, span_rows), jnp.float32),
        jnp.zeros((groups_here, HEADS, span_rows, HD), jnp.float32),
    )
    tops, totals, accums = lax.fori_loop(0, slots_here, visit, empty)
    own = lax.dynamic_slice_in_dim(tops, me_kv * heads_loc, heads_loc, 1)
    with_new = lax.dynamic_update_slice_in_dim(
        tops, jnp.maximum(own, top_new), me_kv * heads_loc, 1
    )
    largest = lax.pmax(with_new, "kv")
    factor = jnp.exp(tops - largest)
    sum_acc, sum_tot = (
        lax.psum_scatter(accums * factor[..., None], "kv", scatter_dimension=1, tiled=True),
        lax.psum_scatter(totals * factor, "kv", scatter_dimension=1, tiled=True),
    )
    own_largest = lax.dynamic_slice_in_dim(largest, me_kv * heads_loc, heads_loc, 1)
    fresh = jnp.exp(top_new - own_largest)
    numer = sum_acc + accum_new * fresh[..., None]
    denom = sum_tot + total_new * fresh
    att = (numer / denom[..., None]).astype(jnp.bfloat16)
    att = jnp.transpose(att, (0, 2, 1, 3)).reshape(rows, width_loc)
    hidden = jax.nn.gelu(up_acc, approximate=False).astype(jnp.bfloat16)
    dense_piece = lax.all_gather(dense_weight, "req", axis=1, tiled=True)
    down_piece = lax.all_gather(down_weight, "req", axis=1, tiled=True)
    value = jnp.dot(att, dense_piece, preferred_element_type=jnp.float32) + jnp.dot(
        hidden, down_piece, preferred_element_type=jnp.float32
    )
    summed = lax.psum_scatter(value, "kv", scatter_dimension=1, tiled=True)
    width_out = D // n_kv
    residual = lax.dynamic_slice_in_dim(x, me_kv * width_out, width_out, 1)
    return residual + summed


def solution(mesh):
    placed = (
        P("req", None),
        P(),
        P("req", None, "kv"),
        P("kv", "req"),
        P("req", "kv"),
        P("kv", "req"),
        P("req", "kv", None, None, None, None),
        P("req"),
        P("req", None),
    )
    return jax.shard_map(
        per_device, mesh=mesh, in_specs=placed, out_specs=P("req", "kv"), check_vma=False
    )
```

profile of v0, /device:TPU:0, one launch (start us, length us, event | category | flops | bytes accessed | tf_op | source)
XLA Modules:
  0.0 1498.5 jit_solution(18109680154599882162)
XLA Ops:
  14.3 34.5 %all-gather.6.cloned.1.call-done = bf16[4096,3,128]{0,2,1:T(8,128)(2,1)} async-done(((bf16[1024,3,128]{0,2,1:T(8,128)(2,1)}), bf16[4096,3,128]{0,2,1:T(8,128)(2,1)}) %all-gather.6.cloned.1.call-update) | async-done | bytes 3145744 | tf_op jit(solution)/shard_map/all_gather | solution.py:68
  48.8 5.1 fusion.17
  56.4 80.3 %all-gather.8.cloned.1.call-done = bf16[512,4096]{0,1:T(8,128)(2,1)} async-done(((bf16[512,128]{0,1:T(8,128)(2,1)}), bf16[512,4096]{0,1:T(8,128)(2,1)}) %all-gather.8.cloned.1.call-update) | async-done | bytes 4194320 | tf_op jit(solution)/shard_map/all_gather | solution.py:94
  136.7 7.0 reshape.289
  143.7 11.1 copy.74
  159.0 171.9 %while.18 = (s32[]{:T(128)}, f32[2,32,256]{2,1,0:T(8,128)S(1)}, f32[2,32,256]{2,1,0:T(8,128)S(1)}, f32[2,32,256,128]{3,2,0,1:T(8,128)}, s32[8]{0:T(128)S(1)}, /*...) while((s32[]{:T(128)}, f32[2,32,256]{2,1,0:T(8,128)S(1)}, ...), condition=%wide.region_7.8_spmd.clone, body=%wide.region_4.7_spmd.clone.sunk | while | flops 552632576 | bytes 50824988 | solution.py:135
  163.9 4.6 select_reduce_fusion.2
  173.2 6.3 bitcast_dynamic-update-slice_fusion.2
  185.4 4.6 select_reduce_fusion.2
  194.7 6.3 bitcast_dynamic-update-slice_fusion.2
  206.9 4.6 select_reduce_fusion.2
  216.1 6.3 bitcast_dynamic-update-slice_fusion.2
  228.4 4.6 select_reduce_fusion.2
  237.6 6.3 bitcast_dynamic-update-slice_fusion.2
  249.9 4.6 select_reduce_fusion.2
  259.1 6.3 bitcast_dynamic-update-slice_fusion.2
  271.4 4.6 select_reduce_fusion.2
  280.6 6.3 bitcast_dynamic-update-slice_fusion.2
  292.9 4.6 select_reduce_fusion.2
  302.1 6.3 bitcast_dynamic-update-slice_fusion.2
  323.6 6.3 bitcast_dynamic-update-slice_fusion.2
  332.9 310.9 %all-reduce.4.cloned.1.call-done = f32[2,32,256]{2,1,0:T(8,128)} async-done(((f32[2,32,256]{2,1,0:T(8,128)}), f32[2,32,256]{2,1,0:T(8,128)}) %all-reduce.4.cloned.1.call-update) | async-done | bytes 65552 | tf_op jit(solution)/shard_map/pmax | solution.py:140
  645.5 8.0 broadcast_multiply_fusion
  655.4 32.9 %all-gather.12.cloned.1.call-done = bf16[4096,512]{1,0:T(8,128)(2,1)} async-done(((bf16[1024,512]{1,0:T(8,128)(2,1)}), bf16[4096,512]{1,0:T(8,128)(2,1)}) %all-gather.12.cloned.1.call-update) | async-done | bytes 4194320 | tf_op jit(solution)/shard_map/all_gather | solution.py:69
  688.3 48.9 %all-gather.14.cloned.1.call-done = bf16[512,4096]{1,0:T(8,128)(2,1)} async-done(((bf16[512,1024]{1,0:T(8,128)(2,1)}), bf16[512,4096]{1,0:T(8,128)(2,1)}) %all-gather.14.cloned.1.call-update) | async-done | bytes 4194320 | tf_op jit(solution)/shard_map/all_gather | solution.py:154
  737.2 14.6 fusion.35
  751.9 302.6 %all-reduce.6.cloned.1.call-done = f32[2,32,256]{2,0,1:T(2,128)} async-done(((f32[2,32,256]{2,0,1:T(2,128)}), f32[2,32,256]{2,0,1:T(2,128)}) %all-reduce.6.cloned.1.call-update) | async-done | bytes 65552
  1056.5 202.3 %reduce-scatter.3.cloned.1.call-done = f32[2,1,256,128]{3,2,0,1:T(8,128)} async-done(((f32[2,32,256,128]{3,2,0,1:T(8,128)}), f32[2,1,256,128]{3,2,0,1:T(8,128)}) %reduce-scatter.3.cloned.1.call-update) | async-done | bytes 262160 | tf_op jit(solution)/shard_map/reduce_scatter | solution.py:143
  1260.2 15.3 %all-gather.10.cloned.1.call-done = bf16[128,4096]{1,0:T(8,128)(2,1)} async-done(((bf16[128,1024]{1,0:T(8,128)(2,1)}), bf16[128,4096]{1,0:T(8,128)(2,1)}) %all-gather.10.cloned.1.call-update) | async-done | bytes 1048592 | tf_op jit(solution)/shard_map/all_gather | solution.py:153
  1275.5 8.2 convolution_add_fusion
  1283.7 6.5 convert_element_type.67
  1290.2 200.0 %reduce-scatter.5.cloned.1.call-done = f32[512,128]{1,0:T(8,128)} async-done(((f32[512,4096]{1,0:T(8,128)}), f32[512,128]{1,0:T(8,128)}) %reduce-scatter.5.cloned.1.call-update) | async-done | bytes 262160 | tf_op jit(solution)/shard_map/reduce_scatter | solution.py:158
  (155 shorter events, 93.3 us)
Async XLA Ops:
  6.5 42.2 %all-gather.6.cloned.1.call-start = ((), (), s32[]{:S(2)}) async-start(), calls=%async_computation.2 | async-start | bytes 3932160 | tf_op jit(solution)/shard_map/all_gather | solution.py:68
  8.9 127.8 %all-gather.8.cloned.1.call-start = ((), (), s32[]{:S(2)}) async-start(), calls=%async_computation.3 | async-start | bytes 4325376 | tf_op jit(solution)/shard_map/all_gather | solution.py:94
  8.9 4.1 copy-start.1
  9.8 4.5 copy-start.3
  48.8 6.2 copy-start.4
  54.9 588.9 %all-reduce.4.cloned.1.call-start = ((), (), s32[]{:S(2)}) async-start(), calls=%async_computation.4 | async-start | bytes 131072 | tf_op jit(solution)/shard_map/pmax | solution.py:140
  154.7 4.3 copy-start.5
  173.2 6.4 copy-start
  194.7 6.4 copy-start
  216.1 6.4 copy-start
  237.6 6.3 copy-start
  259.1 6.3 copy-start
  280.6 6.4 copy-start
  302.1 6.4 copy-start
  323.6 6.4 copy-start
  331.0 0.6 copy-start.2
  331.7 356.7 %all-gather.12.cloned.1.call-start = ((), (), s32[]{:S(2)}) async-start(), calls=%async_computation.7 | async-start | bytes 5242880 | tf_op jit(solution)/shard_map/all_gather | solution.py:69
  332.2 405.0 %all-gather.14.cloned.1.call-start = ((), (), s32[]{:S(2)}) async-start(), calls=%async_computation.8 | async-start | bytes 5242880 | tf_op jit(solution)/shard_map/all_gather | solution.py:154
  332.8 721.7 %all-reduce.6.cloned.1.call-start = ((), (), s32[]{:S(2)}) async-start(), calls=%async_computation.10 | async-start | bytes 131072
  645.4 613.4 %reduce-scatter.3.cloned.1.call-start = ((), (), s32[]{:S(2)}) async-start(), calls=%async_computation.5 | async-start | bytes 8650752 | tf_op jit(solution)/shard_map/reduce_scatter | solution.py:143
  653.5 1.0 copy-start.6
  653.5 621.9 %all-gather.10.cloned.1.call-start = ((), (), s32[]{:S(2)}) async-start(), calls=%async_computation.6 | async-start | bytes 1310720 | tf_op jit(solution)/shard_map/all_gather | solution.py:153
  654.3 835.9 %reduce-scatter.5.cloned.1.call-start = ((), (), s32[]{:S(2)}) async-start(), calls=%async_computation.9 | async-start | bytes 8650752 | tf_op jit(solution)/shard_map/reduce_scatter | solution.py:158
Sparse Core Ops, SparseCore 0:
  9.0 39.7 all-gather.5
  55.0 81.6 all-gather.7
  331.8 311.9 all-reduce.3
  645.3 42.9 all-gather.11
  689.8 47.3 all-gather.13
  739.6 314.8 all-reduce.5
  1056.9 201.8 reduce-scatter.2
  1260.5 14.9 all-gather.9
  1283.8 206.3 reduce-scatter.4
where the time goes:
time: 1500 us
  waiting for transfers between devices  1230 us (82%)
  matrix products  117 us (8%)
  local copies, waits for them, and re-layouts  79.7 us (5%)
  other arithmetic  37.5 us (2%)
  loops' own time  20.4 us (1%)
    pmax x1, waiting for transfers between devices, per_device(): largest = lax.pmax(with_new, 'kv')  311 us
    unnamed x10, waiting for transfers between devices  304 us
    reduce_scatter x1, waiting for transfers between devices, per_device(): lax.psum_scatter(accums * factor[..., None], 'kv', scatter_dimension=1, t...  202 us
    reduce_scatter x1, waiting for transfers between devices, per_device(): summed = lax.psum_scatter(value, 'kv', scatter_dimension=1, tiled=True)  200 us
    all_gather x1, waiting for transfers between devices, per_device(): lax.all_gather(query.reshape(rows, width_loc), 'kv', axis=1, tiled=True)  80.3 us
    dot_general x8, matrix products, online_update(): jnp.einsum('hqk,hkd->hqd', weights, values, preferred_element_type=jnp.fl...  50.8 us
    all_gather x1, waiting for transfers between devices, per_device(): down_piece = lax.all_gather(down_weight, 'req', axis=1, tiled=True)  48.9 us
    dot_general x8, matrix products, visit(): jnp.einsum('qhd,hkd->hqk', q_req, page_kv[0], preferred_element_type=jnp....  36.8 us
  transfers between devices with their start and end apart: 9, of which 9 were waited for; matrix products, arithmetic and copies ran while one was open for 3% of the time, Pallas kernels for 0%

commit v1 on v0

--- a/solution.py
+++ b/solution.py
@@ -137,12 +137,13 @@
     with_new = lax.dynamic_update_slice_in_dim(
         tops, jnp.maximum(own, top_new), me_kv * heads_loc, 1
     )
-    largest = lax.pmax(with_new, "kv")
+    largest = jnp.max(lax.all_gather(with_new, "kv", axis=0, tiled=False), axis=0)
     factor = jnp.exp(tops - largest)
-    sum_acc, sum_tot = (
-        lax.psum_scatter(accums * factor[..., None], "kv", scatter_dimension=1, tiled=True),
-        lax.psum_scatter(totals * factor, "kv", scatter_dimension=1, tiled=True),
-    )
+    tot_rows = (totals * factor).reshape(groups_here, HEADS, span_rows // HD, HD)
+    packed = jnp.concatenate([accums * factor[..., None], tot_rows], axis=2)
+    summed = lax.psum_scatter(packed, "kv", scatter_dimension=1, tiled=True)
+    sum_acc = summed[:, :, :span_rows]
+    sum_tot = summed[:, :, span_rows:].reshape(groups_here, heads_loc, span_rows)
     own_largest = lax.dynamic_slice_in_dim(largest, me_kv * heads_loc, heads_loc, 1)
     fresh = jnp.exp(top_new - own_largest)
     numer = sum_acc + accum_new * fresh[..., None]

time: 1500 us -> 988 us (0.66)
  waiting for transfers between devices: 1230 us -> 718 us
    pmax x1 -> x0, waiting for transfers between devices: 311 us -> none  [per_device(): largest = lax.pmax(with_new, 'kv')]
    unnamed x10 -> x8, waiting for transfers between devices: 304 us -> 1.83 us
    all_gather x0 -> x1, waiting for transfers between devices: none -> 68.3 us  [per_device(): lax.all_gather(with_new, 'kv', axis=0, tiled=False)]
    reduce_scatter x1, waiting for transfers between devices: 202 us -> 235 us  [per_device(): summed = lax.psum_scatter(packed, 'kv', scatter_dimension=1, tiled=True)]
  transfers between devices with their start and end apart: 9 -> 8, of which waited for: 9 -> 8; matrix products, arithmetic and copies ran while one was open for 3% -> 4% of each run, Pallas kernels for 0% -> 0%
where the time goes in v1:
time: 988 us; the launch traced here: 987 us
  waiting for transfers between devices  718 us (73%)
  matrix products  117 us (12%)
  local copies, waits for them, and re-layouts  77.7 us (8%)
  other arithmetic  39.3 us (4%)
  loops' own time  20.3 us (2%)
  between operations  13.8 us (1%)
    reduce_scatter x1, waiting for transfers between devices, per_device(): summed = lax.psum_scatter(packed, 'kv', scatter_dimension=1, tiled=True)  235 us
    reduce_scatter x1, waiting for transfers between devices, per_device(): summed = lax.psum_scatter(value, 'kv', scatter_dimension=1, tiled=True)  200 us
    all_gather x1, waiting for transfers between devices, per_device(): lax.all_gather(query.reshape(rows, width_loc), 'kv', axis=1, tiled=True)  80.3 us
    all_gather x1, waiting for transfers between devices, per_device(): lax.all_gather(with_new, 'kv', axis=0, tiled=False)  68.3 us
    dot_general x8, matrix products, online_update(): jnp.einsum('hqk,hkd->hqd', weights, values, preferred_element_type=jnp.fl...  51 us
    all_gather x1, waiting for transfers between devices, per_device(): down_piece = lax.all_gather(down_weight, 'req', axis=1, tiled=True)  48.9 us
    dynamic_slice x8, local copies, waits for them, and re-layouts, visit(): lax.dynamic_index_in_dim(accums, req, 0, keepdims=False)  36.7 us
    dot_general x8, matrix products, visit(): jnp.einsum('qhd,hkd->hqk', q_req, page_kv[0], preferred_element_type=jnp....  36.5 us
  transfers between devices with their start and end apart: 8, of which 8 were waited for; matrix products, arithmetic and copies ran while one was open for 4% of the time, Pallas kernels for 0%

profile of v1, /device:TPU:0, one launch (start us, length us, event | category | flops | bytes accessed | tf_op | source)
XLA Modules:
  0.0 986.6 jit_solution(8438326795556615646)
XLA Ops:
  14.3 34.5 %all-gather.7.cloned.1.call-done = bf16[4096,3,128]{0,2,1:T(8,128)(2,1)} async-done(((bf16[1024,3,128]{0,2,1:T(8,128)(2,1)}), bf16[4096,3,128]{0,2,1:T(8,128)(2,1)}) %all-gather.7.cloned.1.call-update) | async-done | bytes 3145744 | tf_op jit(solution)/shard_map/all_gather | solution.py:68
  48.8 5.1 fusion.17
  56.4 80.3 %all-gather.9.cloned.1.call-done = bf16[512,4096]{0,1:T(8,128)(2,1)} async-done(((bf16[512,128]{0,1:T(8,128)(2,1)}), bf16[512,4096]{0,1:T(8,128)(2,1)}) %all-gather.9.cloned.1.call-update) | async-done | bytes 4194320 | tf_op jit(solution)/shard_map/all_gather | solution.py:94
  136.7 7.0 reshape.297
  143.7 11.1 %copy.60 = bf16[2,256,32,128]{3,1,2,0:T(8,128)(2,1)} copy(bf16[2,256,32,128]{1,0,3,2:T(2,128)(2,1)} %reshape.297) | data formatting | bytes 8388608
  159.0 171.4 %while.18 = (s32[]{:T(128)}, f32[2,32,256]{2,1,0:T(8,128)S(1)}, f32[2,32,256]{2,1,0:T(8,128)S(1)}, f32[2,32,256,128]{3,2,0,1:T(8,128)}, s32[8]{0:T(128)S(1)}, /*...) while((s32[]{:T(128)}, f32[2,32,256]{2,1,0:T(8,128)S(1)}, ...), condition=%wide.region_7.8_spmd.clone, body=%wide.region_4.7_spmd.clone.sunk | while | flops 552632576 | bytes 50824988 | solution.py:135
  168.5 4.6 constant_dynamic-slice_fusion.2
  173.1 6.4 bitcast_dynamic-update-slice_fusion.2
  189.9 4.6 constant_dynamic-slice_fusion.2
  194.5 6.3 bitcast_dynamic-update-slice_fusion.2
  211.4 4.6 constant_dynamic-slice_fusion.2
  215.9 6.4 bitcast_dynamic-update-slice_fusion.2
  232.8 4.6 constant_dynamic-slice_fusion.2
  237.4 6.4 bitcast_dynamic-update-slice_fusion.2
  254.2 4.6 constant_dynamic-slice_fusion.2
  258.8 6.4 bitcast_dynamic-update-slice_fusion.2
  275.7 4.6 constant_dynamic-slice_fusion.2
  280.3 6.4 bitcast_dynamic-update-slice_fusion.2
  297.1 4.6 constant_dynamic-slice_fusion.2
  301.7 6.3 bitcast_dynamic-update-slice_fusion.2
  318.5 4.6 constant_dynamic-slice_fusion.2
  323.1 6.4 bitcast_dynamic-update-slice_fusion.2
  332.4 68.3 %all-gather.11.cloned.1.call-done = f32[32,2,32,256]{3,2,1,0:T(8,128)} async-done(((f32[1,2,32,256]{3,2,1,0:T(8,128)}), f32[32,2,32,256]{3,2,1,0:T(8,128)}) %all-gather.11.cloned.1.call-update) | async-done | bytes 2097168 | tf_op jit(solution)/shard_map/all_gather | solution.py:140
  402.6 5.2 broadcast_multiply_fusion
  413.5 32.6 %all-gather.15.cloned.1.call-done = bf16[4096,512]{1,0:T(8,128)(2,1)} async-done(((bf16[1024,512]{1,0:T(8,128)(2,1)}), bf16[4096,512]{1,0:T(8,128)(2,1)}) %all-gather.15.cloned.1.call-update) | async-done | bytes 4194320 | tf_op jit(solution)/shard_map/all_gather | solution.py:69
  446.1 48.9 %all-gather.17.cloned.1.call-done = bf16[512,4096]{1,0:T(8,128)(2,1)} async-done(((bf16[512,1024]{1,0:T(8,128)(2,1)}), bf16[512,4096]{1,0:T(8,128)(2,1)}) %all-gather.17.cloned.1.call-update) | async-done | bytes 4194320 | tf_op jit(solution)/shard_map/all_gather | solution.py:155
  495.0 14.6 %fusion.35 = f32[512,4096]{1,0:T(8,128)} fusion(bf16[512,4096]{1,0:T(8,128)(2,1)} %all-gather.17.cloned.1.call-done, bf16[4096,512]{1,0:T(8,128)(2,1)} %all-gather.15.cloned.1.call-done, bf16[512,4096]{1,0:T(8,128)(2,1)} %param.11, f32[4096]{0:T(1024)S(1)} %bitcast.139, f32[512]{0:T(512)S(1)} %add_rsqrt_fusion, f32[512]{0:T(512)S(1)} %broadcast_multiply_fusion.1), kind=kOutput, calls=%fused_computation.64 | convolution fusion | flops 4322492416 | bytes 20992000 | tf_op jit(solution)/shard_map/dot_general | solution.py:156
  509.6 234.7 %reduce-scatter.3.cloned.1.call-done = f32[2,1,258,128]{3,2,0,1:T(8,128)} async-done(((f32[2,32,258,128]{3,2,0,1:T(8,128)}), f32[2,1,258,128]{3,2,0,1:T(8,128)}) %reduce-scatter.3.cloned.1.call-update) | async-done | bytes 264208 | tf_op jit(solution)/shard_map/reduce_scatter | solution.py:144
  746.4 16.7 %all-gather.13.cloned.1.call-done = bf16[128,4096]{1,0:T(8,128)(2,1)} async-done(((bf16[128,1024]{1,0:T(8,128)(2,1)}), bf16[128,4096]{1,0:T(8,128)(2,1)}) %all-gather.13.cloned.1.call-update) | async-done | bytes 1048592 | tf_op jit(solution)/shard_map/all_gather | solution.py:154
  763.1 8.2 convolution_add_fusion
  771.3 6.5 convert_element_type.67
  777.8 200.2 %reduce-scatter.5.cloned.1.call-done = f32[512,128]{1,0:T(8,128)} async-done(((f32[512,4096]{1,0:T(8,128)}), f32[512,128]{1,0:T(8,128)}) %reduce-scatter.5.cloned.1.call-update) | async-done | bytes 262160 | tf_op jit(solution)/shard_map/reduce_scatter | solution.py:159
  (151 shorter events, 91.0 us)
Async XLA Ops:
  6.5 42.2 %all-gather.7.cloned.1.call-start = ((), (), s32[]{:S(2)}) async-start(), calls=%async_computation.2 | async-start | bytes 3932160 | tf_op jit(solution)/shard_map/all_gather | solution.py:68
  8.9 127.8 %all-gather.9.cloned.1.call-start = ((), (), s32[]{:S(2)}) async-start(), calls=%async_computation.3 | async-start | bytes 4325376 | tf_op jit(solution)/shard_map/all_gather | solution.py:94
  8.9 4.1 copy-start.1
  9.8 4.5 copy-start.3
  48.8 6.2 copy-start.4
  54.9 345.8 %all-gather.11.cloned.1.call-start = ((), (), s32[]{:S(2)}) async-start(), calls=%async_computation.4 | async-start | bytes 2162688 | tf_op jit(solution)/shard_map/all_gather | solution.py:140
  154.8 4.3 copy-start.5
  173.1 6.4 copy-start
  194.5 6.4 copy-start
  215.9 6.4 copy-start
  237.4 6.4 copy-start
  258.8 6.4 copy-start
  280.3 6.4 copy-start
  301.7 6.4 copy-start
  323.1 6.4 copy-start
  330.6 0.6 copy-start.2
  331.2 114.9 %all-gather.15.cloned.1.call-start = ((), (), s32[]{:S(2)}) async-start(), calls=%async_computation.7 | async-start | bytes 5242880 | tf_op jit(solution)/shard_map/all_gather | solution.py:69
  331.8 163.2 %all-gather.17.cloned.1.call-start = ((), (), s32[]{:S(2)}) async-start(), calls=%async_computation.8 | async-start | bytes 5242880 | tf_op jit(solution)/shard_map/all_gather | solution.py:155
  332.4 411.9 %reduce-scatter.3.cloned.1.call-start = ((), (), s32[]{:S(2)}) async-start(), calls=%async_computation.5 | async-start | bytes 8921088 | tf_op jit(solution)/shard_map/reduce_scatter | solution.py:144
  412.2 350.9 %all-gather.13.cloned.1.call-start = ((), (), s32[]{:S(2)}) async-start(), calls=%async_computation.6 | async-start | bytes 1310720 | tf_op jit(solution)/shard_map/all_gather | solution.py:154
  413.0 565.1 %reduce-scatter.5.cloned.1.call-start = ((), (), s32[]{:S(2)}) async-start(), calls=%async_computation.9 | async-start | bytes 8650752 | tf_op jit(solution)/shard_map/reduce_scatter | solution.py:159
Sparse Core Ops, SparseCore 0:
  9.0 39.7 all-gather.6
  55.0 81.6 all-gather.8
  331.3 69.3 all-gather.10
  402.2 43.8 all-gather.14
  447.6 47.3 all-gather.16
  500.1 244.1 reduce-scatter.2
  746.0 17.1 all-gather.12
  771.4 206.5 reduce-scatter.4

commit v2 on v1

--- a/solution.py
+++ b/solution.py
@@ -2,6 +2,7 @@
 import jax.numpy as jnp
 from jax import lax
 from jax.sharding import PartitionSpec as P
+from jax.experimental import pallas as pl
 
 D = 4096
 HEADS = 32
@@ -30,17 +31,57 @@
     )
 
 
-def online_update(state, scores, live, values):
-    top, total, accum = state
-    masked = jnp.where(live, scores, -1e30)
-    new_top = jnp.maximum(top, jnp.max(masked, axis=-1))
-    weights = jnp.where(live, jnp.exp(scores - new_top[..., None]), 0.0).astype(jnp.bfloat16)
-    factor = jnp.exp(top - new_top)
-    total = total * factor + jnp.sum(weights.astype(jnp.float32), axis=-1)
-    accum = accum * factor[..., None] + jnp.einsum(
-        "hqk,hkd->hqd", weights, values, preferred_element_type=jnp.float32
-    )
-    return (new_top, total, accum)
+def attend_kernel(q_ref, k_ref, v_ref, live_ref, acc_ref, top_ref, tot_ref):
+    scale = 1.0 / HD**0.5
+    slots = k_ref.shape[0]
+    q = q_ref[...]
+    k = k_ref[...].reshape(slots * PAGE, HD)
+    v = v_ref[...].reshape(slots * PAGE, HD)
+    scores = (
+        lax.dot_general(q, k, (((1,), (1,)), ((), ())), preferred_element_type=jnp.float32)
+        * scale
+    )
+    live = live_ref[...] > 0
+    top = jnp.max(jnp.where(live, scores, -1e30), axis=1, keepdims=True)
+    weights = jnp.where(live, jnp.exp(scores - top), 0.0).astype(jnp.bfloat16)
+    tot_ref[...] = jnp.sum(weights.astype(jnp.float32), axis=1, keepdims=True)
+    top_ref[...] = top
+    acc_ref[...] = jnp.dot(weights, v, preferred_element_type=jnp.float32)
+
+
+def attend_pages(q_all, local_cache, live):
+    groups, span = live.shape[0], q_all.shape[0] // live.shape[0]
+    slots = local_cache.shape[0]
+    heads = local_cache.shape[2]
+    page_spec = lambda kv: pl.BlockSpec(
+        (slots, None, None, PAGE, HD), lambda g, h: (0, kv, h, 0, 0)
+    )
+    return pl.pallas_call(
+        attend_kernel,
+        grid=(groups, heads),
+        in_specs=[
+            pl.BlockSpec((span, HD), lambda g, h: (g, h)),
+            page_spec(0),
+            page_spec(1),
+            pl.BlockSpec((None, 1, slots * PAGE), lambda g, h: (g, 0, 0)),
+        ],
+        out_specs=[
+            pl.BlockSpec((None, None, span, HD), lambda g, h: (h, g, 0, 0)),
+            pl.BlockSpec((None, None, span, 1), lambda g, h: (h, g, 0, 0)),
+            pl.BlockSpec((None, None, span, 1), lambda g, h: (h, g, 0, 0)),
+        ],
+        out_shape=[
+            jax.ShapeDtypeStruct((heads, groups, span, HD), jnp.float32),
+            jax.ShapeDtypeStruct((heads, groups, span, 1), jnp.float32),
+            jax.ShapeDtypeStruct((heads, groups, span, 1), jnp.float32),
+        ],
+        cost_estimate=pl.CostEstimate(
+            flops=4 * groups * heads * span * slots * PAGE * HD,
+            transcendentals=groups * heads * span * slots * PAGE,
+            bytes_accessed=groups * local_cache.size * 2 + q_all.size * 2
+            + groups * heads * span * HD * 4,
+        ),
+    )(q_all, local_cache, local_cache, live)
 
 
 def per_device(
@@ -92,7 +133,6 @@
     total_new = jnp.sum(p_new.astype(jnp.float32), axis=-1)
     accum_new = jnp.einsum("ghqk,gkhd->ghqd", p_new, v_grp, preferred_element_type=jnp.float32)
     q_all = lax.all_gather(query.reshape(rows, width_loc), "kv", axis=1, tiled=True)
-    q_all = q_all.reshape(groups_here, span_rows, HEADS, HD)
     local_cache = cache[0]
     slots_here = local_cache.shape[0]
     slot_ids = me_kv * slots_here + jnp.arange(slots_here, dtype=jnp.int32)
@@ -104,52 +144,34 @@
         match * jnp.arange(page_table.shape[1], dtype=jnp.int32)[None, None, :], axis=(1, 2)
     )
     page_pos = jnp.arange(PAGE, dtype=jnp.int32)
-
-    def visit(slot, state):
-        tops, totals, accums = state
-        req = owner_req[slot]
-        page_kv = lax.dynamic_index_in_dim(local_cache, slot, 0, keepdims=False)
-        q_req = lax.dynamic_index_in_dim(q_all, req, 0, keepdims=False)
-        scores = (
-            jnp.einsum("qhd,hkd->hqk", q_req, page_kv[0], preferred_element_type=jnp.float32)
-            * scale
-        )
-        length = lax.dynamic_index_in_dim(cached_len, req, 0, keepdims=False)
-        live = (owner_page[slot] * PAGE + page_pos < length)[None, None, :]
-        part_state = (
-            lax.dynamic_index_in_dim(tops, req, 0, keepdims=False),
-            lax.dynamic_index_in_dim(totals, req, 0, keepdims=False),
-            lax.dynamic_index_in_dim(accums, req, 0, keepdims=False),
-        )
-        top, total, accum = online_update(part_state, scores, live, page_kv[1])
-        tops = lax.dynamic_update_index_in_dim(tops, top, req, 0)
-        totals = lax.dynamic_update_index_in_dim(totals, total, req, 0)
-        accums = lax.dynamic_update_index_in_dim(accums, accum, req, 0)
-        return (tops, totals, accums)
-
-    empty = (
-        jnp.full((groups_here, HEADS, span_rows), -1e30, jnp.float32),
-        jnp.zeros((groups_here, HEADS, span_rows), jnp.float32),
-        jnp.zeros((groups_here, HEADS, span_rows, HD), jnp.float32),
-    )
-    tops, totals, accums = lax.fori_loop(0, slots_here, visit, empty)
-    own = lax.dynamic_slice_in_dim(tops, me_kv * heads_loc, heads_loc, 1)
+    reqs = jnp.arange(groups_here, dtype=jnp.int32)
+    live = (owner_req[None, :, None] == reqs[:, None, None]) & (
+        owner_page[None, :, None] * PAGE + page_pos[None, None, :] < cached_len[:, None, None]
+    )
+    live = live.astype(jnp.int32).reshape(groups_here, 1, slots_here * PAGE)
+    accums, tops, totals = attend_pages(q_all, local_cache, live)
+    tops = tops.reshape(HEADS, groups_here, span_rows)
+    totals = totals.reshape(HEADS, groups_here, span_rows)
+    top_new = jnp.transpose(top_new, (1, 0, 2))
+    total_new = jnp.transpose(total_new, (1, 0, 2))
+    accum_new = jnp.transpose(accum_new, (1, 0, 2, 3))
+    own = lax.dynamic_slice_in_dim(tops, me_kv * heads_loc, heads_loc, 0)
     with_new = lax.dynamic_update_slice_in_dim(
-        tops, jnp.maximum(own, top_new), me_kv * heads_loc, 1
+        tops, jnp.maximum(own, top_new), me_kv * heads_loc, 0
     )
     largest = jnp.max(lax.all_gather(with_new, "kv", axis=0, tiled=False), axis=0)
     factor = jnp.exp(tops - largest)
-    tot_rows = (totals * factor).reshape(groups_here, HEADS, span_rows // HD, HD)
+    tot_rows = (totals * factor).reshape(HEADS, groups_here, span_rows // HD, HD)
     packed = jnp.concatenate([accums * factor[..., None], tot_rows], axis=2)
-    summed = lax.psum_scatter(packed, "kv", scatter_dimension=1, tiled=True)
+    summed = lax.psum_scatter(packed, "kv", scatter_dimension=0, tiled=True)
     sum_acc = summed[:, :, :span_rows]
-    sum_tot = summed[:, :, span_rows:].reshape(groups_here, heads_loc, span_rows)
-    own_largest = lax.dynamic_slice_in_dim(largest, me_kv * heads_loc, heads_loc, 1)
+    sum_tot = summed[:, :, span_rows:].reshape(heads_loc, groups_here, span_rows)
+    own_largest = lax.dynamic_slice_in_dim(largest, me_kv * heads_loc, heads_loc, 0)
     fresh = jnp.exp(top_new - own_largest)
     numer = sum_acc + accum_new * fresh[..., None]
     denom = sum_tot + total_new * fresh
     att = (numer / denom[..., None]).astype(jnp.bfloat16)
-    att = jnp.transpose(att, (0, 2, 1, 3)).reshape(rows, width_loc)
+    att = jnp.transpose(att, (1, 2, 0, 3)).reshape(rows, width_loc)
     hidden = jax.nn.gelu(up_acc, approximate=False).astype(jnp.bfloat16)
     dense_piece = lax.all_gather(dense_weight, "req", axis=1, tiled=True)
     down_piece = lax.all_gather(down_weight, "req", axis=1, tiled=True)

time: 988 us -> 876 us (0.89)
  matrix products: 117 us -> 30.5 us
  Pallas kernels: 0 us -> 63.2 us
  local copies, waits for them, and re-layouts: 77.7 us -> 20.7 us
  loops' own time: 20.3 us -> 0 us
  waiting for transfers between devices: 718 us -> 699 us
    dot_general x16 -> x0, matrix products: 87.5 us -> none  [the longest x8 51 us: online_update(): jnp.einsum('hqk,hkd->hqd', weights, values, preferred_element_type=jnp.fl...]
    pallas_call x0 -> x1, Pallas kernels: none -> 63.2 us  [attend_pages(): pl.pallas_call(attend_kernel, grid=(groups, heads), in_specs=[pl.BlockSpe...]
    dynamic_slice x32 -> x1, local copies, waits for them, and re-layouts: 50.5 us -> 1.1 us  [per_device(): own = lax.dynamic_slice_in_dim(tops, me_kv * heads_loc, heads_loc, 0)]
    all_gather x1, waiting for transfers between devices: 32.6 us -> 11.6 us  [per_device(): up_piece = lax.all_gather(up_weight, 'req', axis=0, tiled=True)]
    another operation x1 -> x0, loops' own time: 20.3 us -> none  [per_device(): tops, totals, accums = lax.fori_loop(0, slots_here, visit, empty)]
    exp x8 -> x1, other arithmetic: 0.12 us -> 11.4 us  [per_device(): factor = jnp.exp(tops - largest)]
    unnamed x15 -> x11, local copies, waits for them, and re-layouts: 14.1 us -> 2.93 us
    all_gather x1, waiting for transfers between devices: 80.3 us -> 90.8 us  [per_device(): lax.all_gather(query.reshape(rows, width_loc), 'kv', axis=1, tiled=True)]
  transfers between devices with their start and end apart: 8 -> 8, of which waited for: 8 -> 8; matrix products, arithmetic and copies ran while one was open for 4% -> 8% of each run, Pallas kernels for 0% -> 0%
where the time goes in v2:
time: 876 us; the launch traced here: 874 us
  waiting for transfers between devices  699 us (80%)
  Pallas kernels  63.2 us (7%)
  other arithmetic  46.5 us (5%)
  matrix products  30.5 us (3%)
  local copies, waits for them, and re-layouts  20.7 us (2%)
  between operations  13.7 us (2%)
    reduce_scatter x1, waiting for transfers between devices, per_device(): summed = lax.psum_scatter(packed, 'kv', scatter_dimension=0, tiled=True)  235 us
    reduce_scatter x1, waiting for transfers between devices, per_device(): summed = lax.psum_scatter(value, 'kv', scatter_dimension=1, tiled=True)  200 us
    all_gather x1, waiting for transfers between devices, per_device(): lax.all_gather(query.reshape(rows, width_loc), 'kv', axis=1, tiled=True)  90.8 us
    pallas_call x1, Pallas kernels, attend_pages(): pl.pallas_call(attend_kernel, grid=(groups, heads), in_specs=[pl.BlockSpe...  63.2 us
    all_gather x1, waiting for transfers between devices, per_device(): lax.all_gather(with_new, 'kv', axis=0, tiled=False)  61.3 us
    all_gather x1, waiting for transfers between devices, per_device(): down_piece = lax.all_gather(down_weight, 'req', axis=1, tiled=True)  48.9 us
    all_gather x1, waiting for transfers between devices, per_device(): qkv_piece = lax.all_gather(qkv_weight, 'req', axis=0, tiled=True)  32.8 us
  transfers between devices with their start and end apart: 8, of which 8 were waited for; matrix products, arithmetic and copies ran while one was open for 8% of the time, Pallas kernels for 0%

profile of v2, /device:TPU:0, one launch (start us, length us, event | category | flops | bytes accessed | tf_op | source)
XLA Modules:
  0.0 874.3 jit_solution(5277916846242197315)
XLA Ops:
  6.5 2.3 copy.72
  8.9 0.7 convert_bitcast_fusion
  9.6 2.8 convert_reduce_fusion
  12.5 3.4 multiply_reduce_fusion
  15.9 32.8 %all-gather.7.cloned.1.call-done = bf16[4096,3,128]{0,2,1:T(8,128)(2,1)} async-done(((bf16[1024,3,128]{0,2,1:T(8,128)(2,1)}), bf16[4096,3,128]{0,2,1:T(8,128)(2,1)}) %all-gather.7.cloned.1.call-update) | async-done | bytes 3145744 | tf_op jit(solution)/shard_map/all_gather | solution.py:109
  48.8 5.9 fusion.8
  54.8 1.3 fusion.72
  56.1 0.8 pad_maximum_fusion.1
  58.8 90.8 %all-gather.9.cloned.1.call-done.q_ref = bf16[512,4096]{1,0:T(8,128)(2,1)} async-done(((bf16[512,128]{1,0:T(8,128)(2,1)}), bf16[512,4096]{1,0:T(8,128)(2,1)}) %all-gather.9.cloned.1.call-update) | async-done | bytes 4194320 | tf_op jit(solution)/shard_map/all_gather | solution.py:135
  149.5 63.2 %shard_map.91 = (f32[32,2,256,128]{3,2,1,0:T(8,128)}, f32[32,2,256,1]{3,2,1,0:T(8,128)}, f32[32,2,256,1]{3,2,1,0:T(8,128)}) custom-call(bf16[512,4096]{1,0:T(8,128)(2,1)} %all-gather.9.cloned.1.call-done.q_ref, bf16[8,2,32,128,128]{4,3,2,1,0:T(8,128)(2,1)} %bitcast.71, bf16[8,2,32,128,128]{4,3,2,1,0:T(8,128)(2,1)} %bitcast.72, ...), custom_call_target="tpu_custom_call" | custom-call | flops 8589934592 | bytes 46137344 | tf_op jit(solution)/shard_map/pallas_call | solution.py:59
  212.7 5.2 copy.76
  218.0 1.1 dynamic-slice_reduce_fusion
  221.2 5.7 reduce.5
  226.9 61.3 %all-gather.11.cloned.1.call-done = f32[32,32,2,256]{3,1,2,0:T(8,128)} async-done(((f32[1,32,2,256]{3,1,2,0:T(8,128)}), f32[32,32,2,256]{3,1,2,0:T(8,128)}) %all-gather.11.cloned.1.call-update) | async-done | bytes 2097168 | tf_op jit(solution)/shard_map/all_gather | solution.py:162
  288.2 1.7 reduce_max.26
  289.9 4.6 copy.78
  294.6 11.4 %subtract_exponential_fusion = (f32[32,2,256,1]{3,2,1,0:T(8,128)}, f32[32,2,256]{2,1,0:T(2,128)S(1)}) fusion(f32[32,2,256,1]{3,2,1,0:T(8,128)} %get-tuple-element.9, f32[32,2,256,1]{3,2,1,0:T(8,128)} %copy.78), kind=kLoop, calls=%fused_computation.2 | loop fusion | flops 16384 | bytes 262144 | tf_op jit(solution)/shard_map/exp | solution.py:163
  306.0 5.3 copy.79
  311.5 5.3 broadcast_multiply_fusion
  316.8 4.0 pad_maximum_fusion
  320.9 0.7 all-gather.13.cloned.1.call-update
  322.0 11.6 %all-gather.15.cloned.1.call-done = bf16[4096,512]{1,0:T(8,128)(2,1)} async-done(((bf16[1024,512]{1,0:T(8,128)(2,1)}), bf16[4096,512]{1,0:T(8,128)(2,1)}) %all-gather.15.cloned.1.call-update) | async-done | bytes 4194320 | tf_op jit(solution)/shard_map/all_gather | solution.py:110
  333.6 48.9 %all-gather.17.cloned.1.call-done = bf16[512,4096]{1,0:T(8,128)(2,1)} async-done(((bf16[512,1024]{1,0:T(8,128)(2,1)}), bf16[512,4096]{1,0:T(8,128)(2,1)}) %all-gather.17.cloned.1.call-update) | async-done | bytes 4194320 | tf_op jit(solution)/shard_map/all_gather | solution.py:177
  382.5 14.6 %fusion.28 = f32[512,4096]{1,0:T(8,128)} fusion(bf16[512,4096]{1,0:T(8,128)(2,1)} %all-gather.17.cloned.1.call-done, bf16[4096,512]{1,0:T(8,128)(2,1)} %all-gather.15.cloned.1.call-done, bf16[512,4096]{1,0:T(8,128)(2,1)} %param.9, f32[4096]{0:T(1024)S(1)} %bitcast.87, f32[512]{0:T(512)S(1)} %add_rsqrt_fusion, f32[512]{0:T(512)S(1)} %broadcast_multiply_fusion.1), kind=kOutput, calls=%fused_computation.42 | convolution fusion | flops 4322492416 | bytes 20992000 | tf_op jit(solution)/shard_map/dot_general | solution.py:178
  397.1 234.7 %reduce-scatter.3.cloned.1.call-done = f32[1,2,258,128]{3,2,1,0:T(8,128)} async-done(((f32[32,2,258,128]{3,2,1,0:T(8,128)}), f32[1,2,258,128]{3,2,1,0:T(8,128)}) %reduce-scatter.3.cloned.1.call-update) | async-done | bytes 264208 | tf_op jit(solution)/shard_map/reduce_scatter | solution.py:166
  631.8 0.7 slice.64
  632.5 1.3 fusion.17
  633.8 16.7 %all-gather.13.cloned.1.call-done = bf16[128,4096]{1,0:T(8,128)(2,1)} async-done(((bf16[128,1024]{1,0:T(8,128)(2,1)}), bf16[128,4096]{1,0:T(8,128)(2,1)}) %all-gather.13.cloned.1.call-update) | async-done | bytes 1048592 | tf_op jit(solution)/shard_map/all_gather | solution.py:176
  650.6 8.2 convolution_add_fusion
  658.8 6.5 convert_element_type.63
  665.3 200.4 %reduce-scatter.5.cloned.1.call-done = f32[512,128]{1,0:T(8,128)} async-done(((f32[512,4096]{1,0:T(8,128)}), f32[512,128]{1,0:T(8,128)}) %reduce-scatter.5.cloned.1.call-update) | async-done | bytes 262160 | tf_op jit(solution)/shard_map/reduce_scatter | solution.py:181
  865.7 1.8 dynamic-slice_add_fusion
  (55 shorter events, 4.8 us)
Async XLA Ops:
  6.5 9.4 %copy-start.1 = (f32[2,4096]{1,0:T(2,128)S(1)}, f32[2,4096]{1,0:T(2,128)}, u32[]{:S(2)}) copy-start(f32[2,4096]{1,0:T(2,128)} %param.10) | copy-start | bytes 98308
  6.5 42.2 %all-gather.7.cloned.1.call-start = ((), (), s32[]{:S(2)}) async-start(), calls=%async_computation.2 | async-start | bytes 3932160 | tf_op jit(solution)/shard_map/all_gather | solution.py:109
  8.9 140.7 %all-gather.9.cloned.1.call-start = ((), (), s32[]{:S(2)}) async-start(), calls=%async_computation.3 | async-start | bytes 4325376 | tf_op jit(solution)/shard_map/all_gather | solution.py:135
  48.8 8.3 copy-start.3
  48.8 8.7 copy-start.2
  57.0 231.2 %all-gather.11.cloned.1.call-start = ((), (), s32[]{:S(2)}) async-start(), calls=%async_computation.4 | async-start | bytes 2162688 | tf_op jit(solution)/shard_map/all_gather | solution.py:162
  219.1 0.6 copy-start
  219.8 113.8 %all-gather.15.cloned.1.call-start = ((), (), s32[]{:S(2)}) async-start(), calls=%async_computation.7 | async-start | bytes 5242880 | tf_op jit(solution)/shard_map/all_gather | solution.py:110
  220.4 162.1 %all-gather.17.cloned.1.call-start = ((), (), s32[]{:S(2)}) async-start(), calls=%async_computation.8 | async-start | bytes 5242880 | tf_op jit(solution)/shard_map/all_gather | solution.py:177
  221.0 410.8 %reduce-scatter.3.cloned.1.call-start = ((), (), s32[]{:S(2)}) async-start(), calls=%async_computation.5 | async-start | bytes 8921088 | tf_op jit(solution)/shard_map/reduce_scatter | solution.py:166
  320.9 329.7 %all-gather.13.cloned.1.call-start = ((), (), s32[]{:S(2)}) async-start(), calls=%async_computation.6 | async-start | bytes 1310720 | tf_op jit(solution)/shard_map/all_gather | solution.py:176
  321.6 544.1 %reduce-scatter.5.cloned.1.call-start = ((), (), s32[]{:S(2)}) async-start(), calls=%async_computation.9 | async-start | bytes 8650752 | tf_op jit(solution)/shard_map/reduce_scatter | solution.py:181
Sparse Core Ops, SparseCore 0:
  9.0 39.7 all-gather.6
  57.1 92.3 all-gather.8
  219.9 68.2 all-gather.10
  289.7 43.8 all-gather.14
  335.1 47.3 all-gather.16
  387.6 244.1 reduce-scatter.2
  633.4 17.1 all-gather.12
  658.9 206.6 reduce-scatter.4

commit v3 on v2

--- a/solution.py
+++ b/solution.py
@@ -9,6 +9,36 @@
 HD = 128
 ROT = 32
 PAGE = 128
+KV = ("z", "xh", "y")
+
+
+def head_slot(h, nz, nxh, ny):
+    return (h % ny * nz + h // (nxh * ny)) * nxh + h // ny % nxh
+
+
+def by_slot(w, split):
+    nz, nxh, ny = split
+    lead = w.shape[0]
+    blocks = w.reshape(lead, nz, nxh, ny, w.shape[1] // (nz * nxh * ny))
+    return jnp.transpose(blocks, (0, 3, 1, 2, 4)).reshape(w.shape)
+
+
+def scatter_staged(x, dim):
+    for name in ("y", "z", "xh"):
+        x = lax.psum_scatter(x, name, scatter_dimension=dim, tiled=True)
+    return x
+
+
+def gather_staged(x, dim):
+    for name in ("y", "xh", "z"):
+        x = lax.all_gather(x, name, axis=dim, tiled=True)
+    return x
+
+
+def max_staged(x):
+    for name in ("y", "xh", "z"):
+        x = jnp.max(lax.all_gather(x, name, axis=0, tiled=False), axis=0)
+    return x
 
 
 def layer_norm(x, gain):
@@ -49,7 +79,7 @@
     acc_ref[...] = jnp.dot(weights, v, preferred_element_type=jnp.float32)
 
 
-def attend_pages(q_all, local_cache, live):
+def attend_pages(q_all, local_cache, live, split):
     groups, span = live.shape[0], q_all.shape[0] // live.shape[0]
     slots = local_cache.shape[0]
     heads = local_cache.shape[2]
@@ -66,9 +96,9 @@
             pl.BlockSpec((None, 1, slots * PAGE), lambda g, h: (g, 0, 0)),
         ],
         out_specs=[
-            pl.BlockSpec((None, None, span, HD), lambda g, h: (h, g, 0, 0)),
-            pl.BlockSpec((None, None, span, 1), lambda g, h: (h, g, 0, 0)),
-            pl.BlockSpec((None, None, span, 1), lambda g, h: (h, g, 0, 0)),
+            pl.BlockSpec((None, None, span, HD), lambda g, h: (head_slot(h, *split), g, 0, 0)),
+            pl.BlockSpec((None, None, span, 1), lambda g, h: (head_slot(h, *split), g, 0, 0)),
+            pl.BlockSpec((None, None, span, 1), lambda g, h: (head_slot(h, *split), g, 0, 0)),
         ],
         out_shape=[
             jax.ShapeDtypeStruct((heads, groups, span, HD), jnp.float32),
@@ -95,8 +125,10 @@
     cached_len,
     page_table,
 ):
-    n_kv = lax.axis_size("kv")
-    me_kv = lax.axis_index("kv")
+    split = tuple(lax.axis_size(name) for name in KV)
+    n_kv = split[0] * split[1] * split[2]
+    me_kv = lax.axis_index(KV)
+    slot_me = head_slot(me_kv, *split)
     rows = hidden_in.shape[0]
     groups_here = cached_len.shape[0]
     span_rows = rows // groups_here
@@ -132,7 +164,7 @@
     )
     total_new = jnp.sum(p_new.astype(jnp.float32), axis=-1)
     accum_new = jnp.einsum("ghqk,gkhd->ghqd", p_new, v_grp, preferred_element_type=jnp.float32)
-    q_all = lax.all_gather(query.reshape(rows, width_loc), "kv", axis=1, tiled=True)
+    q_all = gather_staged(query.reshape(rows, width_loc), 1)
     local_cache = cache[0]
     slots_here = local_cache.shape[0]
     slot_ids = me_kv * slots_here + jnp.arange(slots_here, dtype=jnp.int32)
@@ -149,53 +181,54 @@
         owner_page[None, :, None] * PAGE + page_pos[None, None, :] < cached_len[:, None, None]
     )
     live = live.astype(jnp.int32).reshape(groups_here, 1, slots_here * PAGE)
-    accums, tops, totals = attend_pages(q_all, local_cache, live)
+    accums, tops, totals = attend_pages(q_all, local_cache, live, split)
     tops = tops.reshape(HEADS, groups_here, span_rows)
     totals = totals.reshape(HEADS, groups_here, span_rows)
     top_new = jnp.transpose(top_new, (1, 0, 2))
     total_new = jnp.transpose(total_new, (1, 0, 2))
     accum_new = jnp.transpose(accum_new, (1, 0, 2, 3))
-    own = lax.dynamic_slice_in_dim(tops, me_kv * heads_loc, heads_loc, 0)
-    with_new = lax.dynamic_update_slice_in_dim(
-        tops, jnp.maximum(own, top_new), me_kv * heads_loc, 0
-    )
-    largest = jnp.max(lax.all_gather(with_new, "kv", axis=0, tiled=False), axis=0)
+    own = lax.dynamic_slice_in_dim(tops, slot_me, heads_loc, 0)
+    with_new = lax.dynamic_update_slice_in_dim(tops, jnp.maximum(own, top_new), slot_me, 0)
+    largest = max_staged(with_new)
     factor = jnp.exp(tops - largest)
     tot_rows = (totals * factor).reshape(HEADS, groups_here, span_rows // HD, HD)
     packed = jnp.concatenate([accums * factor[..., None], tot_rows], axis=2)
-    summed = lax.psum_scatter(packed, "kv", scatter_dimension=0, tiled=True)
+    summed = scatter_staged(packed, 0)
     sum_acc = summed[:, :, :span_rows]
     sum_tot = summed[:, :, span_rows:].reshape(heads_loc, groups_here, span_rows)
-    own_largest = lax.dynamic_slice_in_dim(largest, me_kv * heads_loc, heads_loc, 0)
+    own_largest = lax.dynamic_slice_in_dim(largest, slot_me, heads_loc, 0)
     fresh = jnp.exp(top_new - own_largest)
     numer = sum_acc + accum_new * fresh[..., None]
     denom = sum_tot + total_new * fresh
     att = (numer / denom[..., None]).astype(jnp.bfloat16)
     att = jnp.transpose(att, (1, 2, 0, 3)).reshape(rows, width_loc)
     hidden = jax.nn.gelu(up_acc, approximate=False).astype(jnp.bfloat16)
-    dense_piece = lax.all_gather(dense_weight, "req", axis=1, tiled=True)
-    down_piece = lax.all_gather(down_weight, "req", axis=1, tiled=True)
+    dense_piece = by_slot(lax.all_gather(dense_weight, "req", axis=1, tiled=True), split)
+    down_piece = by_slot(lax.all_gather(down_weight, "req", axis=1, tiled=True), split)
     value = jnp.dot(att, dense_piece, preferred_element_type=jnp.float32) + jnp.dot(
         hidden, down_piece, preferred_element_type=jnp.float32
     )
-    summed = lax.psum_scatter(value, "kv", scatter_dimension=1, tiled=True)
+    summed = scatter_staged(value, 1)
     width_out = D // n_kv
     residual = lax.dynamic_slice_in_dim(x, me_kv * width_out, width_out, 1)
     return residual + summed
 
 
 def solution(mesh):
+    kv_split = (4, 2, 4)
+    devices = mesh.devices.reshape((mesh.shape["req"],) + kv_split)
+    torus = jax.sharding.Mesh(devices, ("req",) + KV)
     placed = (
         P("req", None),
         P(),
-        P("req", None, "kv"),
-        P("kv", "req"),
-        P("req", "kv"),
-        P("kv", "req"),
-        P("req", "kv", None, None, None, None),
+        P("req", None, KV),
+        P(KV, "req"),
+        P("req", KV),
+        P(KV, "req"),
+        P("req", KV, None, None, None, None),
         P("req"),
         P("req", None),
     )
     return jax.shard_map(
-        per_device, mesh=mesh, in_specs=placed, out_specs=P("req", "kv"), check_vma=False
-    )
+        per_device, mesh=torus, in_specs=placed, out_specs=P("req", KV), check_vma=False
+    )

time: 876 us -> 693 us (0.79)
  waiting for transfers between devices: 699 us -> 464 us
  blocking collectives: 0 us -> 46.7 us
    reduce_scatter x2 -> x6, waiting for transfers between devices: 435 us -> 243 us  [scatter_staged(): x = lax.psum_scatter(x, name, scatter_dimension=dim, tiled=True)]
    all_gather x4, waiting for transfers between devices: 218 us -> 141 us  [the longest x2 73.3 us: gather_staged(): x = lax.all_gather(x, name, axis=dim, tiled=True)]
    all_gather x0 -> x4, blocking collectives: none -> 46.7 us  [the longest x3 31.7 us: max_staged(): x = jnp.max(lax.all_gather(x, name, axis=0, tiled=False), axis=0)]
    all_gather x1, waiting for transfers between devices: 11.6 us -> 46.8 us  [per_device(): up_piece = lax.all_gather(up_weight, 'req', axis=0, tiled=True)]
  transfers between devices with their start and end apart: 8 -> 12, of which waited for: 8 -> 12; matrix products, arithmetic and copies ran while one was open for 8% -> 5% of each run, Pallas kernels for 0% -> 0%
where the time goes in v3:
time: 693 us; the launch traced here: 691 us
  waiting for transfers between devices  464 us (67%)
  Pallas kernels  63.2 us (9%)
  blocking collectives  46.7 us (7%)
  other arithmetic  42.6 us (6%)
  matrix products  30.2 us (4%)
  local copies, waits for them, and re-layouts  29.3 us (4%)
  between operations  13.9 us (2%)
    reduce_scatter x6, waiting for transfers between devices, scatter_staged(): x = lax.psum_scatter(x, name, scatter_dimension=dim, tiled=True)  243 us
    all_gather x2, waiting for transfers between devices, gather_staged(): x = lax.all_gather(x, name, axis=dim, tiled=True)  73.3 us
    pallas_call x1, Pallas kernels, attend_pages(): pl.pallas_call(attend_kernel, grid=(groups, heads), in_specs=[pl.BlockSpe...  63.2 us
    all_gather x1, waiting for transfers between devices, per_device(): lax.all_gather(down_weight, 'req', axis=1, tiled=True)  47.2 us
    all_gather x1, waiting for transfers between devices, per_device(): up_piece = lax.all_gather(up_weight, 'req', axis=0, tiled=True)  46.8 us
    all_gather x1, waiting for transfers between devices, per_device(): qkv_piece = lax.all_gather(qkv_weight, 'req', axis=0, tiled=True)  32.8 us
    all_gather x3, blocking collectives, max_staged(): x = jnp.max(lax.all_gather(x, name, axis=0, tiled=False), axis=0)  31.7 us
    all_gather x1, waiting for transfers between devices, per_device(): lax.all_gather(dense_weight, 'req', axis=1, tiled=True)  20.6 us
  transfers between devices with their start and end apart: 12, of which 12 were waited for; matrix products, arithmetic and copies ran while one was open for 5% of the time, Pallas kernels for 0%

profile of v3, /device:TPU:0, one launch (start us, length us, event | category | flops | bytes accessed | tf_op | source)
XLA Modules:
  0.0 690.7 jit_solution(1692946652037406762)
XLA Ops:
  6.5 2.3 copy.103
  9.7 2.8 convert_reduce_fusion
  12.5 3.4 multiply_reduce_fusion
  16.0 32.8 %all-gather.9.cloned.1.call-done = bf16[4096,3,128]{0,2,1:T(8,128)(2,1)} async-done(((bf16[1024,3,128]{0,2,1:T(8,128)(2,1)}), bf16[4096,3,128]{0,2,1:T(8,128)(2,1)}) %all-gather.9.cloned.1.call-update) | async-done | bytes 3145744 | tf_op jit(solution)/shard_map/all_gather | solution.py:141
  48.8 5.9 fusion.8
  56.3 15.0 %all_gather.40 = bf16[512,512]{1,0:T(8,128)(2,1)} all-gather(bf16[512,128]{1,0:T(8,128)(2,1)S(1)} %pad_maximum_fusion.1), channel_id=1, replica_groups=mesh['req'=4,'z'=4,'xh'=2,'y'=4] {'y'}, dimensions={1}, use_global_device_ids=true | all-gather | bytes 655360 | tf_op jit(solution)/shard_map/all_gather | solution.py:34
  71.4 25.6 %all-gather.11.cloned.1.call-done = bf16[512,1024]{1,0:T(8,128)(2,1)} async-done(((bf16[512,512]{1,0:T(8,128)(2,1)}), bf16[512,1024]{1,0:T(8,128)(2,1)}) %all-gather.11.cloned.1.call-update) | async-done | bytes 1048592 | tf_op jit(solution)/shard_map/all_gather | solution.py:34
  98.9 47.7 %all-gather.13.cloned.1.call-done.q_ref = bf16[512,4096]{1,0:T(8,128)(2,1)} async-done(((bf16[512,1024]{1,0:T(8,128)(2,1)}), bf16[512,4096]{1,0:T(8,128)(2,1)}) %all-gather.13.cloned.1.call-update) | async-done | bytes 4194320 | tf_op jit(solution)/shard_map/all_gather | solution.py:34
  146.6 63.2 %shard_map.91 = (f32[32,2,256,128]{3,2,1,0:T(8,128)}, f32[32,2,256,1]{3,2,1,0:T(8,128)}, f32[32,2,256,1]{3,2,1,0:T(8,128)}) custom-call(bf16[512,4096]{1,0:T(8,128)(2,1)} %all-gather.13.cloned.1.call-done.q_ref, bf16[8,2,32,128,128]{4,3,2,1,0:T(8,128)(2,1)} %bitcast.85, bf16[8,2,32,128,128]{4,3,2,1,0:T(8,128)(2,1)} %bitcast.86, ...), custom_call_target="tpu_custom_call" | custom-call | flops 8589934592 | bytes 46137344 | tf_op jit(solution)/shard_map/pallas_call | solution.py:89
  209.7 5.2 copy.107
  216.1 12.6 %all_gather.44 = f32[4,32,2,256]{3,1,2,0:T(8,128)S(1)} all-gather(f32[1,32,2,256]{3,1,2,0:T(8,128)S(1)} %dynamic_update_slice.4), channel_id=1, replica_groups=mesh['req'=4,'z'=4,'xh'=2,'y'=4] {'y'}, dimensions={0}, use_global_device_ids=true | all-gather | bytes 327680 | tf_op jit(solution)/shard_map/all_gather | solution.py:40
  228.8 6.4 all-gather
  235.3 12.6 %all-gather.1 = f32[128,2,256]{2,1,0:T(2,128)S(1)} all-gather(f32[32,2,256]{2,1,0:T(2,128)S(1)} %reduce_max.45), channel_id=3, replica_groups=mesh['req'=4,'z'=4,'xh'=2,'y'=4] {'z'}, dimensions={0}, use_global_device_ids=true | all-gather | bytes 327680 | tf_op jit(solution)/shard_map/all_gather | solution.py:40
  248.2 4.9 copy.111
  253.0 9.7 %subtract_exponential_fusion = (f32[32,2,256,1]{3,2,1,0:T(8,128)}, f32[32,2,256]{2,1,0:T(2,128)S(1)}) fusion(f32[32,2,256,1]{3,2,1,0:T(8,128)} %get-tuple-element.9, f32[32,2,256,1]{3,2,1,0:T(8,128)} %copy.111), kind=kLoop, calls=%fused_computation.2 | loop fusion | flops 16384 | bytes 262144 | tf_op jit(solution)/shard_map/exp | solution.py:193
  262.8 5.2 copy.112
  268.1 5.7 reduce.5
  273.9 5.2 broadcast_multiply_fusion
  279.2 4.0 pad_maximum_fusion
  286.5 78.4 %reduce-scatter.7.cloned.1.call-done = f32[8,2,258,128]{3,2,1,0:T(8,128)} async-done(((f32[32,2,258,128]{3,2,1,0:T(8,128)}), f32[8,2,258,128]{3,2,1,0:T(8,128)}) %reduce-scatter.7.cloned.1.call-update) | async-done | bytes 2113552 | tf_op jit(solution)/shard_map/reduce_scatter | solution.py:28
  365.7 20.6 %all-gather.15.cloned.1.call-done = bf16[128,4096]{0,1:T(8,128)(2,1)} async-done(((bf16[128,1024]{0,1:T(8,128)(2,1)}), bf16[128,4096]{0,1:T(8,128)(2,1)}) %all-gather.15.cloned.1.call-update) | async-done | bytes 1048592 | tf_op jit(solution)/shard_map/all_gather | solution.py:206
  387.8 47.2 %all-gather.19.cloned.1.call-done = bf16[512,4096]{0,1:T(8,128)(2,1)} async-done(((bf16[512,1024]{0,1:T(8,128)(2,1)}), bf16[512,4096]{0,1:T(8,128)(2,1)}) %all-gather.19.cloned.1.call-update) | async-done | bytes 4194320 | tf_op jit(solution)/shard_map/all_gather | solution.py:207
  435.0 4.5 copy.125
  439.5 29.9 %reduce-scatter.9.cloned.1.call-done = f32[2,2,258,128]{3,2,1,0:T(8,128)} async-done(((f32[8,2,258,128]{3,2,1,0:T(8,128)}), f32[2,2,258,128]{3,2,1,0:T(8,128)}) %reduce-scatter.9.cloned.1.call-update) | async-done | bytes 528400 | tf_op jit(solution)/shard_map/reduce_scatter | solution.py:28
  469.8 46.8 %all-gather.17.cloned.1.call-done = bf16[4096,512]{1,0:T(8,128)(2,1)} async-done(((bf16[1024,512]{1,0:T(8,128)(2,1)}), bf16[4096,512]{1,0:T(8,128)(2,1)}) %all-gather.17.cloned.1.call-update) | async-done | bytes 4194320 | tf_op jit(solution)/shard_map/all_gather | solution.py:142
  516.5 14.6 %fusion.28 = f32[512,4096]{1,0:T(8,128)} fusion(bf16[512,4096]{0,1:T(8,128)(2,1)} %bitcast.89, bf16[4096,512]{1,0:T(8,128)(2,1)} %all-gather.17.cloned.1.call-done, bf16[512,4096]{1,0:T(8,128)(2,1)} %param.9, f32[4096]{0:T(1024)S(1)} %bitcast.107, f32[512]{0:T(512)S(1)} %add_rsqrt_fusion, f32[512]{0:T(512)S(1)} %broadcast_multiply_fusion.1), kind=kOutput, calls=%fused_computation.42 | convolution fusion | flops 4322492416 | bytes 20992000 | tf_op jit(solution)/shard_map/dot_general | solution.py:208
  531.1 8.2 %reduce-scatter.11.cloned.1.call-done = f32[1,2,258,128]{3,2,1,0:T(8,128)} async-done(((f32[2,2,258,128]{3,2,1,0:T(8,128)}), f32[1,2,258,128]{3,2,1,0:T(8,128)}) %reduce-scatter.11.cloned.1.call-update) | async-done | bytes 264208 | tf_op jit(solution)/shard_map/reduce_scatter | solution.py:28
  541.4 7.9 %convolution_add_fusion = f32[512,4096]{1,0:T(8,128)} fusion(f32[512,4096]{1,0:T(8,128)} %fusion.28, bf16[512,128]{1,0:T(8,128)(2,1)S(1)} %bitcast.104, bf16[128,4096]{0,1:T(8,128)(2,1)S(1)} %bitcast.87), kind=kOutput, calls=%fused_computation.6 | convolution fusion | flops 538968064 | bytes 17956864 | tf_op jit(solution)/shard_map/dot_general | solution.py:208
  549.4 80.1 %reduce-scatter.13.cloned.1.call-done = f32[512,1024]{1,0:T(8,128)} async-done(((f32[512,4096]{1,0:T(8,128)}), f32[512,1024]{1,0:T(8,128)}) %reduce-scatter.13.cloned.1.call-update) | async-done | bytes 2097168 | tf_op jit(solution)/shard_map/reduce_scatter | solution.py:28
  629.6 32.0 %reduce-scatter.15.cloned.1.call-done = f32[512,256]{1,0:T(8,128)} async-done(((f32[512,1024]{1,0:T(8,128)}), f32[512,256]{1,0:T(8,128)}) %reduce-scatter.15.cloned.1.call-update) | async-done | bytes 524304 | tf_op jit(solution)/shard_map/reduce_scatter | solution.py:28
  661.6 6.5 convert_element_type.63
  668.1 13.9 %reduce-scatter.17.cloned.1.call-done = f32[512,128]{1,0:T(8,128)} async-done(((f32[512,256]{1,0:T(8,128)}), f32[512,128]{1,0:T(8,128)}) %reduce-scatter.17.cloned.1.call-update) | async-done | bytes 262160 | tf_op jit(solution)/shard_map/reduce_scatter | solution.py:28
  (80 shorter events, 15.7 us)
Async XLA Ops:
  6.5 9.4 %copy-start.2 = (f32[2,4096]{1,0:T(2,128)S(1)}, f32[2,4096]{1,0:T(2,128)}, u32[]{:S(2)}) copy-start(f32[2,4096]{1,0:T(2,128)} %param.10) | copy-start | bytes 98308
  6.5 42.2 %all-gather.9.cloned.1.call-start = ((), (), s32[]{:S(2)}) async-start(), calls=%async_computation.6 | async-start | bytes 3932160 | tf_op jit(solution)/shard_map/all_gather | solution.py:141
  8.9 88.1 %all-gather.11.cloned.1.call-start = ((), (), s32[]{:S(2)}) async-start(), calls=%async_computation.7 | async-start | bytes 1572864 | tf_op jit(solution)/shard_map/all_gather | solution.py:34
  48.8 48.4 %copy-start.4 = (s32[2,128]{1,0:T(2,128)S(1)}, s32[2,128]{1,0:T(2,128)}, u32[]{:S(2)}) copy-start(s32[2,128]{1,0:T(2,128)} %param.17) | copy-start | bytes 3076
  48.8 48.8 %copy-start.3 = (s32[2]{0:T(128)S(1)}, s32[2]{0:T(128)}, u32[]{:S(2)}) copy-start(s32[2]{0:T(128)} %param.16) | copy-start | bytes 28
  71.3 75.3 %all-gather.13.cloned.1.call-start = ((), (), s32[]{:S(2)}) async-start(), calls=%async_computation.8 | async-start | bytes 5242880 | tf_op jit(solution)/shard_map/all_gather | solution.py:34
  97.0 267.9 %reduce-scatter.7.cloned.1.call-start = ((), (), s32[]{:S(2)}) async-start(), calls=%async_computation.9 | async-start | bytes 10813440 | tf_op jit(solution)/shard_map/reduce_scatter | solution.py:28
  283.2 0.9 copy-start.1
  283.2 1.9 copy-start
  283.2 103.1 %all-gather.15.cloned.1.call-start = ((), (), s32[]{:S(2)}) async-start(), calls=%async_computation.12 | async-start | bytes 1310720 | tf_op jit(solution)/shard_map/all_gather | solution.py:206
  285.0 150.0 %all-gather.19.cloned.1.call-start = ((), (), s32[]{:S(2)}) async-start(), calls=%async_computation.14 | async-start | bytes 5242880 | tf_op jit(solution)/shard_map/all_gather | solution.py:207
  286.4 183.1 %reduce-scatter.9.cloned.1.call-start = ((), (), s32[]{:S(2)}) async-start(), calls=%async_computation.10 | async-start | bytes 2703360 | tf_op jit(solution)/shard_map/reduce_scatter | solution.py:28
  364.9 151.6 %all-gather.17.cloned.1.call-start = ((), (), s32[]{:S(2)}) async-start(), calls=%async_computation.13 | async-start | bytes 5242880 | tf_op jit(solution)/shard_map/all_gather | solution.py:142
  365.7 173.7 %reduce-scatter.11.cloned.1.call-start = ((), (), s32[]{:S(2)}) async-start(), calls=%async_computation.11 | async-start | bytes 811008 | tf_op jit(solution)/shard_map/reduce_scatter | solution.py:28
  469.5 160.0 %reduce-scatter.13.cloned.1.call-start = ((), (), s32[]{:S(2)}) async-start(), calls=%async_computation.15 | async-start | bytes 10485760 | tf_op jit(solution)/shard_map/reduce_scatter | solution.py:28
  549.4 112.2 %reduce-scatter.15.cloned.1.call-start = ((), (), s32[]{:S(2)}) async-start(), calls=%async_computation.16 | async-start | bytes 2621440 | tf_op jit(solution)/shard_map/reduce_scatter | solution.py:28
  629.5 52.5 %reduce-scatter.17.cloned.1.call-start = ((), (), s32[]{:S(2)}) async-start(), calls=%async_computation.17 | async-start | bytes 786432 | tf_op jit(solution)/shard_map/reduce_scatter | solution.py:28
Sparse Core Ops, SparseCore 0:
  9.0 39.7 all-gather.8
  71.4 25.5 all-gather.10
  98.7 47.8 all-gather.12
  283.3 81.5 reduce-scatter.6
  366.4 19.8 all-gather.14
  387.8 47.1 all-gather.18
  437.4 32.0 reduce-scatter.8
  471.1 45.3 all-gather.16
  518.9 20.4 reduce-scatter.10
  549.5 79.9 reduce-scatter.12
  631.9 29.6 reduce-scatter.14
  663.8 18.2 reduce-scatter.16

commit v4 on v3

--- a/solution.py
+++ b/solution.py
@@ -139,12 +139,10 @@
     h1 = layer_norm(x, ln_gains[0]).astype(jnp.bfloat16)
     h2 = layer_norm(x, ln_gains[1]).astype(jnp.bfloat16)
     qkv_piece = lax.all_gather(qkv_weight, "req", axis=0, tiled=True)
-    up_piece = lax.all_gather(up_weight, "req", axis=0, tiled=True)
     count = qkv_piece.shape[0]
     qkv_acc = jnp.dot(
         h1, qkv_piece.reshape(count, 3 * width_loc), preferred_element_type=jnp.float32
     )
-    up_acc = jnp.dot(h2, up_piece, preferred_element_type=jnp.float32)
     qkv = qkv_acc
     qkv = qkv.reshape(rows, 3, heads_loc, HD)
     offsets = jnp.arange(span_rows, dtype=jnp.int32)
@@ -165,6 +163,12 @@
     total_new = jnp.sum(p_new.astype(jnp.float32), axis=-1)
     accum_new = jnp.einsum("ghqk,gkhd->ghqd", p_new, v_grp, preferred_element_type=jnp.float32)
     q_all = gather_staged(query.reshape(rows, width_loc), 1)
+    up_weight, dense_weight, down_weight, q_all = lax.optimization_barrier(
+        (up_weight, dense_weight, down_weight, q_all)
+    )
+    up_piece = lax.all_gather(up_weight, "req", axis=0, tiled=True)
+    dense_piece = by_slot(lax.all_gather(dense_weight, "req", axis=1, tiled=True), split)
+    down_piece = by_slot(lax.all_gather(down_weight, "req", axis=1, tiled=True), split)
     local_cache = cache[0]
     slots_here = local_cache.shape[0]
     slot_ids = me_kv * slots_here + jnp.arange(slots_here, dtype=jnp.int32)
@@ -193,6 +197,9 @@
     factor = jnp.exp(tops - largest)
     tot_rows = (totals * factor).reshape(HEADS, groups_here, span_rows // HD, HD)
     packed = jnp.concatenate([accums * factor[..., None], tot_rows], axis=2)
+    packed, up_piece, dense_piece, down_piece = lax.optimization_barrier(
+        (packed, up_piece, dense_piece, down_piece)
+    )
     summed = scatter_staged(packed, 0)
     sum_acc = summed[:, :, :span_rows]
     sum_tot = summed[:, :, span_rows:].reshape(heads_loc, groups_here, span_rows)
@@ -202,9 +209,8 @@
     denom = sum_tot + total_new * fresh
     att = (numer / denom[..., None]).astype(jnp.bfloat16)
     att = jnp.transpose(att, (1, 2, 0, 3)).reshape(rows, width_loc)
+    up_acc = jnp.dot(h2, up_piece, preferred_element_type=jnp.float32)
     hidden = jax.nn.gelu(up_acc, approximate=False).astype(jnp.bfloat16)
-    dense_piece = by_slot(lax.all_gather(dense_weight, "req", axis=1, tiled=True), split)
-    down_piece = by_slot(lax.all_gather(down_weight, "req", axis=1, tiled=True), split)
     value = jnp.dot(att, dense_piece, preferred_element_type=jnp.float32) + jnp.dot(
         hidden, down_piece, preferred_element_type=jnp.float32
     )

time: 693 us -> 585 us (0.84)
  waiting for transfers between devices: 464 us -> 355 us
    all_gather x1, waiting for transfers between devices: 47.2 us -> 0.02 us  [per_device(): lax.all_gather(down_weight, 'req', axis=1, tiled=True)]
    all_gather x1, waiting for transfers between devices: 46.8 us -> 0.01 us  [per_device(): up_piece = lax.all_gather(up_weight, 'req', axis=0, tiled=True)]
    all_gather x1, waiting for transfers between devices: 20.6 us -> 0.01 us  [per_device(): lax.all_gather(dense_weight, 'req', axis=1, tiled=True)]
  transfers between devices with their start and end apart: 12 -> 12, of which waited for: 12 -> 9; matrix products, arithmetic and copies ran while one was open for 5% -> 14% of each run, Pallas kernels for 0% -> 11%
where the time goes in v4:
time: 585 us; the launch traced here: 582 us
  waiting for transfers between devices  355 us (61%)
  Pallas kernels  63.5 us (11%)
  blocking collectives  48.2 us (8%)
  other arithmetic  42.6 us (7%)
  matrix products  30.2 us (5%)
  local copies, waits for them, and re-layouts  28.4 us (5%)
  between operations  13.9 us (2%)
    reduce_scatter x6, waiting for transfers between devices, scatter_staged(): x = lax.psum_scatter(x, name, scatter_dimension=dim, tiled=True)  246 us
    all_gather x2, waiting for transfers between devices, gather_staged(): x = lax.all_gather(x, name, axis=dim, tiled=True)  75.1 us
    pallas_call x1, Pallas kernels, attend_pages(): pl.pallas_call(attend_kernel, grid=(groups, heads), in_specs=[pl.BlockSpe...  63.5 us
    all_gather x3, blocking collectives, max_staged(): x = jnp.max(lax.all_gather(x, name, axis=0, tiled=False), axis=0)  33.2 us
    all_gather x1, waiting for transfers between devices, per_device(): qkv_piece = lax.all_gather(qkv_weight, 'req', axis=0, tiled=True)  32.8 us
    all_gather x1, blocking collectives, gather_staged(): x = lax.all_gather(x, name, axis=dim, tiled=True)  15 us
    dot_general x1, matrix products, per_device(): jnp.dot(hidden, down_piece, preferred_element_type=jnp.float32)  14.6 us
  transfers between devices with their start and end apart: 12, of which 9 were waited for; matrix products, arithmetic and copies ran while one was open for 14% of the time, Pallas kernels for 11%

profile of v4, /device:TPU:0, one launch (start us, length us, event | category | flops | bytes accessed | tf_op | source)
XLA Modules:
  0.0 582.1 jit_solution(12788668315760026246)
XLA Ops:
  6.5 2.3 copy.103
  9.7 2.8 convert_reduce_fusion
  12.5 3.4 multiply_reduce_fusion
  16.0 32.8 %all-gather.9.cloned.1.call-done = bf16[4096,3,128]{0,2,1:T(8,128)(2,1)} async-done(((bf16[1024,3,128]{0,2,1:T(8,128)(2,1)}), bf16[4096,3,128]{0,2,1:T(8,128)(2,1)}) %all-gather.9.cloned.1.call-update) | async-done | bytes 3145744 | tf_op jit(solution)/shard_map/all_gather | solution.py:141
  48.8 6.0 %fusion.8 = f32[512,3,1,128]{3,0,2,1:T(8,128)S(1)} fusion(bf16[4096,3,128]{0,2,1:T(8,128)(2,1)} %all-gather.9.cloned.1.call-done, bf16[512,4096]{1,0:T(8,128)(2,1)} %param.9, f32[4096]{0:T(1024)S(1)} %bitcast.108, f32[512]{0:T(512)S(1)} %add_rsqrt_fusion, f32[512]{0:T(512)S(1)} %broadcast_multiply_fusion.1), kind=kOutput, calls=%fused_computation.16 | convolution fusion | flops 1621098496 | bytes 8146944 | tf_op jit(solution)/shard_map/dot_general | solution.py:143
  56.4 15.0 %all_gather.40 = bf16[512,512]{1,0:T(8,128)(2,1)} all-gather(bf16[512,128]{1,0:T(8,128)(2,1)S(1)} %pad_maximum_fusion.1), channel_id=1, replica_groups=mesh['req'=4,'z'=4,'xh'=2,'y'=4] {'y'}, dimensions={1}, use_global_device_ids=true | all-gather | bytes 655360 | tf_op jit(solution)/shard_map/all_gather | solution.py:34
  71.5 25.6 %all-gather.11.cloned.1.call-done = bf16[512,1024]{1,0:T(8,128)(2,1)} async-done(((bf16[512,512]{1,0:T(8,128)(2,1)}), bf16[512,1024]{1,0:T(8,128)(2,1)}) %all-gather.11.cloned.1.call-update) | async-done | bytes 1048592 | tf_op jit(solution)/shard_map/all_gather | solution.py:34
  97.2 49.5 %all-gather.13.cloned.1.call-done.q_ref = bf16[512,4096]{1,0:T(8,128)(2,1)} async-done(((bf16[512,1024]{1,0:T(8,128)(2,1)}), bf16[512,4096]{1,0:T(8,128)(2,1)}) %all-gather.13.cloned.1.call-update) | async-done | bytes 4194320 | tf_op jit(solution)/shard_map/all_gather | solution.py:34
  147.6 1.3 copy.123
  151.4 63.5 %shard_map.91 = (f32[32,2,256,128]{3,2,1,0:T(8,128)}, f32[32,2,256,1]{3,2,1,0:T(8,128)}, f32[32,2,256,1]{3,2,1,0:T(8,128)}) custom-call(bf16[512,4096]{1,0:T(8,128)(2,1)} %all-gather.13.cloned.1.call-done.q_ref, bf16[8,2,32,128,128]{4,3,2,1,0:T(8,128)(2,1)} %bitcast.85, bf16[8,2,32,128,128]{4,3,2,1,0:T(8,128)(2,1)} %bitcast.86, ...), custom_call_target="tpu_custom_call" | custom-call | flops 8589934592 | bytes 46137344 | tf_op jit(solution)/shard_map/pallas_call | solution.py:89
  214.9 5.7 reduce.5
  220.6 5.2 copy.107
  227.0 12.6 %all_gather.44 = f32[4,32,2,256]{3,1,2,0:T(8,128)S(1)} all-gather(f32[1,32,2,256]{3,1,2,0:T(8,128)S(1)} %dynamic_update_slice.4), channel_id=1, replica_groups=mesh['req'=4,'z'=4,'xh'=2,'y'=4] {'y'}, dimensions={0}, use_global_device_ids=true | all-gather | bytes 327680 | tf_op jit(solution)/shard_map/all_gather | solution.py:40
  239.7 8.0 %all-gather = f32[64,2,256]{2,1,0:T(2,128)S(1)} all-gather(f32[32,2,256]{2,1,0:T(2,128)S(1)} %copy.109), channel_id=2, replica_groups=mesh['req'=4,'z'=4,'xh'=2,'y'=4] {'xh'}, dimensions={0}, use_global_device_ids=true | all-gather | bytes 196608 | tf_op jit(solution)/shard_map/all_gather | solution.py:40
  247.7 12.7 %all-gather.1 = f32[128,2,256]{2,1,0:T(2,128)S(1)} all-gather(f32[32,2,256]{2,1,0:T(2,128)S(1)} %reduce_max.45), channel_id=3, replica_groups=mesh['req'=4,'z'=4,'xh'=2,'y'=4] {'z'}, dimensions={0}, use_global_device_ids=true | all-gather | bytes 327680 | tf_op jit(solution)/shard_map/all_gather | solution.py:40
  260.6 4.8 copy.111
  265.5 9.7 %subtract_exponential_fusion = (f32[32,2,256,1]{3,2,1,0:T(8,128)}, f32[32,2,256]{2,1,0:T(2,128)S(1)}) fusion(f32[32,2,256,1]{3,2,1,0:T(8,128)} %get-tuple-element.18, f32[32,2,256,1]{3,2,1,0:T(8,128)} %copy.111), kind=kLoop, calls=%fused_computation.2 | loop fusion | flops 16384 | bytes 262144 | tf_op jit(solution)/shard_map/exp | solution.py:197
  275.3 5.2 copy.112
  280.7 5.2 broadcast_multiply_fusion
  285.9 4.0 pad_maximum_fusion
  291.2 4.6 copy.124
  295.9 81.5 %reduce-scatter.7.cloned.1.call-done = f32[8,2,258,128]{3,2,1,0:T(8,128)} async-done(((f32[32,2,258,128]{3,2,1,0:T(8,128)}), f32[8,2,258,128]{3,2,1,0:T(8,128)}) %reduce-scatter.7.cloned.1.call-update) | async-done | bytes 2113552 | tf_op jit(solution)/shard_map/reduce_scatter | solution.py:28
  377.6 32.4 %reduce-scatter.9.cloned.1.call-done = f32[2,2,258,128]{3,2,1,0:T(8,128)} async-done(((f32[8,2,258,128]{3,2,1,0:T(8,128)}), f32[2,2,258,128]{3,2,1,0:T(8,128)}) %reduce-scatter.9.cloned.1.call-update) | async-done | bytes 528400 | tf_op jit(solution)/shard_map/reduce_scatter | solution.py:28
  410.1 14.6 %fusion.28 = f32[512,4096]{1,0:T(8,128)} fusion(bf16[512,4096]{0,1:T(8,128)(2,1)} %bitcast.89, bf16[4096,512]{1,0:T(8,128)(2,1)} %all-gather.15.cloned.1.call-done, bf16[512,4096]{1,0:T(8,128)(2,1)} %param.9, f32[4096]{0:T(1024)S(1)} %bitcast.107, f32[512]{0:T(512)S(1)} %add_rsqrt_fusion, f32[512]{0:T(512)S(1)} %broadcast_multiply_fusion.1), kind=kOutput, calls=%fused_computation.42 | convolution fusion | flops 4322492416 | bytes 20992000 | tf_op jit(solution)/shard_map/dot_general | solution.py:214
  424.7 6.1 %reduce-scatter.11.cloned.1.call-done = f32[1,2,258,128]{3,2,1,0:T(8,128)} async-done(((f32[2,2,258,128]{3,2,1,0:T(8,128)}), f32[1,2,258,128]{3,2,1,0:T(8,128)}) %reduce-scatter.11.cloned.1.call-update) | async-done | bytes 264208 | tf_op jit(solution)/shard_map/reduce_scatter | solution.py:28
  431.5 1.3 fusion.17
  432.9 7.9 %convolution_add_fusion = f32[512,4096]{1,0:T(8,128)} fusion(f32[512,4096]{1,0:T(8,128)} %fusion.28, bf16[512,128]{1,0:T(8,128)(2,1)S(1)} %bitcast.104, bf16[128,4096]{0,1:T(8,128)(2,1)S(1)} %bitcast.87), kind=kOutput, calls=%fused_computation.6 | convolution fusion | flops 538968064 | bytes 17956864 | tf_op jit(solution)/shard_map/dot_general | solution.py:214
  440.9 80.1 %reduce-scatter.13.cloned.1.call-done = f32[512,1024]{1,0:T(8,128)} async-done(((f32[512,4096]{1,0:T(8,128)}), f32[512,1024]{1,0:T(8,128)}) %reduce-scatter.13.cloned.1.call-update) | async-done | bytes 2097168 | tf_op jit(solution)/shard_map/reduce_scatter | solution.py:28
  521.0 32.0 %reduce-scatter.15.cloned.1.call-done = f32[512,256]{1,0:T(8,128)} async-done(((f32[512,1024]{1,0:T(8,128)}), f32[512,256]{1,0:T(8,128)}) %reduce-scatter.15.cloned.1.call-update) | async-done | bytes 524304 | tf_op jit(solution)/shard_map/reduce_scatter | solution.py:28
  553.0 6.5 %convert_element_type.63 = f32[512,4096]{1,0:T(8,128)} convert(bf16[512,4096]{1,0:T(8,128)(2,1)} %param.9) | non-fusion elementwise | flops 2097152 | bytes 12582912 | tf_op jit(solution)/shard_map/convert_element_type | solution.py:138
  559.5 13.9 %reduce-scatter.17.cloned.1.call-done = f32[512,128]{1,0:T(8,128)} async-done(((f32[512,256]{1,0:T(8,128)}), f32[512,128]{1,0:T(8,128)}) %reduce-scatter.17.cloned.1.call-update) | async-done | bytes 262160 | tf_op jit(solution)/shard_map/reduce_scatter | solution.py:28
  573.5 1.8 dynamic-slice_add_fusion
  (80 shorter events, 10.0 us)
Async XLA Ops:
  6.5 9.4 %copy-start.2 = (f32[2,4096]{1,0:T(2,128)S(1)}, f32[2,4096]{1,0:T(2,128)}, u32[]{:S(2)}) copy-start(f32[2,4096]{1,0:T(2,128)} %param.10) | copy-start | bytes 98308
  6.5 42.2 %all-gather.9.cloned.1.call-start = ((), (), s32[]{:S(2)}) async-start(), calls=%async_computation.6 | async-start | bytes 3932160 | tf_op jit(solution)/shard_map/all_gather | solution.py:141
  8.9 88.2 %all-gather.11.cloned.1.call-start = ((), (), s32[]{:S(2)}) async-start(), calls=%async_computation.7 | async-start | bytes 1572864 | tf_op jit(solution)/shard_map/all_gather | solution.py:34
  48.8 97.9 %copy-start.1 = (bf16[128,1024]{1,0:T(8,128)(2,1)S(1)}, bf16[128,1024]{1,0:T(8,128)(2,1)}, u32[]{:S(2)}) copy-start(bf16[128,1024]{1,0:T(8,128)(2,1)} %param.12) | copy-start | bytes 786436
  48.8 98.8 %copy-start = (bf16[512,1024]{1,0:T(8,128)(2,1)S(1)}, bf16[512,1024]{1,0:T(8,128)(2,1)}, u32[]{:S(2)}) copy-start(bf16[512,1024]{1,0:T(8,128)(2,1)} %param.14) | copy-start | bytes 3145732
  54.8 94.8 %copy-start.4 = (s32[2,128]{1,0:T(2,128)S(1)}, s32[2,128]{1,0:T(2,128)}, u32[]{:S(2)}) copy-start(s32[2,128]{1,0:T(2,128)} %param.17) | copy-start | bytes 3076
  54.8 95.3 %copy-start.3 = (s32[2]{0:T(128)S(1)}, s32[2]{0:T(128)}, u32[]{:S(2)}) copy-start(s32[2]{0:T(128)} %param.16) | copy-start | bytes 28
  71.4 75.2 %all-gather.13.cloned.1.call-start = ((), (), s32[]{:S(2)}) async-start(), calls=%async_computation.8 | async-start | bytes 5242880 | tf_op jit(solution)/shard_map/all_gather | solution.py:34
  97.1 192.8 %all-gather.17.cloned.1.call-start = ((), (), s32[]{:S(2)}) async-start(), calls=%async_computation.10 | async-start | bytes 1310720 | tf_op jit(solution)/shard_map/all_gather | solution.py:170
  147.5 143.7 %all-gather.19.cloned.1.call-start = ((), (), s32[]{:S(2)}) async-start(), calls=%async_computation.11 | async-start | bytes 5242880 | tf_op jit(solution)/shard_map/all_gather | solution.py:171
  148.9 146.9 %all-gather.15.cloned.1.call-start = ((), (), s32[]{:S(2)}) async-start(), calls=%async_computation.9 | async-start | bytes 5242880 | tf_op jit(solution)/shard_map/all_gather | solution.py:169
  149.5 227.9 %reduce-scatter.7.cloned.1.call-start = ((), (), s32[]{:S(2)}) async-start(), calls=%async_computation.12 | async-start | bytes 10813440 | tf_op jit(solution)/shard_map/reduce_scatter | solution.py:28
  295.8 114.2 %reduce-scatter.9.cloned.1.call-start = ((), (), s32[]{:S(2)}) async-start(), calls=%async_computation.13 | async-start | bytes 2703360 | tf_op jit(solution)/shard_map/reduce_scatter | solution.py:28
  377.4 53.4 %reduce-scatter.11.cloned.1.call-start = ((), (), s32[]{:S(2)}) async-start(), calls=%async_computation.14 | async-start | bytes 811008 | tf_op jit(solution)/shard_map/reduce_scatter | solution.py:28
  410.0 110.9 %reduce-scatter.13.cloned.1.call-start = ((), (), s32[]{:S(2)}) async-start(), calls=%async_computation.15 | async-start | bytes 10485760 | tf_op jit(solution)/shard_map/reduce_scatter | solution.py:28
  440.8 112.2 %reduce-scatter.15.cloned.1.call-start = ((), (), s32[]{:S(2)}) async-start(), calls=%async_computation.16 | async-start | bytes 2621440 | tf_op jit(solution)/shard_map/reduce_scatter | solution.py:28
  521.0 52.5 %reduce-scatter.17.cloned.1.call-start = ((), (), s32[]{:S(2)}) async-start(), calls=%async_computation.17 | async-start | bytes 786432 | tf_op jit(solution)/shard_map/reduce_scatter | solution.py:28
Sparse Core Ops, SparseCore 0:
  9.0 39.7 all-gather.8
  71.6 25.5 all-gather.10
  98.8 47.8 all-gather.12
  148.2 20.3 all-gather.16
  170.1 47.1 all-gather.18
  218.8 48.7 all-gather.14
  295.9 81.3 reduce-scatter.6
  379.8 30.1 reduce-scatter.8
  412.4 18.3 reduce-scatter.10
  440.9 79.9 reduce-scatter.12
  523.4 29.6 reduce-scatter.14
  555.2 18.1 reduce-scatter.16

commit v5 on v4

--- a/solution.py
+++ b/solution.py
@@ -68,15 +68,17 @@
     k = k_ref[...].reshape(slots * PAGE, HD)
     v = v_ref[...].reshape(slots * PAGE, HD)
     scores = (
-        lax.dot_general(q, k, (((1,), (1,)), ((), ())), preferred_element_type=jnp.float32)
+        lax.dot_general(k, q, (((1,), (1,)), ((), ())), preferred_element_type=jnp.float32)
         * scale
     )
     live = live_ref[...] > 0
-    top = jnp.max(jnp.where(live, scores, -1e30), axis=1, keepdims=True)
+    top = jnp.max(jnp.where(live, scores, -1e30), axis=0, keepdims=True)
     weights = jnp.where(live, jnp.exp(scores - top), 0.0).astype(jnp.bfloat16)
-    tot_ref[...] = jnp.sum(weights.astype(jnp.float32), axis=1, keepdims=True)
+    tot_ref[...] = jnp.sum(weights.astype(jnp.float32), axis=0, keepdims=True)
     top_ref[...] = top
-    acc_ref[...] = jnp.dot(weights, v, preferred_element_type=jnp.float32)
+    acc_ref[...] = lax.dot_general(
+        weights, v, (((0,), (0,)), ((), ())), preferred_element_type=jnp.float32
+    )
 
 
 def attend_pages(q_all, local_cache, live, split):
@@ -86,6 +88,7 @@
     page_spec = lambda kv: pl.BlockSpec(
         (slots, None, None, PAGE, HD), lambda g, h: (0, kv, h, 0, 0)
     )
+    row_spec = pl.BlockSpec((None, None, 1, span), lambda g, h: (head_slot(h, *split), g, 0, 0))
     return pl.pallas_call(
         attend_kernel,
         grid=(groups, heads),
@@ -93,17 +96,17 @@
             pl.BlockSpec((span, HD), lambda g, h: (g, h)),
             page_spec(0),
             page_spec(1),
-            pl.BlockSpec((None, 1, slots * PAGE), lambda g, h: (g, 0, 0)),
+            pl.BlockSpec((None, slots * PAGE, 1), lambda g, h: (g, 0, 0)),
         ],
         out_specs=[
             pl.BlockSpec((None, None, span, HD), lambda g, h: (head_slot(h, *split), g, 0, 0)),
-            pl.BlockSpec((None, None, span, 1), lambda g, h: (head_slot(h, *split), g, 0, 0)),
-            pl.BlockSpec((None, None, span, 1), lambda g, h: (head_slot(h, *split), g, 0, 0)),
+            row_spec,
+            row_spec,
         ],
         out_shape=[
             jax.ShapeDtypeStruct((heads, groups, span, HD), jnp.float32),
-            jax.ShapeDtypeStruct((heads, groups, span, 1), jnp.float32),
-            jax.ShapeDtypeStruct((heads, groups, span, 1), jnp.float32),
+            jax.ShapeDtypeStruct((heads, groups, 1, span), jnp.float32),
+            jax.ShapeDtypeStruct((heads, groups, 1, span), jnp.float32),
         ],
         cost_estimate=pl.CostEstimate(
             flops=4 * groups * heads * span * slots * PAGE * HD,
@@ -138,18 +141,20 @@
     x = hidden_in.astype(jnp.float32)
     h1 = layer_norm(x, ln_gains[0]).astype(jnp.bfloat16)
     h2 = layer_norm(x, ln_gains[1]).astype(jnp.bfloat16)
-    qkv_piece = lax.all_gather(qkv_weight, "req", axis=0, tiled=True)
-    count = qkv_piece.shape[0]
-    qkv_acc = jnp.dot(
-        h1, qkv_piece.reshape(count, 3 * width_loc), preferred_element_type=jnp.float32
-    )
-    qkv = qkv_acc
-    qkv = qkv.reshape(rows, 3, heads_loc, HD)
+    q_piece = lax.all_gather(qkv_weight[:, 0], "req", axis=0, tiled=True)
+    q_acc = jnp.dot(h1, q_piece, preferred_element_type=jnp.float32)
     offsets = jnp.arange(span_rows, dtype=jnp.int32)
     pos = (cached_len[:, None] + offsets[None, :]).reshape(rows).astype(jnp.float32)
-    query = rotate(qkv[:, 0], pos).astype(jnp.bfloat16)
-    key_new = rotate(qkv[:, 1], pos).astype(jnp.bfloat16)
-    value_new = qkv[:, 2].astype(jnp.bfloat16)
+    query = rotate(q_acc.reshape(rows, heads_loc, HD), pos).astype(jnp.bfloat16)
+    q_all = gather_staged(query.reshape(rows, width_loc), 1)
+    kv_weight, q_all = lax.optimization_barrier((qkv_weight[:, 1:], q_all))
+    kv_piece = lax.all_gather(kv_weight, "req", axis=0, tiled=True)
+    count = kv_piece.shape[0]
+    kv_acc = jnp.dot(
+        h1, kv_piece.reshape(count, 2 * width_loc), preferred_element_type=jnp.float32
+    ).reshape(rows, 2, heads_loc, HD)
+    key_new = rotate(kv_acc[:, 0], pos).astype(jnp.bfloat16)
+    value_new = kv_acc[:, 1].astype(jnp.bfloat16)
     q_grp = query.reshape(groups_here, span_rows, heads_loc, HD)
     k_grp = key_new.reshape(groups_here, span_rows, heads_loc, HD)
     v_grp = value_new.reshape(groups_here, span_rows, heads_loc, HD)
@@ -162,9 +167,8 @@
     )
     total_new = jnp.sum(p_new.astype(jnp.float32), axis=-1)
     accum_new = jnp.einsum("ghqk,gkhd->ghqd", p_new, v_grp, preferred_element_type=jnp.float32)
-    q_all = gather_staged(query.reshape(rows, width_loc), 1)
-    up_weight, dense_weight, down_weight, q_all = lax.optimization_barrier(
-        (up_weight, dense_weight, down_weight, q_all)
+    up_weight, dense_weight, down_weight, kv_piece = lax.optimization_barrier(
+        (up_weight, dense_weight, down_weight, kv_piece)
     )
     up_piece = lax.all_gather(up_weight, "req", axis=0, tiled=True)
     dense_piece = by_slot(lax.all_gather(dense_weight, "req", axis=1, tiled=True), split)
@@ -184,7 +188,7 @@
     live = (owner_req[None, :, None] == reqs[:, None, None]) & (
         owner_page[None, :, None] * PAGE + page_pos[None, None, :] < cached_len[:, None, None]
     )
-    live = live.astype(jnp.int32).reshape(groups_here, 1, slots_here * PAGE)
+    live = live.astype(jnp.int32).reshape(groups_here, slots_here * PAGE, 1)
     accums, tops, totals = attend_pages(q_all, local_cache, live, split)
     tops = tops.reshape(HEADS, groups_here, span_rows)
     totals = totals.reshape(HEADS, groups_here, span_rows)
@@ -200,7 +204,13 @@
     packed, up_piece, dense_piece, down_piece = lax.optimization_barrier(
         (packed, up_piece, dense_piece, down_piece)
     )
-    summed = scatter_staged(packed, 0)
+    summed = lax.psum_scatter(packed, "y", scatter_dimension=0, tiled=True)
+    up_acc = jnp.dot(h2, up_piece, preferred_element_type=jnp.float32)
+    hidden = jax.nn.gelu(up_acc, approximate=False).astype(jnp.bfloat16)
+    mlp = jnp.dot(hidden, down_piece, preferred_element_type=jnp.float32)
+    summed, mlp = lax.optimization_barrier((summed, mlp))
+    for name in ("z", "xh"):
+        summed = lax.psum_scatter(summed, name, scatter_dimension=0, tiled=True)
     sum_acc = summed[:, :, :span_rows]
     sum_tot = summed[:, :, span_rows:].reshape(heads_loc, groups_here, span_rows)
     own_largest = lax.dynamic_slice_in_dim(largest, slot_me, heads_loc, 0)
@@ -209,11 +219,7 @@
     denom = sum_tot + total_new * fresh
     att = (numer / denom[..., None]).astype(jnp.bfloat16)
     att = jnp.transpose(att, (1, 2, 0, 3)).reshape(rows, width_loc)
-    up_acc = jnp.dot(h2, up_piece, preferred_element_type=jnp.float32)
-    hidden = jax.nn.gelu(up_acc, approximate=False).astype(jnp.bfloat16)
-    value = jnp.dot(att, dense_piece, preferred_element_type=jnp.float32) + jnp.dot(
-        hidden, down_piece, preferred_element_type=jnp.float32
-    )
+    value = jnp.dot(att, dense_piece, preferred_element_type=jnp.float32) + mlp
     summed = scatter_staged(value, 1)
     width_out = D // n_kv
     residual = lax.dynamic_slice_in_dim(x, me_kv * width_out, width_out, 1)

time: 585 us -> 585 us (level)
  local copies, waits for them, and re-layouts: 28.4 us -> 15.1 us
  Pallas kernels: 63.5 us -> 76 us
  other arithmetic: 42.6 us -> 33 us
  waiting for transfers between devices: 355 us -> 364 us
    reduce_scatter x0 -> x3, waiting for transfers between devices: none -> 121 us  [the longest x1 67.8 us: per_device(): summed = lax.psum_scatter(packed, 'y', scatter_dimension=0, tiled=True)]
    reduce_scatter x6 -> x3, waiting for transfers between devices: 246 us -> 126 us  [scatter_staged(): x = lax.psum_scatter(x, name, scatter_dimension=dim, tiled=True)]
    pallas_call x1, Pallas kernels: 63.5 us -> 76 us  [attend_pages(): pl.pallas_call(attend_kernel, grid=(groups, heads), in_specs=[pl.BlockSpe...]
    exp x1, other arithmetic: 9.72 us -> 0.06 us  [per_device(): factor = jnp.exp(tops - largest)]
    all_gather x1 -> x2, waiting for transfers between devices: 32.8 us -> 41.9 us  [the longest x1 30.4 us: per_device(): kv_piece = lax.all_gather(kv_weight, 'req', axis=0, tiled=True)]
    dot_general x3 -> x4, matrix products: 28.5 us -> 31 us  [the longest x1 14.6 us: per_device(): mlp = jnp.dot(hidden, down_piece, preferred_element_type=jnp.float32)]
  transfers between devices with their start and end apart: 12 -> 13, of which waited for: 9 -> 10; matrix products, arithmetic and copies ran while one was open for 14% -> 11% of each run, Pallas kernels for 11% -> 13%
where the time goes in v5:
time: 585 us; the launch traced here: 584 us
  waiting for transfers between devices  364 us (62%)
  Pallas kernels  76 us (13%)
  blocking collectives  48.4 us (8%)
  other arithmetic  33 us (6%)
  matrix products  32.8 us (6%)
  local copies, waits for them, and re-layouts  15.1 us (3%)
  between operations  13.6 us (2%)
    reduce_scatter x3, waiting for transfers between devices, scatter_staged(): x = lax.psum_scatter(x, name, scatter_dimension=dim, tiled=True)  126 us
    pallas_call x1, Pallas kernels, attend_pages(): pl.pallas_call(attend_kernel, grid=(groups, heads), in_specs=[pl.BlockSpe...  76 us
    all_gather x2, waiting for transfers between devices, gather_staged(): x = lax.all_gather(x, name, axis=dim, tiled=True)  74.3 us
    reduce_scatter x1, waiting for transfers between devices, per_device(): summed = lax.psum_scatter(packed, 'y', scatter_dimension=0, tiled=True)  67.8 us
    reduce_scatter x2, waiting for transfers between devices, per_device(): summed = lax.psum_scatter(summed, name, scatter_dimension=0, tiled=True)  53 us
    all_gather x3, blocking collectives, max_staged(): x = jnp.max(lax.all_gather(x, name, axis=0, tiled=False), axis=0)  33.3 us
    all_gather x1, waiting for transfers between devices, per_device(): kv_piece = lax.all_gather(kv_weight, 'req', axis=0, tiled=True)  30.4 us
    all_gather x1, blocking collectives, gather_staged(): x = lax.all_gather(x, name, axis=dim, tiled=True)  15 us
  transfers between devices with their start and end apart: 13, of which 10 were waited for; matrix products, arithmetic and copies ran while one was open for 11% of the time, Pallas kernels for 13%

profile of v5, /device:TPU:0, one launch (start us, length us, event | category | flops | bytes accessed | tf_op | source)
XLA Modules:
  0.0 583.6 jit_solution(4596234834259337808)
XLA Ops:
  6.5 1.7 slice.46
  9.3 3.1 convert_reduce_fusion
  12.3 3.4 multiply_reduce_fusion
  15.9 4.3 multiply_convert_fusion.1
  20.2 11.5 %all-gather.23.cloned.1.call-done = bf16[4096,1,128]{2,0,1:T(8,128)(2,1)} async-done(((bf16[1024,1,128]{2,0,1:T(8,128)(2,1)}), bf16[4096,1,128]{2,0,1:T(8,128)(2,1)}) %all-gather.23.cloned.1.call-update) | async-done | bytes 1048592 | tf_op jit(solution)/shard_map/all_gather | solution.py:144
  31.7 3.7 convolution_bitcast_fusion
  36.9 15.0 %all_gather.43 = bf16[512,512]{1,0:T(8,128)(2,1)} all-gather(bf16[512,128]{1,0:T(8,128)(2,1)S(1)} %pad_maximum_fusion.1), channel_id=1, replica_groups=mesh['req'=4,'z'=4,'xh'=2,'y'=4] {'y'}, dimensions={1}, use_global_device_ids=true | all-gather | bytes 655360 | tf_op jit(solution)/shard_map/all_gather | solution.py:34
  52.0 25.8 %all-gather.11.cloned.1.call-done = bf16[512,1024]{1,0:T(8,128)(2,1)} async-done(((bf16[512,512]{1,0:T(8,128)(2,1)}), bf16[512,1024]{1,0:T(8,128)(2,1)}) %all-gather.11.cloned.1.call-update) | async-done | bytes 1048592 | tf_op jit(solution)/shard_map/all_gather | solution.py:34
  79.0 48.4 %all-gather.13.cloned.1.call-done.q_ref = bf16[512,4096]{1,0:T(8,128)(2,1)} async-done(((bf16[512,1024]{1,0:T(8,128)(2,1)}), bf16[512,4096]{1,0:T(8,128)(2,1)}) %all-gather.13.cloned.1.call-update) | async-done | bytes 4194320 | tf_op jit(solution)/shard_map/all_gather | solution.py:34
  127.5 30.4 %all-gather.15.cloned.1.call-done = bf16[4096,2,128]{0,2,1:T(8,128)(2,1)} async-done(((bf16[1024,2,128]{0,2,1:T(8,128)(2,1)}), bf16[4096,2,128]{0,2,1:T(8,128)(2,1)}) %all-gather.15.cloned.1.call-update) | async-done | bytes 2097168 | tf_op jit(solution)/shard_map/all_gather | solution.py:151
  158.8 1.3 copy.68
  162.7 1.2 and_convert_fusion.live_ref
  164.0 76.0 %shard_map.91 = (f32[32,2,256,128]{3,2,1,0:T(8,128)}, f32[32,2,1,256]{3,2,1,0:T(1,128)}, f32[32,2,1,256]{3,2,1,0:T(1,128)}) custom-call(bf16[512,4096]{1,0:T(8,128)(2,1)} %all-gather.13.cloned.1.call-done.q_ref, bf16[8,2,32,128,128]{4,3,2,1,0:T(8,128)(2,1)} %bitcast.97, bf16[8,2,32,128,128]{4,3,2,1,0:T(8,128)(2,1)} %bitcast.98, ...), custom_call_target="tpu_custom_call" | custom-call | flops 8589934592 | bytes 46137344 | tf_op jit(solution)/shard_map/pallas_call | solution.py:92
  241.0 4.7 fusion.7
  247.6 12.6 %all_gather.48 = f32[4,32,2,256]{3,1,2,0:T(8,128)S(1)} all-gather(f32[1,32,2,256]{3,1,2,0:T(8,128)S(1)} %copy.64), channel_id=1, replica_groups=mesh['req'=4,'z'=4,'xh'=2,'y'=4] {'y'}, dimensions={0}, use_global_device_ids=true | all-gather | bytes 327680 | tf_op jit(solution)/shard_map/all_gather | solution.py:40
  260.3 8.0 %all-gather.1 = f32[64,2,256]{2,1,0:T(2,128)S(1)} all-gather(f32[32,2,256]{2,1,0:T(2,128)S(1)} %copy.65), channel_id=3, replica_groups=mesh['req'=4,'z'=4,'xh'=2,'y'=4] {'xh'}, dimensions={0}, use_global_device_ids=true | all-gather | bytes 196608 | tf_op jit(solution)/shard_map/all_gather | solution.py:40
  268.3 12.7 %all-gather.2 = f32[128,2,256]{2,1,0:T(2,128)S(1)} all-gather(f32[32,2,256]{2,1,0:T(2,128)S(1)} %reduce_max.43), channel_id=4, replica_groups=mesh['req'=4,'z'=4,'xh'=2,'y'=4] {'z'}, dimensions={0}, use_global_device_ids=true | all-gather | bytes 327680 | tf_op jit(solution)/shard_map/all_gather | solution.py:40
  281.4 5.2 broadcast_multiply_fusion
  286.6 4.0 pad_maximum_fusion
  290.7 1.3 copy.67
  292.0 4.6 copy.69
  296.9 14.6 %fusion.28 = f32[512,4096]{1,0:T(8,128)} fusion(bf16[512,4096]{0,1:T(8,128)(2,1)} %bitcast.101, bf16[4096,512]{1,0:T(8,128)(2,1)} %all-gather.17.cloned.1.call-done, bf16[512,4096]{1,0:T(8,128)(2,1)} %param.9, f32[4096]{0:T(1024)S(1)} %bitcast.122, f32[512]{0:T(512)S(1)} %add_rsqrt_fusion, f32[512]{0:T(512)S(1)} %broadcast_multiply_fusion.1), kind=kOutput, calls=%fused_computation.43 | convolution fusion | flops 4322492416 | bytes 20992000 | tf_op jit(solution)/shard_map/dot_general | solution.py:210
  311.5 67.8 %reduce-scatter.7.cloned.1.call-done = f32[8,2,258,128]{3,2,1,0:T(8,128)} async-done(((f32[32,2,258,128]{3,2,1,0:T(8,128)}), f32[8,2,258,128]{3,2,1,0:T(8,128)}) %reduce-scatter.7.cloned.1.call-update) | async-done | bytes 2113552 | tf_op jit(solution)/shard_map/reduce_scatter | solution.py:207
  379.4 32.6 %reduce-scatter.9.cloned.1.call-done = f32[2,2,258,128]{3,2,1,0:T(8,128)} async-done(((f32[8,2,258,128]{3,2,1,0:T(8,128)}), f32[2,2,258,128]{3,2,1,0:T(8,128)}) %reduce-scatter.9.cloned.1.call-update) | async-done | bytes 528400 | tf_op jit(solution)/shard_map/reduce_scatter | solution.py:213
  412.2 20.4 %reduce-scatter.11.cloned.1.call-done = f32[1,2,258,128]{3,2,1,0:T(8,128)} async-done(((f32[2,2,258,128]{3,2,1,0:T(8,128)}), f32[1,2,258,128]{3,2,1,0:T(8,128)}) %reduce-scatter.11.cloned.1.call-update) | async-done | bytes 264208 | tf_op jit(solution)/shard_map/reduce_scatter | solution.py:213
  433.4 1.3 fusion.16
  434.7 7.9 %convolution_add_fusion = f32[512,4096]{1,0:T(8,128)} fusion(f32[512,4096]{1,0:T(8,128)} %fusion.28, bf16[512,128]{1,0:T(8,128)(2,1)S(1)} %bitcast.115, bf16[128,4096]{0,1:T(8,128)(2,1)S(1)} %bitcast.99), kind=kOutput, calls=%fused_computation.5 | convolution fusion | flops 538968064 | bytes 17956864 | tf_op jit(solution)/shard_map/dot_general | solution.py:222
  442.7 80.1 %reduce-scatter.13.cloned.1.call-done = f32[512,1024]{1,0:T(8,128)} async-done(((f32[512,4096]{1,0:T(8,128)}), f32[512,1024]{1,0:T(8,128)}) %reduce-scatter.13.cloned.1.call-update) | async-done | bytes 2097168 | tf_op jit(solution)/shard_map/reduce_scatter | solution.py:28
  522.9 31.9 %reduce-scatter.15.cloned.1.call-done = f32[512,256]{1,0:T(8,128)} async-done(((f32[512,1024]{1,0:T(8,128)}), f32[512,256]{1,0:T(8,128)}) %reduce-scatter.15.cloned.1.call-update) | async-done | bytes 524304 | tf_op jit(solution)/shard_map/reduce_scatter | solution.py:28
  554.8 6.6 %convert_element_type.63 = f32[512,4096]{1,0:T(8,128)} convert(bf16[512,4096]{1,0:T(8,128)(2,1)} %param.9) | non-fusion elementwise | flops 2097152 | bytes 12582912 | tf_op jit(solution)/shard_map/convert_element_type | solution.py:141
  561.3 14.0 %reduce-scatter.17.cloned.1.call-done = f32[512,128]{1,0:T(8,128)} async-done(((f32[512,256]{1,0:T(8,128)}), f32[512,128]{1,0:T(8,128)}) %reduce-scatter.17.cloned.1.call-update) | async-done | bytes 262160 | tf_op jit(solution)/shard_map/reduce_scatter | solution.py:28
  575.3 1.8 dynamic-slice_add_fusion
  (85 shorter events, 11.8 us)
Async XLA Ops:
  6.5 9.2 %copy-start.5 = (s32[2]{0:T(128)S(1)}, s32[2]{0:T(128)}, u32[]{:S(2)}) copy-start(s32[2]{0:T(128)} %param.16) | copy-start | bytes 28
  6.5 25.2 %all-gather.23.cloned.1.call-start = ((), (), s32[]{:S(2)}) async-start(), calls=%async_computation.18 | async-start | bytes 1310720 | tf_op jit(solution)/shard_map/all_gather | solution.py:144
  8.2 69.6 %all-gather.11.cloned.1.call-start = ((), (), s32[]{:S(2)}) async-start(), calls=%async_computation.6 | async-start | bytes 1572864 | tf_op jit(solution)/shard_map/all_gather | solution.py:34
  8.3 7.6 %copy-start = (bf16[512,4096]{1,0:T(8,128)(2,1)S(1)}, bf16[512,4096]{1,0:T(8,128)(2,1)}, u32[]{:S(2)}) copy-start(bf16[512,4096]{1,0:T(8,128)(2,1)} %param.9) | copy-start | bytes 12582916
  15.9 62.1 %slice-start = ((bf16[1024,3,128]{2,0,1:T(8,128)(2,1)}), bf16[1024,2,128]{2,0,1:T(8,128)(2,1)S(1)}, s32[]{:S(2)}) async-start(bf16[1024,3,128]{2,0,1:T(8,128)(2,1)} %param.11), calls=%async_computation.19 | async-start | bytes 1048576 | tf_op jit(solution)/shard_map/slice | solution.py:150
  15.9 142.0 %copy-start.3 = (bf16[128,1024]{1,0:T(8,128)(2,1)S(1)}, bf16[128,1024]{1,0:T(8,128)(2,1)}, u32[]{:S(2)}) copy-start(bf16[128,1024]{1,0:T(8,128)(2,1)} %param.12) | copy-start | bytes 786436
  20.2 138.6 %copy-start.1 = (bf16[512,1024]{1,0:T(8,128)(2,1)S(1)}, bf16[512,1024]{1,0:T(8,128)(2,1)}, u32[]{:S(2)}) copy-start(bf16[512,1024]{1,0:T(8,128)(2,1)} %param.14) | copy-start | bytes 3145732
  20.2 141.0 %copy-start.6 = (s32[2,128]{1,0:T(2,128)S(1)}, s32[2,128]{1,0:T(2,128)}, u32[]{:S(2)}) copy-start(s32[2,128]{1,0:T(2,128)} %param.17) | copy-start | bytes 3076
  52.0 75.5 %all-gather.13.cloned.1.call-start = ((), (), s32[]{:S(2)}) async-start(), calls=%async_computation.7 | async-start | bytes 5242880 | tf_op jit(solution)/shard_map/all_gather | solution.py:34
  77.9 80.0 %all-gather.15.cloned.1.call-start = ((), (), s32[]{:S(2)}) async-start(), calls=%async_computation.8 | async-start | bytes 2621440 | tf_op jit(solution)/shard_map/all_gather | solution.py:151
  127.5 163.2 %all-gather.19.cloned.1.call-start = ((), (), s32[]{:S(2)}) async-start(), calls=%async_computation.10 | async-start | bytes 1310720 | tf_op jit(solution)/shard_map/all_gather | solution.py:174
  158.8 133.2 %all-gather.21.cloned.1.call-start = ((), (), s32[]{:S(2)}) async-start(), calls=%async_computation.11 | async-start | bytes 5242880 | tf_op jit(solution)/shard_map/all_gather | solution.py:175
  160.2 136.4 %all-gather.17.cloned.1.call-start = ((), (), s32[]{:S(2)}) async-start(), calls=%async_computation.9 | async-start | bytes 5242880 | tf_op jit(solution)/shard_map/all_gather | solution.py:173
  160.9 218.4 %reduce-scatter.7.cloned.1.call-start = ((), (), s32[]{:S(2)}) async-start(), calls=%async_computation.12 | async-start | bytes 10813440 | tf_op jit(solution)/shard_map/reduce_scatter | solution.py:207
  240.1 7.4 %copy-start.2 = (f32[32,2,1,256]{3,2,1,0:T(1,128)S(1)}, f32[32,2,1,256]{3,2,1,0:T(1,128)}, u32[]{:S(2)}) copy-start(f32[32,2,1,256]{3,2,1,0:T(1,128)} %get-tuple-element.21) | copy-start | bytes 196612
  240.1 41.2 %copy-start.4 = (f32[32,2,1,256]{3,2,1,0:T(1,128)S(1)}, f32[32,2,1,256]{3,2,1,0:T(1,128)}, u32[]{:S(2)}) copy-start(f32[32,2,1,256]{3,2,1,0:T(1,128)} %get-tuple-element.23) | copy-start | bytes 196612
  296.6 115.4 %reduce-scatter.9.cloned.1.call-start = ((), (), s32[]{:S(2)}) async-start(), calls=%async_computation.13 | async-start | bytes 2703360 | tf_op jit(solution)/shard_map/reduce_scatter | solution.py:213
  379.4 53.3 %reduce-scatter.11.cloned.1.call-start = ((), (), s32[]{:S(2)}) async-start(), calls=%async_computation.14 | async-start | bytes 811008 | tf_op jit(solution)/shard_map/reduce_scatter | solution.py:213
  412.0 110.8 %reduce-scatter.13.cloned.1.call-start = ((), (), s32[]{:S(2)}) async-start(), calls=%async_computation.15 | async-start | bytes 10485760 | tf_op jit(solution)/shard_map/reduce_scatter | solution.py:28
  442.7 112.1 %reduce-scatter.15.cloned.1.call-start = ((), (), s32[]{:S(2)}) async-start(), calls=%async_computation.16 | async-start | bytes 2621440 | tf_op jit(solution)/shard_map/reduce_scatter | solution.py:28
  522.8 52.5 %reduce-scatter.17.cloned.1.call-start = ((), (), s32[]{:S(2)}) async-start(), calls=%async_computation.17 | async-start | bytes 786432 | tf_op jit(solution)/shard_map/reduce_scatter | solution.py:28
Sparse Core Ops, SparseCore 0:
  9.0 22.6 all-gather.22
  52.1 25.7 all-gather.10
  79.5 47.8 all-gather.12
  129.0 28.8 all-gather.14
  159.4 21.3 all-gather.18
  182.3 47.1 all-gather.20
  231.2 48.7 all-gather.16
  296.8 82.5 reduce-scatter.6
  381.8 30.1 reduce-scatter.8
  414.2 18.3 reduce-scatter.10
  442.8 79.9 reduce-scatter.12
  525.1 29.6 reduce-scatter.14
  557.1 18.1 reduce-scatter.16

commit v6 on v5

--- a/solution.py
+++ b/solution.py
@@ -117,7 +117,7 @@
     )(q_all, local_cache, local_cache, live)
 
 
-def per_device(
+def layer(
     hidden_in,
     ln_gains,
     qkv_weight,
@@ -147,7 +147,9 @@
     pos = (cached_len[:, None] + offsets[None, :]).reshape(rows).astype(jnp.float32)
     query = rotate(q_acc.reshape(rows, heads_loc, HD), pos).astype(jnp.bfloat16)
     q_all = gather_staged(query.reshape(rows, width_loc), 1)
-    kv_weight, q_all = lax.optimization_barrier((qkv_weight[:, 1:], q_all))
+    kv_weight, up_weight, dense_weight, down_weight, q_all = lax.optimization_barrier(
+        (qkv_weight[:, 1:], up_weight, dense_weight, down_weight, q_all)
+    )
     kv_piece = lax.all_gather(kv_weight, "req", axis=0, tiled=True)
     count = kv_piece.shape[0]
     kv_acc = jnp.dot(
@@ -167,12 +169,11 @@
     )
     total_new = jnp.sum(p_new.astype(jnp.float32), axis=-1)
     accum_new = jnp.einsum("ghqk,gkhd->ghqd", p_new, v_grp, preferred_element_type=jnp.float32)
-    up_weight, dense_weight, down_weight, kv_piece = lax.optimization_barrier(
-        (up_weight, dense_weight, down_weight, kv_piece)
-    )
     up_piece = lax.all_gather(up_weight, "req", axis=0, tiled=True)
-    dense_piece = by_slot(lax.all_gather(dense_weight, "req", axis=1, tiled=True), split)
-    down_piece = by_slot(lax.all_gather(down_weight, "req", axis=1, tiled=True), split)
+    dense_piece = lax.all_gather(dense_weight, "req", axis=1, tiled=True)
+    down_piece = lax.all_gather(down_weight, "req", axis=1, tiled=True)
+    dense_piece = by_slot(dense_piece, split)
+    down_piece = by_slot(down_piece, split)
     local_cache = cache[0]
     slots_here = local_cache.shape[0]
     slot_ids = me_kv * slots_here + jnp.arange(slots_here, dtype=jnp.int32)
@@ -242,5 +243,5 @@
         P("req", None),
     )
     return jax.shard_map(
-        per_device, mesh=torus, in_specs=placed, out_specs=P("req", KV), check_vma=False
-    )
+        layer, mesh=torus, in_specs=placed, out_specs=P("req", KV), check_vma=False
+    )

time: 585 us -> 572 us (0.978)
  waiting for transfers between devices: 364 us -> 352 us
    all_gather x5, waiting for transfers between devices: 41.9 us -> 26.2 us  [the longest x1 14.7 us: layer(): up_piece = lax.all_gather(up_weight, 'req', axis=0, tiled=True)]
where the time goes in v6:
time: 572 us; the launch traced here: 570 us
  waiting for transfers between devices  352 us (62%)
  Pallas kernels  76 us (13%)
  blocking collectives  46.6 us (8%)
  other arithmetic  33.1 us (6%)
  matrix products  32.6 us (6%)
  local copies, waits for them, and re-layouts  15.1 us (3%)
  between operations  13.6 us (2%)
    reduce_scatter x3, waiting for transfers between devices, scatter_staged(): x = lax.psum_scatter(x, name, scatter_dimension=dim, tiled=True)  126 us
    pallas_call x1, Pallas kernels, attend_pages(): pl.pallas_call(attend_kernel, grid=(groups, heads), in_specs=[pl.BlockSpe...  76 us
    all_gather x2, waiting for transfers between devices, gather_staged(): x = lax.all_gather(x, name, axis=dim, tiled=True)  74.3 us
    reduce_scatter x1, waiting for transfers between devices, layer(): summed = lax.psum_scatter(packed, 'y', scatter_dimension=0, tiled=True)  71.5 us
    reduce_scatter x2, waiting for transfers between devices, layer(): summed = lax.psum_scatter(summed, name, scatter_dimension=0, tiled=True)  53 us
    all_gather x3, blocking collectives, max_staged(): x = jnp.max(lax.all_gather(x, name, axis=0, tiled=False), axis=0)  31.5 us
    all_gather x1, blocking collectives, gather_staged(): x = lax.all_gather(x, name, axis=dim, tiled=True)  15 us
    dot_general x1, matrix products, layer(): mlp = jnp.dot(hidden, down_piece, preferred_element_type=jnp.float32)  15 us
  transfers between devices with their start and end apart: 13, of which 10 were waited for; matrix products, arithmetic and copies ran while one was open for 11% of the time, Pallas kernels for 13%

profile of v6, /device:TPU:0, one launch (start us, length us, event | category | flops | bytes accessed | tf_op | source)
XLA Modules:
  0.0 570.2 jit_solution(8131457908129677591)
XLA Ops:
  6.5 1.7 slice.46
  9.3 3.1 convert_reduce_fusion
  12.3 3.4 multiply_reduce_fusion
  15.9 4.3 multiply_convert_fusion.1
  20.2 11.5 %all-gather.23.cloned.1.call-done = bf16[4096,1,128]{2,0,1:T(8,128)(2,1)} async-done(((bf16[1024,1,128]{2,0,1:T(8,128)(2,1)}), bf16[4096,1,128]{2,0,1:T(8,128)(2,1)}) %all-gather.23.cloned.1.call-update) | async-done | bytes 1048592 | tf_op jit(solution)/shard_map/all_gather | solution.py:144
  31.7 3.7 convolution_bitcast_fusion
  35.5 1.2 fusion.68
  36.9 15.0 %all_gather.43 = bf16[512,512]{1,0:T(8,128)(2,1)} all-gather(bf16[512,128]{1,0:T(8,128)(2,1)S(1)} %pad_maximum_fusion.1), channel_id=1, replica_groups=mesh['req'=4,'z'=4,'xh'=2,'y'=4] {'y'}, dimensions={1}, use_global_device_ids=true | all-gather | bytes 655360 | tf_op jit(solution)/shard_map/all_gather | solution.py:34
  52.0 25.8 %all-gather.11.cloned.1.call-done = bf16[512,1024]{1,0:T(8,128)(2,1)} async-done(((bf16[512,512]{1,0:T(8,128)(2,1)}), bf16[512,1024]{1,0:T(8,128)(2,1)}) %all-gather.11.cloned.1.call-update) | async-done | bytes 1048592 | tf_op jit(solution)/shard_map/all_gather | solution.py:34
  79.0 48.5 %all-gather.13.cloned.1.call-done.q_ref = bf16[512,4096]{1,0:T(8,128)(2,1)} async-done(((bf16[512,1024]{1,0:T(8,128)(2,1)}), bf16[512,4096]{1,0:T(8,128)(2,1)}) %all-gather.13.cloned.1.call-update) | async-done | bytes 4194320 | tf_op jit(solution)/shard_map/all_gather | solution.py:34
  129.0 1.4 copy.68
  134.2 76.0 %shard_map.91 = (f32[32,2,256,128]{3,2,1,0:T(8,128)}, f32[32,2,1,256]{3,2,1,0:T(1,128)}, f32[32,2,1,256]{3,2,1,0:T(1,128)}) custom-call(bf16[512,4096]{1,0:T(8,128)(2,1)} %all-gather.13.cloned.1.call-done.q_ref, bf16[8,2,32,128,128]{4,3,2,1,0:T(8,128)(2,1)} %bitcast.97, bf16[8,2,32,128,128]{4,3,2,1,0:T(8,128)(2,1)} %bitcast.98, ...), custom_call_target="tpu_custom_call" | custom-call | flops 8589934592 | bytes 46137344 | tf_op jit(solution)/shard_map/pallas_call | solution.py:92
  211.1 1.3 copy.67
  212.4 4.2 fusion.7
  218.5 12.6 %all_gather.48 = f32[4,32,2,256]{3,1,2,0:T(8,128)S(1)} all-gather(f32[1,32,2,256]{3,1,2,0:T(8,128)S(1)} %copy.64), channel_id=1, replica_groups=mesh['req'=4,'z'=4,'xh'=2,'y'=4] {'y'}, dimensions={0}, use_global_device_ids=true | all-gather | bytes 327680 | tf_op jit(solution)/shard_map/all_gather | solution.py:40
  231.2 6.4 %all-gather.1 = f32[64,2,256]{2,1,0:T(2,128)S(1)} all-gather(f32[32,2,256]{2,1,0:T(2,128)S(1)} %copy.65), channel_id=3, replica_groups=mesh['req'=4,'z'=4,'xh'=2,'y'=4] {'xh'}, dimensions={0}, use_global_device_ids=true | all-gather | bytes 196608 | tf_op jit(solution)/shard_map/all_gather | solution.py:40
  237.7 12.5 %all-gather.2 = f32[128,2,256]{2,1,0:T(2,128)S(1)} all-gather(f32[32,2,256]{2,1,0:T(2,128)S(1)} %reduce_max.43), channel_id=4, replica_groups=mesh['req'=4,'z'=4,'xh'=2,'y'=4] {'z'}, dimensions={0}, use_global_device_ids=true | all-gather | bytes 327680 | tf_op jit(solution)/shard_map/all_gather | solution.py:40
  250.6 5.3 broadcast_multiply_fusion
  255.9 4.0 pad_maximum_fusion
  259.9 4.6 copy.69
  264.6 14.7 %all-gather.17.cloned.1.call-done = bf16[4096,512]{1,0:T(8,128)(2,1)} async-done(((bf16[1024,512]{1,0:T(8,128)(2,1)}), bf16[4096,512]{1,0:T(8,128)(2,1)}) %all-gather.17.cloned.1.call-update) | async-done | bytes 4194320 | tf_op jit(solution)/shard_map/all_gather | solution.py:172
  279.6 15.0 %fusion.28 = f32[512,4096]{1,0:T(8,128)} fusion(bf16[512,4096]{0,1:T(8,128)(2,1)} %bitcast.101, bf16[4096,512]{1,0:T(8,128)(2,1)} %all-gather.17.cloned.1.call-done, bf16[512,4096]{1,0:T(8,128)(2,1)} %param.9, f32[4096]{0:T(1024)S(1)} %bitcast.122, f32[512]{0:T(512)S(1)} %add_rsqrt_fusion, f32[512]{0:T(512)S(1)} %broadcast_multiply_fusion.1), kind=kOutput, calls=%fused_computation.43 | convolution fusion | flops 4322492416 | bytes 20992000 | tf_op jit(solution)/shard_map/dot_general | solution.py:211
  294.5 71.5 %reduce-scatter.7.cloned.1.call-done = f32[8,2,258,128]{3,2,1,0:T(8,128)} async-done(((f32[32,2,258,128]{3,2,1,0:T(8,128)}), f32[8,2,258,128]{3,2,1,0:T(8,128)}) %reduce-scatter.7.cloned.1.call-update) | async-done | bytes 2113552 | tf_op jit(solution)/shard_map/reduce_scatter | solution.py:208
  366.1 32.6 %reduce-scatter.9.cloned.1.call-done = f32[2,2,258,128]{3,2,1,0:T(8,128)} async-done(((f32[8,2,258,128]{3,2,1,0:T(8,128)}), f32[2,2,258,128]{3,2,1,0:T(8,128)}) %reduce-scatter.9.cloned.1.call-update) | async-done | bytes 528400 | tf_op jit(solution)/shard_map/reduce_scatter | solution.py:214
  398.9 20.4 %reduce-scatter.11.cloned.1.call-done = f32[1,2,258,128]{3,2,1,0:T(8,128)} async-done(((f32[2,2,258,128]{3,2,1,0:T(8,128)}), f32[1,2,258,128]{3,2,1,0:T(8,128)}) %reduce-scatter.11.cloned.1.call-update) | async-done | bytes 264208 | tf_op jit(solution)/shard_map/reduce_scatter | solution.py:214
  420.0 1.3 fusion.16
  421.3 7.9 %convolution_add_fusion = f32[512,4096]{1,0:T(8,128)} fusion(f32[512,4096]{1,0:T(8,128)} %fusion.28, bf16[512,128]{1,0:T(8,128)(2,1)S(1)} %bitcast.115, bf16[128,4096]{0,1:T(8,128)(2,1)S(1)} %bitcast.99), kind=kOutput, calls=%fused_computation.5 | convolution fusion | flops 538968064 | bytes 17956864 | tf_op jit(solution)/shard_map/dot_general | solution.py:223
  429.3 80.1 %reduce-scatter.13.cloned.1.call-done = f32[512,1024]{1,0:T(8,128)} async-done(((f32[512,4096]{1,0:T(8,128)}), f32[512,1024]{1,0:T(8,128)}) %reduce-scatter.13.cloned.1.call-update) | async-done | bytes 2097168 | tf_op jit(solution)/shard_map/reduce_scatter | solution.py:28
  509.5 31.9 %reduce-scatter.15.cloned.1.call-done = f32[512,256]{1,0:T(8,128)} async-done(((f32[512,1024]{1,0:T(8,128)}), f32[512,256]{1,0:T(8,128)}) %reduce-scatter.15.cloned.1.call-update) | async-done | bytes 524304 | tf_op jit(solution)/shard_map/reduce_scatter | solution.py:28
  541.4 6.6 %convert_element_type.63 = f32[512,4096]{1,0:T(8,128)} convert(bf16[512,4096]{1,0:T(8,128)(2,1)} %param.9) | non-fusion elementwise | flops 2097152 | bytes 12582912 | tf_op jit(solution)/shard_map/convert_element_type | solution.py:141
  547.9 14.0 %reduce-scatter.17.cloned.1.call-done = f32[512,128]{1,0:T(8,128)} async-done(((f32[512,256]{1,0:T(8,128)}), f32[512,128]{1,0:T(8,128)}) %reduce-scatter.17.cloned.1.call-update) | async-done | bytes 262160 | tf_op jit(solution)/shard_map/reduce_scatter | solution.py:28
  562.0 1.8 dynamic-slice_add_fusion
  (85 shorter events, 12.2 us)
Async XLA Ops:
  6.5 9.2 %copy-start.5 = (s32[2]{0:T(128)S(1)}, s32[2]{0:T(128)}, u32[]{:S(2)}) copy-start(s32[2]{0:T(128)} %param.16) | copy-start | bytes 28
  6.5 25.2 %all-gather.23.cloned.1.call-start = ((), (), s32[]{:S(2)}) async-start(), calls=%async_computation.18 | async-start | bytes 1310720 | tf_op jit(solution)/shard_map/all_gather | solution.py:144
  8.2 69.6 %all-gather.11.cloned.1.call-start = ((), (), s32[]{:S(2)}) async-start(), calls=%async_computation.6 | async-start | bytes 1572864 | tf_op jit(solution)/shard_map/all_gather | solution.py:34
  8.3 7.6 %copy-start = (bf16[512,4096]{1,0:T(8,128)(2,1)S(1)}, bf16[512,4096]{1,0:T(8,128)(2,1)}, u32[]{:S(2)}) copy-start(bf16[512,4096]{1,0:T(8,128)(2,1)} %param.9) | copy-start | bytes 12582916
  15.9 62.1 %slice-start = ((bf16[1024,3,128]{2,0,1:T(8,128)(2,1)}), bf16[1024,2,128]{2,0,1:T(8,128)(2,1)S(1)}, s32[]{:S(2)}) async-start(bf16[1024,3,128]{2,0,1:T(8,128)(2,1)} %param.11), calls=%async_computation.19 | async-start | bytes 1048576 | tf_op jit(solution)/shard_map/slice | solution.py:151
  15.9 111.6 %copy-start.3 = (bf16[128,1024]{1,0:T(8,128)(2,1)S(1)}, bf16[128,1024]{1,0:T(8,128)(2,1)}, u32[]{:S(2)}) copy-start(bf16[128,1024]{1,0:T(8,128)(2,1)} %param.12) | copy-start | bytes 786436
  20.2 108.7 %copy-start.1 = (bf16[512,1024]{1,0:T(8,128)(2,1)S(1)}, bf16[512,1024]{1,0:T(8,128)(2,1)}, u32[]{:S(2)}) copy-start(bf16[512,1024]{1,0:T(8,128)(2,1)} %param.14) | copy-start | bytes 3145732
  20.2 111.2 %copy-start.6 = (s32[2,128]{1,0:T(2,128)S(1)}, s32[2,128]{1,0:T(2,128)}, u32[]{:S(2)}) copy-start(s32[2,128]{1,0:T(2,128)} %param.17) | copy-start | bytes 3076
  52.0 75.5 %all-gather.13.cloned.1.call-start = ((), (), s32[]{:S(2)}) async-start(), calls=%async_computation.7 | async-start | bytes 5242880 | tf_op jit(solution)/shard_map/all_gather | solution.py:34
  77.9 133.2 %all-gather.19.cloned.1.call-start = ((), (), s32[]{:S(2)}) async-start(), calls=%async_computation.10 | async-start | bytes 1310720 | tf_op jit(solution)/shard_map/all_gather | solution.py:173
  128.3 84.1 %all-gather.15.cloned.1.call-start = ((), (), s32[]{:S(2)}) async-start(), calls=%async_computation.8 | async-start | bytes 2621440 | tf_op jit(solution)/shard_map/all_gather | solution.py:153
  128.9 131.0 %all-gather.21.cloned.1.call-start = ((), (), s32[]{:S(2)}) async-start(), calls=%async_computation.11 | async-start | bytes 5242880 | tf_op jit(solution)/shard_map/all_gather | solution.py:174
  130.3 148.9 %all-gather.17.cloned.1.call-start = ((), (), s32[]{:S(2)}) async-start(), calls=%async_computation.9 | async-start | bytes 5242880 | tf_op jit(solution)/shard_map/all_gather | solution.py:172
  131.1 234.9 %reduce-scatter.7.cloned.1.call-start = ((), (), s32[]{:S(2)}) async-start(), calls=%async_computation.12 | async-start | bytes 10813440 | tf_op jit(solution)/shard_map/reduce_scatter | solution.py:208
  210.2 8.3 %copy-start.2 = (f32[32,2,1,256]{3,2,1,0:T(1,128)S(1)}, f32[32,2,1,256]{3,2,1,0:T(1,128)}, u32[]{:S(2)}) copy-start(f32[32,2,1,256]{3,2,1,0:T(1,128)} %get-tuple-element.21) | copy-start | bytes 196612
  210.2 40.3 %copy-start.4 = (f32[32,2,1,256]{3,2,1,0:T(1,128)S(1)}, f32[32,2,1,256]{3,2,1,0:T(1,128)}, u32[]{:S(2)}) copy-start(f32[32,2,1,256]{3,2,1,0:T(1,128)} %get-tuple-element.23) | copy-start | bytes 196612
  279.3 119.3 %reduce-scatter.9.cloned.1.call-start = ((), (), s32[]{:S(2)}) async-start(), calls=%async_computation.13 | async-start | bytes 2703360 | tf_op jit(solution)/shard_map/reduce_scatter | solution.py:214
  366.0 53.2 %reduce-scatter.11.cloned.1.call-start = ((), (), s32[]{:S(2)}) async-start(), calls=%async_computation.14 | async-start | bytes 811008 | tf_op jit(solution)/shard_map/reduce_scatter | solution.py:214
  398.7 110.8 %reduce-scatter.13.cloned.1.call-start = ((), (), s32[]{:S(2)}) async-start(), calls=%async_computation.15 | async-start | bytes 10485760 | tf_op jit(solution)/shard_map/reduce_scatter | solution.py:28
  429.2 112.1 %reduce-scatter.15.cloned.1.call-start = ((), (), s32[]{:S(2)}) async-start(), calls=%async_computation.16 | async-start | bytes 2621440 | tf_op jit(solution)/shard_map/reduce_scatter | solution.py:28
  509.4 52.5 %reduce-scatter.17.cloned.1.call-start = ((), (), s32[]{:S(2)}) async-start(), calls=%async_computation.17 | async-start | bytes 786432 | tf_op jit(solution)/shard_map/reduce_scatter | solution.py:28
Sparse Core Ops, SparseCore 0:
  9.0 22.6 all-gather.22
  52.1 25.7 all-gather.10
  79.5 47.8 all-gather.12
  129.0 20.4 all-gather.18
  151.0 30.1 all-gather.14
  182.7 47.0 all-gather.20
  231.4 47.7 all-gather.16
  281.7 84.2 reduce-scatter.6
  368.4 30.1 reduce-scatter.8
  400.8 18.3 reduce-scatter.10
  429.4 80.0 reduce-scatter.12
  511.7 29.6 reduce-scatter.14
  543.7 18.2 reduce-scatter.16

commit v7 on v6

--- a/solution.py
+++ b/solution.py
@@ -24,13 +24,13 @@
 
 
 def scatter_staged(x, dim):
-    for name in ("y", "z", "xh"):
+    for name in ("y", ("z", "xh")):
         x = lax.psum_scatter(x, name, scatter_dimension=dim, tiled=True)
     return x
 
 
 def gather_staged(x, dim):
-    for name in ("y", "xh", "z"):
+    for name in ("y", ("z", "xh")):
         x = lax.all_gather(x, name, axis=dim, tiled=True)
     return x
 
@@ -210,8 +210,7 @@
     hidden = jax.nn.gelu(up_acc, approximate=False).astype(jnp.bfloat16)
     mlp = jnp.dot(hidden, down_piece, preferred_element_type=jnp.float32)
     summed, mlp = lax.optimization_barrier((summed, mlp))
-    for name in ("z", "xh"):
-        summed = lax.psum_scatter(summed, name, scatter_dimension=0, tiled=True)
+    summed = lax.psum_scatter(summed, ("z", "xh"), scatter_dimension=0, tiled=True)
     sum_acc = summed[:, :, :span_rows]
     sum_tot = summed[:, :, span_rows:].reshape(heads_loc, groups_here, span_rows)
     own_largest = lax.dynamic_slice_in_dim(largest, slot_me, heads_loc, 0)

time: 572 us -> 620 us (1.084)
  waiting for transfers between devices: 352 us -> 401 us
    reduce_scatter x2 -> x1, waiting for transfers between devices: 53 us -> 79.9 us  [layer(): lax.psum_scatter(summed, ('z', 'xh'), scatter_dimension=0, tiled=True)]
    reduce_scatter x3 -> x2, waiting for transfers between devices: 126 us -> 152 us  [scatter_staged(): x = lax.psum_scatter(x, name, scatter_dimension=dim, tiled=True)]
    all_gather x2 -> x1, waiting for transfers between devices: 74.3 us -> 72.7 us  [gather_staged(): x = lax.all_gather(x, name, axis=dim, tiled=True)]
  transfers between devices with their start and end apart: 13 -> 10, of which waited for: 10 -> 7; matrix products, arithmetic and copies ran while one was open for 11% -> 10% of each run, Pallas kernels for 13% -> 12%
where the time goes in v7:
time: 620 us; the launch traced here: 619 us
  waiting for transfers between devices  401 us (65%)
  Pallas kernels  76 us (12%)
  blocking collectives  46.3 us (7%)
  other arithmetic  33.1 us (5%)
  matrix products  32.6 us (5%)
  local copies, waits for them, and re-layouts  15.2 us (2%)
  between operations  13.9 us (2%)
    reduce_scatter x2, waiting for transfers between devices, scatter_staged(): x = lax.psum_scatter(x, name, scatter_dimension=dim, tiled=True)  152 us
    reduce_scatter x1, waiting for transfers between devices, layer(): lax.psum_scatter(summed, ('z', 'xh'), scatter_dimension=0, tiled=True)  79.9 us
    pallas_call x1, Pallas kernels, attend_pages(): pl.pallas_call(attend_kernel, grid=(groups, heads), in_specs=[pl.BlockSpe...  76 us
    all_gather x1, waiting for transfers between devices, gather_staged(): x = lax.all_gather(x, name, axis=dim, tiled=True)  72.7 us
    reduce_scatter x1, waiting for transfers between devices, layer(): summed = lax.psum_scatter(packed, 'y', scatter_dimension=0, tiled=True)  71.5 us
    all_gather x3, blocking collectives, max_staged(): x = jnp.max(lax.all_gather(x, name, axis=0, tiled=False), axis=0)  31.3 us
    all_gather x1, blocking collectives, gather_staged(): x = lax.all_gather(x, name, axis=dim, tiled=True)  15 us
    dot_general x1, matrix products, layer(): mlp = jnp.dot(hidden, down_piece, preferred_element_type=jnp.float32)  15 us
  transfers between devices with their start and end apart: 10, of which 7 were waited for; matrix products, arithmetic and copies ran while one was open for 10% of the time, Pallas kernels for 12%

profile of v7, /device:TPU:0, one launch (start us, length us, event | category | flops | bytes accessed | tf_op | source)
XLA Modules:
  0.0 619.1 jit_solution(3368599570567684169)
XLA Ops:
  6.5 1.7 slice.46
  9.3 3.1 convert_reduce_fusion
  12.3 3.4 multiply_reduce_fusion
  15.9 4.4 multiply_convert_fusion.1
  20.3 11.4 %all-gather.20.cloned.1.call-done = bf16[4096,1,128]{2,0,1:T(8,128)(2,1)} async-done(((bf16[1024,1,128]{2,0,1:T(8,128)(2,1)}), bf16[4096,1,128]{2,0,1:T(8,128)(2,1)}) %all-gather.20.cloned.1.call-update) | async-done | bytes 1048592 | tf_op jit(solution)/shard_map/all_gather | solution.py:144
  31.7 3.7 convolution_bitcast_fusion
  35.5 1.2 fusion.68
  36.9 15.0 %all_gather.40 = bf16[512,512]{1,0:T(8,128)(2,1)} all-gather(bf16[512,128]{1,0:T(8,128)(2,1)S(1)} %pad_maximum_fusion.1), channel_id=1, replica_groups=mesh['req'=4,'z'=4,'xh'=2,'y'=4] {'y'}, dimensions={1}, use_global_device_ids=true | all-gather | bytes 655360 | tf_op jit(solution)/shard_map/all_gather | solution.py:34
  53.0 72.7 %all-gather.10.cloned.1.call-done.q_ref = bf16[512,4096]{1,0:T(8,128)(2,1)} async-done(((bf16[512,512]{1,0:T(8,128)(2,1)}), bf16[512,4096]{1,0:T(8,128)(2,1)}) %all-gather.10.cloned.1.call-update) | async-done | bytes 4194320 | tf_op jit(solution)/shard_map/all_gather | solution.py:34
  127.2 1.4 copy.68
  129.7 1.0 and.45
  130.9 1.2 and_convert_fusion.live_ref
  132.2 76.0 %shard_map.91 = (f32[32,2,256,128]{3,2,1,0:T(8,128)}, f32[32,2,1,256]{3,2,1,0:T(1,128)}, f32[32,2,1,256]{3,2,1,0:T(1,128)}) custom-call(bf16[512,4096]{1,0:T(8,128)(2,1)} %all-gather.10.cloned.1.call-done.q_ref, bf16[8,2,32,128,128]{4,3,2,1,0:T(8,128)(2,1)} %bitcast.97, bf16[8,2,32,128,128]{4,3,2,1,0:T(8,128)(2,1)} %bitcast.98, ...), custom_call_target="tpu_custom_call" | custom-call | flops 8589934592 | bytes 46137344 | tf_op jit(solution)/shard_map/pallas_call | solution.py:92
  209.1 1.3 copy.67
  210.5 4.2 fusion.7
  214.8 1.2 fusion.72
  216.5 12.6 %all_gather.44 = f32[4,32,2,256]{3,1,2,0:T(8,128)S(1)} all-gather(f32[1,32,2,256]{3,1,2,0:T(8,128)S(1)} %copy.64), channel_id=1, replica_groups=mesh['req'=4,'z'=4,'xh'=2,'y'=4] {'y'}, dimensions={0}, use_global_device_ids=true | all-gather | bytes 327680 | tf_op jit(solution)/shard_map/all_gather | solution.py:40
  229.2 6.4 %all-gather.1 = f32[64,2,256]{2,1,0:T(2,128)S(1)} all-gather(f32[32,2,256]{2,1,0:T(2,128)S(1)} %copy.65), channel_id=3, replica_groups=mesh['req'=4,'z'=4,'xh'=2,'y'=4] {'xh'}, dimensions={0}, use_global_device_ids=true | all-gather | bytes 196608 | tf_op jit(solution)/shard_map/all_gather | solution.py:40
  235.7 12.3 %all-gather.2 = f32[128,2,256]{2,1,0:T(2,128)S(1)} all-gather(f32[32,2,256]{2,1,0:T(2,128)S(1)} %reduce_max.43), channel_id=4, replica_groups=mesh['req'=4,'z'=4,'xh'=2,'y'=4] {'z'}, dimensions={0}, use_global_device_ids=true | all-gather | bytes 327680 | tf_op jit(solution)/shard_map/all_gather | solution.py:40
  248.3 5.3 broadcast_multiply_fusion
  253.6 4.0 pad_maximum_fusion
  257.6 4.7 copy.69
  262.4 12.3 %all-gather.14.cloned.1.call-done = bf16[4096,512]{1,0:T(8,128)(2,1)} async-done(((bf16[1024,512]{1,0:T(8,128)(2,1)}), bf16[4096,512]{1,0:T(8,128)(2,1)}) %all-gather.14.cloned.1.call-update) | async-done | bytes 4194320 | tf_op jit(solution)/shard_map/all_gather | solution.py:172
  274.9 15.0 %fusion.28 = f32[512,4096]{1,0:T(8,128)} fusion(bf16[512,4096]{0,1:T(8,128)(2,1)} %bitcast.101, bf16[4096,512]{1,0:T(8,128)(2,1)} %all-gather.14.cloned.1.call-done, bf16[512,4096]{1,0:T(8,128)(2,1)} %param.9, f32[4096]{0:T(1024)S(1)} %bitcast.122, f32[512]{0:T(512)S(1)} %add_rsqrt_fusion, f32[512]{0:T(512)S(1)} %broadcast_multiply_fusion.1), kind=kOutput, calls=%fused_computation.43 | convolution fusion | flops 4322492416 | bytes 20992000 | tf_op jit(solution)/shard_map/dot_general | solution.py:211
  289.9 71.5 %reduce-scatter.5.cloned.1.call-done = f32[8,2,258,128]{3,2,1,0:T(8,128)} async-done(((f32[32,2,258,128]{3,2,1,0:T(8,128)}), f32[8,2,258,128]{3,2,1,0:T(8,128)}) %reduce-scatter.5.cloned.1.call-update) | async-done | bytes 2113552 | tf_op jit(solution)/shard_map/reduce_scatter | solution.py:208
  361.6 79.9 %reduce-scatter.7.cloned.1.call-done = f32[1,2,258,128]{3,2,1,0:T(8,128)} async-done(((f32[8,2,258,128]{3,2,1,0:T(8,128)}), f32[1,2,258,128]{3,2,1,0:T(8,128)}) %reduce-scatter.7.cloned.1.call-update) | async-done | bytes 264208 | tf_op jit(solution)/shard_map/reduce_scatter | solution.py:213
  442.2 1.3 fusion.16
  443.5 7.9 %convolution_add_fusion = f32[512,4096]{1,0:T(8,128)} fusion(f32[512,4096]{1,0:T(8,128)} %fusion.28, bf16[512,128]{1,0:T(8,128)(2,1)S(1)} %bitcast.115, bf16[128,4096]{0,1:T(8,128)(2,1)S(1)} %bitcast.99), kind=kOutput, calls=%fused_computation.5 | convolution fusion | flops 538968064 | bytes 17956864 | tf_op jit(solution)/shard_map/dot_general | solution.py:222
  451.5 79.4 %reduce-scatter.9.cloned.1.call-done = f32[512,1024]{1,0:T(8,128)} async-done(((f32[512,4096]{1,0:T(8,128)}), f32[512,1024]{1,0:T(8,128)}) %reduce-scatter.9.cloned.1.call-update) | async-done | bytes 2097168 | tf_op jit(solution)/shard_map/reduce_scatter | solution.py:28
  530.9 6.6 %convert_element_type.63 = f32[512,4096]{1,0:T(8,128)} convert(bf16[512,4096]{1,0:T(8,128)(2,1)} %param.9) | non-fusion elementwise | flops 2097152 | bytes 12582912 | tf_op jit(solution)/shard_map/convert_element_type | solution.py:141
  537.5 73.0 %reduce-scatter.11.cloned.1.call-done = f32[512,128]{1,0:T(8,128)} async-done(((f32[512,1024]{1,0:T(8,128)}), f32[512,128]{1,0:T(8,128)}) %reduce-scatter.11.cloned.1.call-update) | async-done | bytes 262160 | tf_op jit(solution)/shard_map/reduce_scatter | solution.py:28
  610.5 1.8 dynamic-slice_add_fusion
  (76 shorter events, 8.4 us)
Async XLA Ops:
  6.5 9.2 %copy-start.5 = (s32[2]{0:T(128)S(1)}, s32[2]{0:T(128)}, u32[]{:S(2)}) copy-start(s32[2]{0:T(128)} %param.16) | copy-start | bytes 28
  6.5 25.2 %all-gather.20.cloned.1.call-start = ((), (), s32[]{:S(2)}) async-start(), calls=%async_computation.13 | async-start | bytes 1310720 | tf_op jit(solution)/shard_map/all_gather | solution.py:144
  8.2 117.5 %all-gather.10.cloned.1.call-start = ((), (), s32[]{:S(2)}) async-start(), calls=%async_computation.4 | async-start | bytes 4718592 | tf_op jit(solution)/shard_map/all_gather | solution.py:34
  8.3 7.6 %copy-start = (bf16[512,4096]{1,0:T(8,128)(2,1)S(1)}, bf16[512,4096]{1,0:T(8,128)(2,1)}, u32[]{:S(2)}) copy-start(bf16[512,4096]{1,0:T(8,128)(2,1)} %param.9) | copy-start | bytes 12582916
  15.9 36.2 %slice-start = ((bf16[1024,3,128]{2,0,1:T(8,128)(2,1)}), bf16[1024,2,128]{2,0,1:T(8,128)(2,1)S(1)}, s32[]{:S(2)}) async-start(bf16[1024,3,128]{2,0,1:T(8,128)(2,1)} %param.11), calls=%async_computation.14 | async-start | bytes 1048576 | tf_op jit(solution)/shard_map/slice | solution.py:151
  15.9 109.8 %copy-start.3 = (bf16[128,1024]{1,0:T(8,128)(2,1)S(1)}, bf16[128,1024]{1,0:T(8,128)(2,1)}, u32[]{:S(2)}) copy-start(bf16[128,1024]{1,0:T(8,128)(2,1)} %param.12) | copy-start | bytes 786436
  15.9 111.3 %copy-start.1 = (bf16[512,1024]{1,0:T(8,128)(2,1)S(1)}, bf16[512,1024]{1,0:T(8,128)(2,1)}, u32[]{:S(2)}) copy-start(bf16[512,1024]{1,0:T(8,128)(2,1)} %param.14) | copy-start | bytes 3145732
  20.3 109.2 %copy-start.6 = (s32[2,128]{1,0:T(2,128)S(1)}, s32[2,128]{1,0:T(2,128)}, u32[]{:S(2)}) copy-start(s32[2,128]{1,0:T(2,128)} %param.17) | copy-start | bytes 3076
  52.0 157.2 %all-gather.16.cloned.1.call-start = ((), (), s32[]{:S(2)}) async-start(), calls=%async_computation.7 | async-start | bytes 1310720 | tf_op jit(solution)/shard_map/all_gather | solution.py:173
  126.6 83.9 %all-gather.12.cloned.1.call-start = ((), (), s32[]{:S(2)}) async-start(), calls=%async_computation.5 | async-start | bytes 2621440 | tf_op jit(solution)/shard_map/all_gather | solution.py:153
  127.1 130.5 %all-gather.18.cloned.1.call-start = ((), (), s32[]{:S(2)}) async-start(), calls=%async_computation.8 | async-start | bytes 5242880 | tf_op jit(solution)/shard_map/all_gather | solution.py:174
  128.6 146.1 %all-gather.14.cloned.1.call-start = ((), (), s32[]{:S(2)}) async-start(), calls=%async_computation.6 | async-start | bytes 5242880 | tf_op jit(solution)/shard_map/all_gather | solution.py:172
  129.2 232.2 %reduce-scatter.5.cloned.1.call-start = ((), (), s32[]{:S(2)}) async-start(), calls=%async_computation.9 | async-start | bytes 10813440 | tf_op jit(solution)/shard_map/reduce_scatter | solution.py:208
  208.2 8.3 %copy-start.2 = (f32[32,2,1,256]{3,2,1,0:T(1,128)S(1)}, f32[32,2,1,256]{3,2,1,0:T(1,128)}, u32[]{:S(2)}) copy-start(f32[32,2,1,256]{3,2,1,0:T(1,128)} %get-tuple-element.21) | copy-start | bytes 196612
  208.2 40.0 %copy-start.4 = (f32[32,2,1,256]{3,2,1,0:T(1,128)S(1)}, f32[32,2,1,256]{3,2,1,0:T(1,128)}, u32[]{:S(2)}) copy-start(f32[32,2,1,256]{3,2,1,0:T(1,128)} %get-tuple-element.23) | copy-start | bytes 196612
  274.7 166.8 %reduce-scatter.7.cloned.1.call-start = ((), (), s32[]{:S(2)}) async-start(), calls=%async_computation.10 | async-start | bytes 2433024 | tf_op jit(solution)/shard_map/reduce_scatter | solution.py:213
  361.4 169.5 %reduce-scatter.9.cloned.1.call-start = ((), (), s32[]{:S(2)}) async-start(), calls=%async_computation.11 | async-start | bytes 10485760 | tf_op jit(solution)/shard_map/reduce_scatter | solution.py:28
  451.5 159.0 %reduce-scatter.11.cloned.1.call-start = ((), (), s32[]{:S(2)}) async-start(), calls=%async_computation.12 | async-start | bytes 2359296 | tf_op jit(solution)/shard_map/reduce_scatter | solution.py:28
Sparse Core Ops, SparseCore 0:
  9.0 22.6 all-gather.19
  52.1 73.5 all-gather.9
  127.4 17.9 all-gather.15
  146.9 30.0 all-gather.11
  178.4 47.0 all-gather.17
  227.0 47.5 all-gather.13
  277.1 84.2 reduce-scatter.4
  365.1 76.3 reduce-scatter.6
  451.6 79.2 reduce-scatter.8
  534.4 76.0 reduce-scatter.10

commit v8 on v6

--- a/solution.py
+++ b/solution.py
@@ -21,6 +21,16 @@
     lead = w.shape[0]
     blocks = w.reshape(lead, nz, nxh, ny, w.shape[1] // (nz * nxh * ny))
     return jnp.transpose(blocks, (0, 3, 1, 2, 4)).reshape(w.shape)
+
+
+def gather_req_ring(w):
+    n = lax.axis_size("req")
+    me = lax.axis_index("req")
+    parts = [w] + [
+        lax.ppermute(w, "req", [(i, (i + s) % n) for i in range(n)]) for s in range(1, n)
+    ]
+    ordered = jnp.take(jnp.stack(parts), (me - jnp.arange(n)) % n, axis=0)
+    return ordered.reshape((n * w.shape[0],) + w.shape[1:])
 
 
 def scatter_staged(x, dim):
@@ -169,7 +179,7 @@
     )
     total_new = jnp.sum(p_new.astype(jnp.float32), axis=-1)
     accum_new = jnp.einsum("ghqk,gkhd->ghqd", p_new, v_grp, preferred_element_type=jnp.float32)
-    up_piece = lax.all_gather(up_weight, "req", axis=0, tiled=True)
+    up_piece = gather_req_ring(up_weight)
     dense_piece = lax.all_gather(dense_weight, "req", axis=1, tiled=True)
     down_piece = lax.all_gather(down_weight, "req", axis=1, tiled=True)
     dense_piece = by_slot(dense_piece, split)

time: 572 us -> 567 us (level)
  waiting for transfers between devices: 352 us -> 334 us
    all_gather x1 -> x0, waiting for transfers between devices: 14.7 us -> none  [layer(): up_piece = lax.all_gather(up_weight, 'req', axis=0, tiled=True)]
  transfers between devices with their start and end apart: 13 -> 15, of which waited for: 10 -> 9; matrix products, arithmetic and copies ran while one was open for 11% -> 12% of each run, Pallas kernels for 13% -> 13%
where the time goes in v8:
time: 567 us; the launch traced here: 566 us
  waiting for transfers between devices  334 us (59%)
  Pallas kernels  76.1 us (13%)
  blocking collectives  48.1 us (8%)
  other arithmetic  38.5 us (7%)
  matrix products  32.1 us (6%)
  local copies, waits for them, and re-layouts  20.7 us (4%)
  between operations  14 us (2%)
    reduce_scatter x3, waiting for transfers between devices, scatter_staged(): x = lax.psum_scatter(x, name, scatter_dimension=dim, tiled=True)  126 us
    pallas_call x1, Pallas kernels, attend_pages(): pl.pallas_call(attend_kernel, grid=(groups, heads), in_specs=[pl.BlockSpe...  76.1 us
    all_gather x2, waiting for transfers between devices, gather_staged(): x = lax.all_gather(x, name, axis=dim, tiled=True)  74.3 us
    reduce_scatter x1, waiting for transfers between devices, layer(): summed = lax.psum_scatter(packed, 'y', scatter_dimension=0, tiled=True)  66.4 us
    reduce_scatter x2, waiting for transfers between devices, layer(): summed = lax.psum_scatter(summed, name, scatter_dimension=0, tiled=True)  53.1 us
    all_gather x3, blocking collectives, max_staged(): x = jnp.max(lax.all_gather(x, name, axis=0, tiled=False), axis=0)  33.1 us
    all_gather x1, blocking collectives, gather_staged(): x = lax.all_gather(x, name, axis=dim, tiled=True)  15 us
    dot_general x1, matrix products, layer(): mlp = jnp.dot(hidden, down_piece, preferred_element_type=jnp.float32)  14.6 us
  transfers between devices with their start and end apart: 15, of which 9 were waited for; matrix products, arithmetic and copies ran while one was open for 12% of the time, Pallas kernels for 13%

profile of v8, /device:TPU:0, one launch (start us, length us, event | category | flops | bytes accessed | tf_op | source)
XLA Modules:
  0.0 566.1 jit_solution(10542176035101009034)
XLA Ops:
  6.5 1.7 slice.46
  9.3 3.1 convert_reduce_fusion
  13.8 4.3 multiply_convert_fusion.1
  18.1 13.6 %all-gather.20.cloned.1.call-done = bf16[4096,1,128]{2,0,1:T(8,128)(2,1)} async-done(((bf16[1024,1,128]{2,0,1:T(8,128)(2,1)}), bf16[4096,1,128]{2,0,1:T(8,128)(2,1)}) %all-gather.20.cloned.1.call-update) | async-done | bytes 1048592 | tf_op jit(solution)/shard_map/all_gather | solution.py:154
  31.7 3.7 convolution_bitcast_fusion
  36.9 15.0 %all_gather.40 = bf16[512,512]{1,0:T(8,128)(2,1)} all-gather(bf16[512,128]{1,0:T(8,128)(2,1)S(1)} %pad_maximum_fusion.2), channel_id=1, replica_groups=mesh['req'=4,'z'=4,'xh'=2,'y'=4] {'y'}, dimensions={1}, use_global_device_ids=true | all-gather | bytes 655360 | tf_op jit(solution)/shard_map/all_gather | solution.py:44
  52.0 25.9 %all-gather.10.cloned.1.call-done = bf16[512,1024]{1,0:T(8,128)(2,1)} async-done(((bf16[512,512]{1,0:T(8,128)(2,1)}), bf16[512,1024]{1,0:T(8,128)(2,1)}) %all-gather.10.cloned.1.call-update) | async-done | bytes 1048592 | tf_op jit(solution)/shard_map/all_gather | solution.py:44
  79.0 48.5 %all-gather.12.cloned.1.call-done.q_ref = bf16[512,4096]{1,0:T(8,128)(2,1)} async-done(((bf16[512,1024]{1,0:T(8,128)(2,1)}), bf16[512,4096]{1,0:T(8,128)(2,1)}) %all-gather.12.cloned.1.call-update) | async-done | bytes 4194320 | tf_op jit(solution)/shard_map/all_gather | solution.py:44
  130.5 1.4 copy.68
  135.1 76.1 %shard_map.91 = (f32[32,2,256,128]{3,2,1,0:T(8,128)}, f32[32,2,1,256]{3,2,1,0:T(1,128)}, f32[32,2,1,256]{3,2,1,0:T(1,128)}) custom-call(bf16[512,4096]{1,0:T(8,128)(2,1)} %all-gather.12.cloned.1.call-done.q_ref, bf16[8,2,32,128,128]{4,3,2,1,0:T(8,128)(2,1)} %bitcast.110, bf16[8,2,32,128,128]{4,3,2,1,0:T(8,128)(2,1)} %bitcast.111, ...), custom_call_target="tpu_custom_call" | custom-call | flops 8589934592 | bytes 46137344 | tf_op jit(solution)/shard_map/pallas_call | solution.py:102
  212.0 3.5 pad_maximum_fusion.1
  215.5 5.5 gather_fusion
  221.0 4.0 bitcast_select_fusion
  225.0 1.3 copy.67
  226.4 4.2 fusion.7
  232.5 12.9 %all_gather.45 = f32[4,32,2,256]{3,1,2,0:T(8,128)S(1)} all-gather(f32[1,32,2,256]{3,1,2,0:T(8,128)S(1)} %copy.64), channel_id=1, replica_groups=mesh['req'=4,'z'=4,'xh'=2,'y'=4] {'y'}, dimensions={0}, use_global_device_ids=true | all-gather | bytes 327680 | tf_op jit(solution)/shard_map/all_gather | solution.py:50
  245.4 8.0 %all-gather.1 = f32[64,2,256]{2,1,0:T(2,128)S(1)} all-gather(f32[32,2,256]{2,1,0:T(2,128)S(1)} %copy.65), channel_id=3, replica_groups=mesh['req'=4,'z'=4,'xh'=2,'y'=4] {'xh'}, dimensions={0}, use_global_device_ids=true | all-gather | bytes 196608 | tf_op jit(solution)/shard_map/all_gather | solution.py:50
  253.5 12.3 %all-gather.2 = f32[128,2,256]{2,1,0:T(2,128)S(1)} all-gather(f32[32,2,256]{2,1,0:T(2,128)S(1)} %reduce_max.43), channel_id=4, replica_groups=mesh['req'=4,'z'=4,'xh'=2,'y'=4] {'z'}, dimensions={0}, use_global_device_ids=true | all-gather | bytes 327680 | tf_op jit(solution)/shard_map/all_gather | solution.py:50
  266.1 5.2 broadcast_multiply_fusion
  271.3 4.1 pad_maximum_fusion
  275.4 4.7 copy.69
  280.4 14.6 %fusion.28 = f32[512,4096]{1,0:T(8,128)} fusion(bf16[512,4096]{0,1:T(8,128)(2,1)} %bitcast.114, bf16[4096,512]{1,0:T(8,128)(2,1)} %bitcast_select_fusion, bf16[512,4096]{1,0:T(8,128)(2,1)} %param.9, f32[4096]{0:T(1024)S(1)} %bitcast.138, f32[512]{0:T(512)S(1)} %add_rsqrt_fusion, f32[512]{0:T(512)S(1)} %broadcast_multiply_fusion.1), kind=kOutput, calls=%fused_computation.46 | convolution fusion | flops 4322492416 | bytes 20992000 | tf_op jit(solution)/shard_map/dot_general | solution.py:221
  295.0 66.4 %reduce-scatter.7.cloned.1.call-done = f32[8,2,258,128]{3,2,1,0:T(8,128)} async-done(((f32[32,2,258,128]{3,2,1,0:T(8,128)}), f32[8,2,258,128]{3,2,1,0:T(8,128)}) %reduce-scatter.7.cloned.1.call-update) | async-done | bytes 2113552 | tf_op jit(solution)/shard_map/reduce_scatter | solution.py:218
  361.5 32.6 %reduce-scatter.9.cloned.1.call-done = f32[2,2,258,128]{3,2,1,0:T(8,128)} async-done(((f32[8,2,258,128]{3,2,1,0:T(8,128)}), f32[2,2,258,128]{3,2,1,0:T(8,128)}) %reduce-scatter.9.cloned.1.call-update) | async-done | bytes 528400 | tf_op jit(solution)/shard_map/reduce_scatter | solution.py:224
  394.2 20.6 %reduce-scatter.11.cloned.1.call-done = f32[1,2,258,128]{3,2,1,0:T(8,128)} async-done(((f32[2,2,258,128]{3,2,1,0:T(8,128)}), f32[1,2,258,128]{3,2,1,0:T(8,128)}) %reduce-scatter.11.cloned.1.call-update) | async-done | bytes 264208 | tf_op jit(solution)/shard_map/reduce_scatter | solution.py:224
  415.6 1.3 fusion.16
  416.9 7.9 %convolution_add_fusion = f32[512,4096]{1,0:T(8,128)} fusion(f32[512,4096]{1,0:T(8,128)} %fusion.28, bf16[512,128]{1,0:T(8,128)(2,1)S(1)} %bitcast.130, bf16[128,4096]{0,1:T(8,128)(2,1)S(1)} %bitcast.112), kind=kOutput, calls=%fused_computation.6 | convolution fusion | flops 538968064 | bytes 17956864 | tf_op jit(solution)/shard_map/dot_general | solution.py:233
  424.8 80.1 %reduce-scatter.13.cloned.1.call-done = f32[512,1024]{1,0:T(8,128)} async-done(((f32[512,4096]{1,0:T(8,128)}), f32[512,1024]{1,0:T(8,128)}) %reduce-scatter.13.cloned.1.call-update) | async-done | bytes 2097168 | tf_op jit(solution)/shard_map/reduce_scatter | solution.py:38
  505.0 32.0 %reduce-scatter.15.cloned.1.call-done = f32[512,256]{1,0:T(8,128)} async-done(((f32[512,1024]{1,0:T(8,128)}), f32[512,256]{1,0:T(8,128)}) %reduce-scatter.15.cloned.1.call-update) | async-done | bytes 524304 | tf_op jit(solution)/shard_map/reduce_scatter | solution.py:38
  537.1 6.6 %convert_element_type.63 = f32[512,4096]{1,0:T(8,128)} convert(bf16[512,4096]{1,0:T(8,128)(2,1)} %param.9) | non-fusion elementwise | flops 2097152 | bytes 12582912 | tf_op jit(solution)/shard_map/convert_element_type | solution.py:151
  543.6 13.9 %reduce-scatter.17.cloned.1.call-done = f32[512,128]{1,0:T(8,128)} async-done(((f32[512,256]{1,0:T(8,128)}), f32[512,128]{1,0:T(8,128)}) %reduce-scatter.17.cloned.1.call-update) | async-done | bytes 262160 | tf_op jit(solution)/shard_map/reduce_scatter | solution.py:38
  557.5 1.8 dynamic-slice_add_fusion
  (98 shorter events, 15.6 us)
Async XLA Ops:
  6.5 25.2 %all-gather.20.cloned.1.call-start = ((), (), s32[]{:S(2)}) async-start(), calls=%async_computation.17 | async-start | bytes 1310720 | tf_op jit(solution)/shard_map/all_gather | solution.py:154
  8.2 69.7 %all-gather.10.cloned.1.call-start = ((), (), s32[]{:S(2)}) async-start(), calls=%async_computation.6 | async-start | bytes 1572864 | tf_op jit(solution)/shard_map/all_gather | solution.py:44
  8.3 4.1 copy-start
  9.3 4.4 copy-start.6
  18.1 59.9 %slice-start = ((bf16[1024,3,128]{2,0,1:T(8,128)(2,1)}), bf16[1024,2,128]{2,0,1:T(8,128)(2,1)S(1)}, s32[]{:S(2)}) async-start(bf16[1024,3,128]{2,0,1:T(8,128)(2,1)} %param.11), calls=%async_computation.18 | async-start | bytes 1048576 | tf_op jit(solution)/shard_map/slice | solution.py:161
  35.4 92.0 %copy-start.4 = (bf16[128,1024]{1,0:T(8,128)(2,1)S(1)}, bf16[128,1024]{1,0:T(8,128)(2,1)}, u32[]{:S(2)}) copy-start(bf16[128,1024]{1,0:T(8,128)(2,1)} %param.12) | copy-start | bytes 786436
  35.4 93.6 %copy-start.7 = (s32[2,128]{1,0:T(2,128)S(1)}, s32[2,128]{1,0:T(2,128)}, u32[]{:S(2)}) copy-start(s32[2,128]{1,0:T(2,128)} %param.17) | copy-start | bytes 3076
  35.4 95.0 %copy-start.1 = (bf16[512,1024]{1,0:T(8,128)(2,1)S(1)}, bf16[512,1024]{1,0:T(8,128)(2,1)}, u32[]{:S(2)}) copy-start(bf16[512,1024]{1,0:T(8,128)(2,1)} %param.14) | copy-start | bytes 3145732
  52.0 75.5 %all-gather.12.cloned.1.call-start = ((), (), s32[]{:S(2)}) async-start(), calls=%async_computation.7 | async-start | bytes 5242880 | tf_op jit(solution)/shard_map/all_gather | solution.py:44
  77.9 147.1 %all-gather.16.cloned.1.call-start = ((), (), s32[]{:S(2)}) async-start(), calls=%async_computation.9 | async-start | bytes 1310720 | tf_op jit(solution)/shard_map/all_gather | solution.py:183
  128.3 98.1 %all-gather.14.cloned.1.call-start = ((), (), s32[]{:S(2)}) async-start(), calls=%async_computation.8 | async-start | bytes 2621440 | tf_op jit(solution)/shard_map/all_gather | solution.py:163
  128.9 146.5 %all-gather.18.cloned.1.call-start = ((), (), s32[]{:S(2)}) async-start(), calls=%async_computation.10 | async-start | bytes 5242880 | tf_op jit(solution)/shard_map/all_gather | solution.py:184
  131.9 229.5 %reduce-scatter.7.cloned.1.call-start = ((), (), s32[]{:S(2)}) async-start(), calls=%async_computation.11 | async-start | bytes 10813440 | tf_op jit(solution)/shard_map/reduce_scatter | solution.py:218
  132.1 79.9 %collective-permute-start.2 = (bf16[1024,512]{1,0:T(8,128)(2,1)}, bf16[1024,512]{1,0:T(8,128)(2,1)S(1)}, u32[]{:S(2)}, u32[]{:S(2)}) collective-permute-start(bf16[1024,512]{1,0:T(8,128)(2,1)} %param.13), channel_id=1, source_target_pairs={{0,96},{32,0},{64,32},{96,64},{1,97},{33,1},{65,33},{97,65},{2,98}... | collective-permute-start | bytes 3145736 | tf_op jit(solution)/shard_map/ppermute | solution.py:30
  132.9 79.1 %collective-permute-start.1 = (bf16[1024,512]{1,0:T(8,128)(2,1)}, bf16[1024,512]{1,0:T(8,128)(2,1)}, u32[]{:S(2)}, u32[]{:S(2)}) collective-permute-start(bf16[1024,512]{1,0:T(8,128)(2,1)} %param.13), channel_id=1, source_target_pairs={{0,64},{32,96},{64,0},{96,32},{1,65},{33,97},{65,1},{97,33},{2,66}... | collective-permute-start | bytes 3145736 | tf_op jit(solution)/shard_map/ppermute | solution.py:30
  133.7 78.3 %collective-permute-start = (bf16[1024,512]{1,0:T(8,128)(2,1)}, bf16[1024,512]{1,0:T(8,128)(2,1)}, u32[]{:S(2)}, u32[]{:S(2)}) collective-permute-start(bf16[1024,512]{1,0:T(8,128)(2,1)} %param.13), channel_id=1, source_target_pairs={{0,32},{32,64},{64,96},{96,0},{1,33},{33,65},{65,97},{97,1},{2,34}... | collective-permute-start | bytes 3145736 | tf_op jit(solution)/shard_map/ppermute | solution.py:30
  135.1 76.9 %copy-start.2 = (bf16[1024,512]{1,0:T(8,128)(2,1)S(1)}, bf16[1024,512]{1,0:T(8,128)(2,1)}, u32[]{:S(2)}) copy-start(bf16[1024,512]{1,0:T(8,128)(2,1)} %param.13) | copy-start | bytes 3145732
  226.4 6.0 %copy-start.3 = (f32[32,2,1,256]{3,2,1,0:T(1,128)S(1)}, f32[32,2,1,256]{3,2,1,0:T(1,128)}, u32[]{:S(2)}) copy-start(f32[32,2,1,256]{3,2,1,0:T(1,128)} %get-tuple-element.21) | copy-start | bytes 196612
  230.6 35.4 %copy-start.5 = (f32[32,2,1,256]{3,2,1,0:T(1,128)S(1)}, f32[32,2,1,256]{3,2,1,0:T(1,128)}, u32[]{:S(2)}) copy-start(f32[32,2,1,256]{3,2,1,0:T(1,128)} %get-tuple-element.23) | copy-start | bytes 196612
  280.1 113.9 %reduce-scatter.9.cloned.1.call-start = ((), (), s32[]{:S(2)}) async-start(), calls=%async_computation.12 | async-start | bytes 2703360 | tf_op jit(solution)/shard_map/reduce_scatter | solution.py:224
  361.4 53.4 %reduce-scatter.11.cloned.1.call-start = ((), (), s32[]{:S(2)}) async-start(), calls=%async_computation.13 | async-start | bytes 811008 | tf_op jit(solution)/shard_map/reduce_scatter | solution.py:224
  394.0 110.9 %reduce-scatter.13.cloned.1.call-start = ((), (), s32[]{:S(2)}) async-start(), calls=%async_computation.14 | async-start | bytes 10485760 | tf_op jit(solution)/shard_map/reduce_scatter | solution.py:38
  424.8 112.2 %reduce-scatter.15.cloned.1.call-start = ((), (), s32[]{:S(2)}) async-start(), calls=%async_computation.15 | async-start | bytes 2621440 | tf_op jit(solution)/shard_map/reduce_scatter | solution.py:38
  505.0 52.5 %reduce-scatter.17.cloned.1.call-start = ((), (), s32[]{:S(2)}) async-start(), calls=%async_computation.16 | async-start | bytes 786432 | tf_op jit(solution)/shard_map/reduce_scatter | solution.py:38
Sparse Core Ops, SparseCore 0:
  9.0 22.6 all-gather.19
  52.1 25.7 all-gather.9
  79.6 47.8 all-gather.11
  129.0 29.2 all-gather.15
  159.8 45.7 all-gather.13
  207.1 47.1 all-gather.17
  280.2 81.1 reduce-scatter.6
  363.8 30.1 reduce-scatter.8
  396.4 18.3 reduce-scatter.10
  424.9 79.9 reduce-scatter.12
  507.3 29.6 reduce-scatter.14
  539.2 18.2 reduce-scatter.16

commit v9 on v8

--- a/solution.py
+++ b/solution.py
@@ -46,7 +46,7 @@
 
 
 def max_staged(x):
-    for name in ("y", "xh", "z"):
+    for name in (("xh", "y"), "z"):
         x = jnp.max(lax.all_gather(x, name, axis=0, tiled=False), axis=0)
     return x
 
@@ -212,9 +212,7 @@
     factor = jnp.exp(tops - largest)
     tot_rows = (totals * factor).reshape(HEADS, groups_here, span_rows // HD, HD)
     packed = jnp.concatenate([accums * factor[..., None], tot_rows], axis=2)
-    packed, up_piece, dense_piece, down_piece = lax.optimization_barrier(
-        (packed, up_piece, dense_piece, down_piece)
-    )
+    packed, dense_piece, down_piece = lax.optimization_barrier((packed, dense_piece, down_piece))
     summed = lax.psum_scatter(packed, "y", scatter_dimension=0, tiled=True)
     up_acc = jnp.dot(h2, up_piece, preferred_element_type=jnp.float32)
     hidden = jax.nn.gelu(up_acc, approximate=False).astype(jnp.bfloat16)

time: 567 us -> 569 us (level)
  blocking collectives: 48.1 us -> 63.6 us
  waiting for transfers between devices: 334 us -> 320 us
    reduce_scatter x1, waiting for transfers between devices: 66.4 us -> 5.85 us  [layer(): summed = lax.psum_scatter(packed, 'y', scatter_dimension=0, tiled=True)]
    ppermute x3, waiting for transfers between devices: 0.01 us -> 46.2 us  [gather_req_ring(): lax.ppermute(w, 'req', [(i, (i + s) % n) for i in range(n)])]
    all_gather x3 -> x2, blocking collectives: 33.1 us -> 48.6 us  [max_staged(): x = jnp.max(lax.all_gather(x, name, axis=0, tiled=False), axis=0)]
  transfers between devices with their start and end apart: 15 -> 15, of which waited for: 9 -> 12; matrix products, arithmetic and copies ran while one was open for 12% -> 12% of each run, Pallas kernels for 13% -> 13%
where the time goes in v9:
time: 569 us; the launch traced here: 567 us
  waiting for transfers between devices  320 us (56%)
  Pallas kernels  76 us (13%)
  blocking collectives  63.6 us (11%)
  other arithmetic  38.5 us (7%)
  matrix products  32.3 us (6%)
  local copies, waits for them, and re-layouts  21.2 us (4%)
  between operations  14 us (2%)
    reduce_scatter x3, waiting for transfers between devices, scatter_staged(): x = lax.psum_scatter(x, name, scatter_dimension=dim, tiled=True)  126 us
    pallas_call x1, Pallas kernels, attend_pages(): pl.pallas_call(attend_kernel, grid=(groups, heads), in_specs=[pl.BlockSpe...  76 us
    all_gather x2, waiting for transfers between devices, gather_staged(): x = lax.all_gather(x, name, axis=dim, tiled=True)  74.3 us
    reduce_scatter x2, waiting for transfers between devices, layer(): summed = lax.psum_scatter(summed, name, scatter_dimension=0, tiled=True)  53.1 us
    all_gather x2, blocking collectives, max_staged(): x = jnp.max(lax.all_gather(x, name, axis=0, tiled=False), axis=0)  48.6 us
    ppermute x3, waiting for transfers between devices, gather_req_ring(): lax.ppermute(w, 'req', [(i, (i + s) % n) for i in range(n)])  46.2 us
    all_gather x1, blocking collectives, gather_staged(): x = lax.all_gather(x, name, axis=dim, tiled=True)  15 us
    dot_general x1, matrix products, layer(): mlp = jnp.dot(hidden, down_piece, preferred_element_type=jnp.float32)  14.7 us
  transfers between devices with their start and end apart: 15, of which 12 were waited for; matrix products, arithmetic and copies ran while one was open for 12% of the time, Pallas kernels for 13%

profile of v9, /device:TPU:0, one launch (start us, length us, event | category | flops | bytes accessed | tf_op | source)
XLA Modules:
  0.0 567.4 jit_solution(3898509204764097183)
XLA Ops:
  6.5 1.7 slice.46
  9.3 3.1 convert_reduce_fusion
  13.8 4.3 multiply_convert_fusion.1
  18.1 13.6 %all-gather.19.cloned.1.call-done = bf16[4096,1,128]{2,0,1:T(8,128)(2,1)} async-done(((bf16[1024,1,128]{2,0,1:T(8,128)(2,1)}), bf16[4096,1,128]{2,0,1:T(8,128)(2,1)}) %all-gather.19.cloned.1.call-update) | async-done | bytes 1048592 | tf_op jit(solution)/shard_map/all_gather | solution.py:154
  31.7 3.7 convolution_bitcast_fusion
  36.9 15.0 %all_gather.34 = bf16[512,512]{1,0:T(8,128)(2,1)} all-gather(bf16[512,128]{1,0:T(8,128)(2,1)S(1)} %pad_maximum_fusion.2), channel_id=1, replica_groups=mesh['req'=4,'z'=4,'xh'=2,'y'=4] {'y'}, dimensions={1}, use_global_device_ids=true | all-gather | bytes 655360 | tf_op jit(solution)/shard_map/all_gather | solution.py:44
  52.0 25.9 %all-gather.9.cloned.1.call-done = bf16[512,1024]{1,0:T(8,128)(2,1)} async-done(((bf16[512,512]{1,0:T(8,128)(2,1)}), bf16[512,1024]{1,0:T(8,128)(2,1)}) %all-gather.9.cloned.1.call-update) | async-done | bytes 1048592 | tf_op jit(solution)/shard_map/all_gather | solution.py:44
  79.0 48.5 %all-gather.11.cloned.1.call-done.q_ref = bf16[512,4096]{1,0:T(8,128)(2,1)} async-done(((bf16[512,1024]{1,0:T(8,128)(2,1)}), bf16[512,4096]{1,0:T(8,128)(2,1)}) %all-gather.11.cloned.1.call-update) | async-done | bytes 4194320 | tf_op jit(solution)/shard_map/all_gather | solution.py:44
  129.0 1.3 copy.68
  133.5 76.0 %shard_map.91 = (f32[32,2,256,128]{3,2,1,0:T(8,128)}, f32[32,2,1,256]{3,2,1,0:T(1,128)}, f32[32,2,1,256]{3,2,1,0:T(1,128)}) custom-call(bf16[512,4096]{1,0:T(8,128)(2,1)} %all-gather.11.cloned.1.call-done.q_ref, bf16[8,2,32,128,128]{4,3,2,1,0:T(8,128)(2,1)} %bitcast.109, bf16[8,2,32,128,128]{4,3,2,1,0:T(8,128)(2,1)} %bitcast.110, ...), custom_call_target="tpu_custom_call" | custom-call | flops 8589934592 | bytes 46137344 | tf_op jit(solution)/shard_map/pallas_call | solution.py:102
  211.7 4.2 fusion.7
  217.7 36.3 %all_gather.39 = f32[8,32,2,256]{3,1,2,0:T(8,128)S(1)} all-gather(f32[1,32,2,256]{3,1,2,0:T(8,128)S(1)} %copy.64), channel_id=1, replica_groups=mesh['req'=4,'z'=4,'xh'=2,'y'=4] {'xh','y'}, dimensions={0}, use_global_device_ids=true | all-gather | bytes 589824 | tf_op jit(solution)/shard_map/all_gather | solution.py:50
  254.2 12.3 %all-gather.1 = f32[128,2,256]{2,1,0:T(2,128)S(1)} all-gather(f32[32,2,256]{2,1,0:T(2,128)S(1)} %copy.65), channel_id=3, replica_groups=mesh['req'=4,'z'=4,'xh'=2,'y'=4] {'z'}, dimensions={0}, use_global_device_ids=true | all-gather | bytes 327680 | tf_op jit(solution)/shard_map/all_gather | solution.py:50
  266.8 5.2 broadcast_multiply_fusion
  272.0 4.0 pad_maximum_fusion
  276.1 4.6 copy.69
  283.3 21.5 %collective-permute-done.2 = bf16[1024,512]{1,0:T(8,128)(2,1)} collective-permute-done((bf16[1024,512]{1,0:T(8,128)(2,1)S(1)}, bf16[1024,512]{1,0:T(8,128)(2,1)}, u32[]{:S(2)}, u32[]{:S(2)}) %collective-permute-start.2) | collective-permute-done | bytes 1048608 | tf_op jit(solution)/shard_map/ppermute | solution.py:30
  304.8 24.2 %collective-permute-done.1 = bf16[1024,512]{1,0:T(8,128)(2,1)} collective-permute-done((bf16[1024,512]{1,0:T(8,128)(2,1)S(1)}, bf16[1024,512]{1,0:T(8,128)(2,1)}, u32[]{:S(2)}, u32[]{:S(2)}) %collective-permute-start.1) | collective-permute-done | bytes 1048608 | tf_op jit(solution)/shard_map/ppermute | solution.py:30
  329.5 3.6 pad_maximum_fusion.1
  333.1 5.0 gather_fusion
  338.2 4.0 bitcast_select_fusion
  342.2 14.7 %fusion.28 = f32[512,4096]{1,0:T(8,128)} fusion(bf16[512,4096]{0,1:T(8,128)(2,1)} %bitcast.113, bf16[4096,512]{1,0:T(8,128)(2,1)} %bitcast_select_fusion, bf16[512,4096]{1,0:T(8,128)(2,1)} %param.9, f32[4096]{0:T(1024)S(1)} %bitcast.135, f32[512]{0:T(512)S(1)} %add_rsqrt_fusion, f32[512]{0:T(512)S(1)} %broadcast_multiply_fusion.1), kind=kOutput, calls=%fused_computation.46 | convolution fusion | flops 4322492416 | bytes 20992000 | tf_op jit(solution)/shard_map/dot_general | solution.py:219
  356.9 5.8 %reduce-scatter.7.cloned.1.call-done = f32[8,2,258,128]{3,2,1,0:T(8,128)} async-done(((f32[32,2,258,128]{3,2,1,0:T(8,128)}), f32[8,2,258,128]{3,2,1,0:T(8,128)}) %reduce-scatter.7.cloned.1.call-update) | async-done | bytes 2113552 | tf_op jit(solution)/shard_map/reduce_scatter | solution.py:216
  362.8 32.6 %reduce-scatter.9.cloned.1.call-done = f32[2,2,258,128]{3,2,1,0:T(8,128)} async-done(((f32[8,2,258,128]{3,2,1,0:T(8,128)}), f32[2,2,258,128]{3,2,1,0:T(8,128)}) %reduce-scatter.9.cloned.1.call-update) | async-done | bytes 528400 | tf_op jit(solution)/shard_map/reduce_scatter | solution.py:222
  395.6 20.6 %reduce-scatter.11.cloned.1.call-done = f32[1,2,258,128]{3,2,1,0:T(8,128)} async-done(((f32[2,2,258,128]{3,2,1,0:T(8,128)}), f32[1,2,258,128]{3,2,1,0:T(8,128)}) %reduce-scatter.11.cloned.1.call-update) | async-done | bytes 264208 | tf_op jit(solution)/shard_map/reduce_scatter | solution.py:222
  416.9 1.3 fusion.16
  418.2 7.9 %convolution_add_fusion = f32[512,4096]{1,0:T(8,128)} fusion(f32[512,4096]{1,0:T(8,128)} %fusion.28, bf16[512,128]{1,0:T(8,128)(2,1)S(1)} %bitcast.127, bf16[128,4096]{0,1:T(8,128)(2,1)S(1)} %bitcast.111), kind=kOutput, calls=%fused_computation.6 | convolution fusion | flops 538968064 | bytes 17956864 | tf_op jit(solution)/shard_map/dot_general | solution.py:231
  426.2 80.1 %reduce-scatter.13.cloned.1.call-done = f32[512,1024]{1,0:T(8,128)} async-done(((f32[512,4096]{1,0:T(8,128)}), f32[512,1024]{1,0:T(8,128)}) %reduce-scatter.13.cloned.1.call-update) | async-done | bytes 2097168 | tf_op jit(solution)/shard_map/reduce_scatter | solution.py:38
  506.3 32.0 %reduce-scatter.15.cloned.1.call-done = f32[512,256]{1,0:T(8,128)} async-done(((f32[512,1024]{1,0:T(8,128)}), f32[512,256]{1,0:T(8,128)}) %reduce-scatter.15.cloned.1.call-update) | async-done | bytes 524304 | tf_op jit(solution)/shard_map/reduce_scatter | solution.py:38
  538.4 6.5 %convert_element_type.63 = f32[512,4096]{1,0:T(8,128)} convert(bf16[512,4096]{1,0:T(8,128)(2,1)} %param.9) | non-fusion elementwise | flops 2097152 | bytes 12582912 | tf_op jit(solution)/shard_map/convert_element_type | solution.py:151
  544.9 13.9 %reduce-scatter.17.cloned.1.call-done = f32[512,128]{1,0:T(8,128)} async-done(((f32[512,256]{1,0:T(8,128)}), f32[512,128]{1,0:T(8,128)}) %reduce-scatter.17.cloned.1.call-update) | async-done | bytes 262160 | tf_op jit(solution)/shard_map/reduce_scatter | solution.py:38
  558.8 1.8 dynamic-slice_add_fusion
  (96 shorter events, 18.1 us)
Async XLA Ops:
  6.5 25.2 %all-gather.19.cloned.1.call-start = ((), (), s32[]{:S(2)}) async-start(), calls=%async_computation.17 | async-start | bytes 1310720 | tf_op jit(solution)/shard_map/all_gather | solution.py:154
  8.2 69.7 %all-gather.9.cloned.1.call-start = ((), (), s32[]{:S(2)}) async-start(), calls=%async_computation.6 | async-start | bytes 1572864 | tf_op jit(solution)/shard_map/all_gather | solution.py:44
  8.3 4.1 copy-start
  9.3 4.4 copy-start.6
  18.1 59.9 %slice-start = ((bf16[1024,3,128]{2,0,1:T(8,128)(2,1)}), bf16[1024,2,128]{2,0,1:T(8,128)(2,1)S(1)}, s32[]{:S(2)}) async-start(bf16[1024,3,128]{2,0,1:T(8,128)(2,1)} %param.11), calls=%async_computation.18 | async-start | bytes 1048576 | tf_op jit(solution)/shard_map/slice | solution.py:161
  35.4 92.0 %copy-start.4 = (bf16[128,1024]{1,0:T(8,128)(2,1)S(1)}, bf16[128,1024]{1,0:T(8,128)(2,1)}, u32[]{:S(2)}) copy-start(bf16[128,1024]{1,0:T(8,128)(2,1)} %param.12) | copy-start | bytes 786436
  35.4 93.5 %copy-start.1 = (bf16[512,1024]{1,0:T(8,128)(2,1)S(1)}, bf16[512,1024]{1,0:T(8,128)(2,1)}, u32[]{:S(2)}) copy-start(bf16[512,1024]{1,0:T(8,128)(2,1)} %param.14) | copy-start | bytes 3145732
  51.9 78.7 %copy-start.7 = (s32[2,128]{1,0:T(2,128)S(1)}, s32[2,128]{1,0:T(2,128)}, u32[]{:S(2)}) copy-start(s32[2,128]{1,0:T(2,128)} %param.17) | copy-start | bytes 3076
  52.0 75.5 %all-gather.11.cloned.1.call-start = ((), (), s32[]{:S(2)}) async-start(), calls=%async_computation.7 | async-start | bytes 5242880 | tf_op jit(solution)/shard_map/all_gather | solution.py:44
  77.9 132.4 %all-gather.15.cloned.1.call-start = ((), (), s32[]{:S(2)}) async-start(), calls=%async_computation.9 | async-start | bytes 1310720 | tf_op jit(solution)/shard_map/all_gather | solution.py:183
  128.3 83.3 %all-gather.13.cloned.1.call-start = ((), (), s32[]{:S(2)}) async-start(), calls=%async_computation.8 | async-start | bytes 2621440 | tf_op jit(solution)/shard_map/all_gather | solution.py:163
  128.9 147.1 %all-gather.17.cloned.1.call-start = ((), (), s32[]{:S(2)}) async-start(), calls=%async_computation.10 | async-start | bytes 5242880 | tf_op jit(solution)/shard_map/all_gather | solution.py:184
  130.3 232.4 %reduce-scatter.7.cloned.1.call-start = ((), (), s32[]{:S(2)}) async-start(), calls=%async_computation.11 | async-start | bytes 10813440 | tf_op jit(solution)/shard_map/reduce_scatter | solution.py:216
  211.6 6.1 %copy-start.3 = (f32[32,2,1,256]{3,2,1,0:T(1,128)S(1)}, f32[32,2,1,256]{3,2,1,0:T(1,128)}, u32[]{:S(2)}) copy-start(f32[32,2,1,256]{3,2,1,0:T(1,128)} %get-tuple-element.20) | copy-start | bytes 196612
  215.9 50.8 %copy-start.5 = (f32[32,2,1,256]{3,2,1,0:T(1,128)S(1)}, f32[32,2,1,256]{3,2,1,0:T(1,128)}, u32[]{:S(2)}) copy-start(f32[32,2,1,256]{3,2,1,0:T(1,128)} %get-tuple-element.22) | copy-start | bytes 196612
  280.6 1.2 copy-start.2
  280.7 114.7 %reduce-scatter.9.cloned.1.call-start = ((), (), s32[]{:S(2)}) async-start(), calls=%async_computation.12 | async-start | bytes 2703360 | tf_op jit(solution)/shard_map/reduce_scatter | solution.py:222
  281.9 22.9 %collective-permute-start.2 = (bf16[1024,512]{1,0:T(8,128)(2,1)S(1)}, bf16[1024,512]{1,0:T(8,128)(2,1)}, u32[]{:S(2)}, u32[]{:S(2)}) collective-permute-start(bf16[1024,512]{1,0:T(8,128)(2,1)S(1)} %copy-done.2), channel_id=1, source_target_pairs={{0,96},{32,0},{64,32},{96,64},{1,97},{33,1},{65,33},{97,65},{2,98}... | collective-permute-start | bytes 3145736 | tf_op jit(solution)/shard_map/ppermute | solution.py:30
  281.9 47.2 %collective-permute-start.1 = (bf16[1024,512]{1,0:T(8,128)(2,1)S(1)}, bf16[1024,512]{1,0:T(8,128)(2,1)}, u32[]{:S(2)}, u32[]{:S(2)}) collective-permute-start(bf16[1024,512]{1,0:T(8,128)(2,1)S(1)} %copy-done.2), channel_id=1, source_target_pairs={{0,64},{32,96},{64,0},{96,32},{1,65},{33,97},{65,1},{97,33},{2,66}... | collective-permute-start | bytes 3145736 | tf_op jit(solution)/shard_map/ppermute | solution.py:30
  282.9 46.6 %collective-permute-start = (bf16[1024,512]{1,0:T(8,128)(2,1)S(1)}, bf16[1024,512]{1,0:T(8,128)(2,1)}, u32[]{:S(2)}, u32[]{:S(2)}) collective-permute-start(bf16[1024,512]{1,0:T(8,128)(2,1)S(1)} %copy-done.2), channel_id=1, source_target_pairs={{0,32},{32,64},{64,96},{96,0},{1,33},{33,65},{65,97},{97,1},{2,34}... | collective-permute-start | bytes 3145736 | tf_op jit(solution)/shard_map/ppermute | solution.py:30
  362.8 53.4 %reduce-scatter.11.cloned.1.call-start = ((), (), s32[]{:S(2)}) async-start(), calls=%async_computation.13 | async-start | bytes 811008 | tf_op jit(solution)/shard_map/reduce_scatter | solution.py:222
  395.4 110.9 %reduce-scatter.13.cloned.1.call-start = ((), (), s32[]{:S(2)}) async-start(), calls=%async_computation.14 | async-start | bytes 10485760 | tf_op jit(solution)/shard_map/reduce_scatter | solution.py:38
  426.1 112.2 %reduce-scatter.15.cloned.1.call-start = ((), (), s32[]{:S(2)}) async-start(), calls=%async_computation.15 | async-start | bytes 2621440 | tf_op jit(solution)/shard_map/reduce_scatter | solution.py:38
  506.3 52.5 %reduce-scatter.17.cloned.1.call-start = ((), (), s32[]{:S(2)}) async-start(), calls=%async_computation.16 | async-start | bytes 786432 | tf_op jit(solution)/shard_map/reduce_scatter | solution.py:38
Sparse Core Ops, SparseCore 0:
  9.0 22.6 all-gather.18
  52.1 25.7 all-gather.8
  79.6 47.8 all-gather.10
  129.0 20.3 all-gather.14
  150.9 30.0 all-gather.12
  182.5 48.3 all-gather.16
  280.8 81.9 reduce-scatter.6
  365.2 30.1 reduce-scatter.8
  397.7 18.3 reduce-scatter.10
  426.2 79.9 reduce-scatter.12
  508.7 29.6 reduce-scatter.14
  540.6 18.1 reduce-scatter.16
